TPU v7x, 512 devices: a whole 4x8x8 slice. The times are simulated.
512 devices in a mesh: ctx: 64 (over z, y), section: 2 (over x_hi), dp: 4 (over x_lo, core).
Axes of the slice: x: 4 (x_hi: 2, x_lo: 2; x = x_hi * 2 + x_lo), y: 8, z: 8, core: 2. Of those that a mesh axis runs over, the one named last changes fastest.
Arguments:
- query_vectors: bfloat16 [4, 8192, 1792], P('dp', 'ctx', 'section'), may hold values from -16 to 16
- key_vectors: bfloat16 [4, 8192, 256], P('dp', 'ctx', 'section'), may hold values from -16 to 16
- value_vectors: bfloat16 [4, 8192, 256], P('dp', 'ctx', 'section'), may hold values from -6 to 6
- grad_output: bfloat16 [4, 8192, 1792], P('dp', 'ctx', 'section'), may hold values from -24 to 24
- output_dots: float32 [4, 14, 8192], P('dp', 'section', 'ctx'), may hold values from -12 to 12
- frame_ids: int32 [4, 8192], P('dp'), may hold values from 0 to 63, never falling along the last dimension, each value on 1 to 256 neighbouring positions
- visual_rows: int32 [4, 64, 32], P('dp', 'ctx'), may hold values from 0 to 127, as said below
- shuffle_source: int32 [4, 128, 64], P('dp', ('ctx', 'section')), may hold values from 0 to 63, each once within a row
- qkv_weight: bfloat16 [2304, 3584], P(None, ('section', 'dp')), may hold values from -0.125 to 0.125
- projector_weight: bfloat16 [3584, 2560], P(('section', 'dp')), may hold values from -0.09375 to 0.09375
Outputs:
- grad_keys: bfloat16 [4, 8192, 256], P('dp', 'ctx', 'section')
- grad_values: bfloat16 [4, 8192, 256], P('dp', 'ctx', 'section')
- patch_grads: bfloat16 [4, 8192, 640], P('dp', ('ctx', 'section'))
Inputs may be any that keep to these rules, and one draw needn't show every extreme that they name: `frame_ids`: frame numbers never fall along a sequence; a frame holds 1 to 256 tokens. `visual_rows`: each block of 128 tokens lists 32 distinct positions in increasing order. `shuffle_source`: each row is a permutation.
All inputs are finite; a program needn't handle non-finite values.
Results may differ from a plain program's by a relative error of at most 0.014.
Values may be sent and summed in bfloat16 or wider, within the bound.
No kernel may reach another device: no remote copies, remote signals or barrier semaphores. Data moves between devices by JAX's collectives and lax.ppermute only.
A program may use at most 128 MiB of HBM per device.

v0:
```python
import math

import jax
import jax.numpy as jnp
from jax import lax
from jax.sharding import PartitionSpec as P

HEAD_DIM = 128
GROUP = 7


MASKED = -1e30


def shifted(value, axis, steps):
    count = lax.axis_size(axis)
    pairs = [(source, (source + steps) % count) for source in range(count)]
    return lax.ppermute(value, axis, pairs)


def shards(
    query_vectors,
    key_vectors,
    value_vectors,
    grad_output,
    output_dots,
    frame_ids,
    visual_rows,
    shuffle_source,
    qkv_weight,
    projector_weight,
):
    loop_size = lax.axis_size("ctx")
    position = lax.axis_index("ctx")
    local_rows = query_vectors.shape[1]
    scale_factor = 1.0 / math.sqrt(HEAD_DIM)
    query_heads = query_vectors[0].reshape(local_rows, GROUP, HEAD_DIM)
    grad_heads = grad_output[0].reshape(local_rows, GROUP, HEAD_DIM)
    corrections = output_dots[0]
    frame_line = frame_ids[0]
    query_first = position * local_rows
    query_pos = query_first + jnp.arange(local_rows, dtype=jnp.int32)
    query_frames = lax.dynamic_slice_in_dim(frame_line, query_first, local_rows)
    last_frame = query_frames[local_rows - 1]
    own_pair = jnp.stack([key_vectors[0], value_vectors[0]])

    def key_mask(key_first, row_count):
        key_pos = key_first + jnp.arange(row_count, dtype=jnp.int32)
        key_frames = lax.dynamic_slice_in_dim(frame_line, key_first, row_count)
        allowed = (key_pos[None, :] <= query_pos[:, None]) | (
            key_frames[None, :] == query_frames[:, None]
        )
        return (allowed, key_frames[0] <= last_frame)

    def scores_for(key_block):
        return (
            jnp.einsum("qhd,kd->hqk", query_heads, key_block, preferred_element_type=jnp.float32)
            * scale_factor
        )

    start_pair = (
        jnp.full((GROUP, local_rows), MASKED, jnp.float32),
        jnp.zeros((GROUP, local_rows), jnp.float32),
    )
    key_block = lax.all_gather(key_vectors, "ctx", axis=1, tiled=True)[0]
    allowed, needed = key_mask(jnp.int32(0), key_block.shape[0])

    def update(pair_state):
        running, summed = pair_state
        scores = jnp.where(allowed[None], scores_for(key_block), MASKED)
        newest = jnp.maximum(running, scores.max(axis=-1))
        summed = jnp.exp(scores - newest[:, :, None]).sum(axis=-1)
        return (newest, summed)

    running, summed = lax.cond(needed, update, lambda unchanged: unchanged, start_pair)
    log_total = running + jnp.log(summed)

    def process(pair_block, grads_block, grad_query, block_index):
        allowed, needed = key_mask(block_index * local_rows, local_rows)

        def compute(state_now):
            grads_now, query_now = state_now
            key_block = pair_block[0]
            value_block = pair_block[1]
            probability = jnp.exp(
                jnp.where(allowed[None], scores_for(key_block) - log_total[:, :, None], MASKED)
            )
            probs_low = probability.astype(jnp.bfloat16)
            grad_probs = jnp.einsum(
                "qhd,kd->hqk", grad_heads, value_block, preferred_element_type=jnp.float32
            )
            grad_scores = (probability * (grad_probs - corrections[:, :, None])).astype(
                jnp.bfloat16
            )
            query_now = (
                query_now
                + jnp.einsum(
                    "hqk,kd->qhd", grad_scores, key_block, preferred_element_type=jnp.float32
                )
                * scale_factor
            )
            key_term = (
                jnp.einsum(
                    "hqk,qhd->kd", grad_scores, query_heads, preferred_element_type=jnp.float32
                )
                * scale_factor
            )
            value_term = jnp.einsum(
                "hqk,qhd->kd", probs_low, grad_heads, preferred_element_type=jnp.float32
            )
            return (grads_now + jnp.stack([key_term, value_term]), query_now)

        return lax.cond(needed, compute, lambda unchanged: unchanged, (grads_block, grad_query))

    def move_keys(pair_block, offset):
        return shifted(pair_block, "ctx", offset)

    def move_grads(grads_block, offset):
        return shifted(grads_block, "ctx", offset)

    zero_grads = jnp.zeros((2, local_rows, HEAD_DIM), jnp.float32)
    zero_query = jnp.zeros((local_rows, GROUP, HEAD_DIM), jnp.float32)

    def one_turn(turn_index, state_now):
        pair_block, grads_block, query_now = state_now
        grads_block, query_now = process(
            pair_block, grads_block, query_now, (position - turn_index) % loop_size
        )
        return (move_keys(pair_block, 1), move_grads(grads_block, 1), query_now)

    carried = (own_pair, zero_grads, zero_query)
    rounds = loop_size // 4

    def four_turns(round_index, state_now):
        for within in range(4):
            state_now = one_turn(round_index * 4 + within, state_now)
        return state_now

    carried = lax.fori_loop(0, rounds, four_turns, carried)
    final_pair, summed_grads, grad_query = carried
    grad_keys_low = summed_grads[0].astype(jnp.bfloat16)
    grad_values_low = summed_grads[1].astype(jnp.bfloat16)
    grad_query_low = grad_query.astype(jnp.bfloat16).reshape(local_rows, GROUP * HEAD_DIM)
    visual_picks = visual_rows[0, 0]
    chosen = jnp.concatenate(
        [grad_query_low[visual_picks], grad_keys_low[visual_picks], grad_values_low[visual_picks]],
        axis=1,
    )
    everyone = lax.all_gather(chosen[None], ("section", "dp"), axis=0, tiled=True)
    groups = lax.axis_size("section")
    replicas = lax.axis_size("dp")
    half_rows = visual_picks.shape[0] // 2
    width_in = chosen.shape[1]
    arranged = (
        everyone.reshape(groups, replicas, 2, half_rows, width_in)
        .transpose(2, 1, 3, 0, 4)
        .reshape(2 * replicas * half_rows, groups * width_in)
    )
    visual_grad = jnp.dot(arranged, qkv_weight, preferred_element_type=jnp.float32).astype(
        jnp.bfloat16
    )
    shuffled = lax.psum_scatter(
        jnp.dot(visual_grad, projector_weight, preferred_element_type=jnp.float32).astype(
            jnp.bfloat16
        ),
        ("section", "dp"),
        scatter_dimension=0,
        tiled=True,
    ).astype(jnp.float32)
    slot_rows = shuffled.reshape(half_rows * 4, projector_weight.shape[1] // 4)
    patches = slot_rows[shuffle_source[0, 0]].astype(jnp.bfloat16)
    return (grad_keys_low[None], grad_values_low[None], patches[None])


def solution(mesh):
    placed = (
        P("dp", "ctx", "section"),
        P("dp", "ctx", "section"),
        P("dp", "ctx", "section"),
        P("dp", "ctx", "section"),
        P("dp", "section", "ctx"),
        P("dp", None),
        P("dp", "ctx", None),
        P("dp", ("ctx", "section"), None),
        P(None, ("section", "dp")),
        P(("section", "dp"), None),
    )
    return jax.shard_map(
        shards,
        mesh=mesh,
        in_specs=placed,
        out_specs=(
            P("dp", "ctx", "section"),
            P("dp", "ctx", "section"),
            P("dp", ("ctx", "section"), None),
        ),
        check_vma=False,
    )
```

profile of v0, /device:TPU:1, one launch (start us, length us, event | category | flops | bytes accessed | tf_op | source)
XLA Modules:
  0.0 1166.7 jit_solution(5192859106076984340)
XLA Ops:
  18.1 78.3 %all-gather.3.cloned.1.call-done = bf16[1,8192,128]{2,1,0:T(8,128)(2,1)} async-done(((bf16[1,128,128]{2,1,0:T(8,128)(2,1)}), bf16[1,8192,128]{2,1,0:T(8,128)(2,1)}) %all-gather.3.cloned.1.call-update) | async-done | bytes 2097168 | tf_op jit(solution)/shard_map/all_gather | solution.py:65
  98.0 29.4 %conditional.5 = (f32[7,128]{1,0:T(8,128)}, f32[7,128]{1,0:T(8,128)S(1)}) conditional(s32[]{:T(128)} %convert_element_type.104, () %tuple.68, (s32[]{:T(128)}, s32[128,1]{0,1:T(1,128)S(1)}, s32[128,8192]{0,1:T(8,128)S(1)}, s32[8192]{0:T(1024)}, s32[128]{0:T(128)}, /*index=5*/bf16[1,8192,128]{2,1,0:T(8,128)(2,1)S(1)}, ...), branch_computations={%region_0.0_spmd, %region_1.4_spmd} | conditional | flops 1933573376 | bytes 68446736 | solution.py:75
  102.3 11.8 %fusion.2 = (f32[7,128]{1,0:T(8,128)S(1)}, f32[8192,128,7]{1,0,2:T(8,128)}) fusion(pred[128,8192]{0,1:T(8,128)(4,1)S(1)} %compare_or_fusion, bf16[128,7,128]{0,2,1:T(8,128)(2,1)S(1)} %get-tuple-element.612, bf16[1,8192,128]{2,1,0:T(8,128)(2,1)S(1)} %get-tuple-element.473), kind=kOutput, calls=%fused_computation.7 | convolution fusion | flops 1901067392 | bytes 32738816 | tf_op jit(solution)/shard_map/cond/branch_1_fun/qhd,kd->hqk/dot_general | solution.py:57
  114.7 12.7 %exponential_reduce_fusion = f32[7,128]{1,0:T(8,128)S(1)} fusion(f32[8192,128,7]{1,0,2:T(8,128)} %get-tuple-element.653, f32[7,128]{1,0:T(8,128)} %broadcast_maximum_fusion, pred[128,8192]{0,1:T(8,128)(4,1)S(1)} %compare_or_fusion), kind=kLoop, calls=%fused_computation.6 | loop fusion | flops 29359232 | bytes 30415872 | tf_op jit(solution)/shard_map/cond/branch_1_fun/reduce_sum | solution.py:72
  128.2 904.5 %while.20 = (s32[]{:T(128)}, bf16[2,128,128]{2,1,0:T(8,128)(2,1)S(1)}, f32[2,128,128]{2,1,0:T(8,128)S(1)}, f32[128,7,128]{2,0,1:T(8,128)S(1)}, s32[]{:T(128)}, /...) while((s32[]{:T(128)}, ...), condition=%wide.region_13.14_spmd.clone, body=%wide.region_4.13_spmd.clone.sunk | while | flops 591856320 | bytes 22070632 | solution.py:139
  145.0 6.1 collective-permute-start.5
  173.9 8.5 collective-permute-done.3
  201.3 6.5 collective-permute-done.5
  213.4 5.2 collective-permute-done.6
  224.9 9.6 collective-permute-done.3
  242.8 5.3 collective-permute-done.4
  253.2 8.4 collective-permute-done.5
  267.5 5.7 collective-permute-done.6
  278.0 10.2 collective-permute-done.3
  306.4 8.4 collective-permute-done.5
  320.4 5.7 collective-permute-done.6
  330.9 9.7 collective-permute-done.3
  359.3 10.4 collective-permute-done.5
  375.3 6.9 collective-permute-done.6
  387.1 9.7 collective-permute-done.3
  415.4 9.3 collective-permute-done.5
  430.3 8.0 collective-permute-done.6
  442.7 12.1 %collective-permute-done.3 = bf16[2,128,128]{2,1,0:T(8,128)(2,1)S(1)} collective-permute-done((bf16[2,128,128]{2,1,0:T(8,128)(2,1)}, bf16[2,128,128]{2,1,0:T(8,128)(2,1)S(1)}, u32[]{:S(2)}, u32[]{:S(2)}) %collective-permute-start.3) | collective-permute-done | bytes 65568 | tf_op jit(solution)/shard_map/while/body/eval_jaxpr/ppermute | solution.py:18
  463.1 6.9 collective-permute-done.4
  475.2 11.0 collective-permute-done.5
  491.1 6.8 collective-permute-done.6
  502.8 10.8 collective-permute-done.3
  521.8 6.1 collective-permute-done.4
  533.6 8.2 collective-permute-done.5
  547.4 5.7 collective-permute-done.6
  558.1 10.6 collective-permute-done.3
  576.9 5.7 collective-permute-done.4
  588.3 9.5 collective-permute-done.5
  603.3 6.6 collective-permute-done.6
  614.8 10.6 collective-permute-done.3
  633.7 6.5 collective-permute-done.4
  645.4 10.1 collective-permute-done.5
  661.0 7.9 collective-permute-done.6
  674.2 11.6 collective-permute-done.3
  694.0 5.6 collective-permute-done.4
  705.9 11.6 collective-permute-done.5
  722.5 5.7 collective-permute-done.6
  733.1 11.1 collective-permute-done.3
  762.9 9.4 collective-permute-done.5
  777.9 5.7 collective-permute-done.6
  788.4 10.0 collective-permute-done.3
  806.7 5.6 collective-permute-done.4
  818.0 9.5 collective-permute-done.5
  833.1 7.3 collective-permute-done.6
  845.0 13.0 %collective-permute-done.3 = bf16[2,128,128]{2,1,0:T(8,128)(2,1)S(1)} collective-permute-done((bf16[2,128,128]{2,1,0:T(8,128)(2,1)}, bf16[2,128,128]{2,1,0:T(8,128)(2,1)S(1)}, u32[]{:S(2)}, u32[]{:S(2)}) %collective-permute-start.3) | collective-permute-done | bytes 65568 | tf_op jit(solution)/shard_map/while/body/eval_jaxpr/ppermute | solution.py:18
  866.3 6.4 collective-permute-done.4
  878.7 10.2 collective-permute-done.5
  895.5 6.7 collective-permute-done.6
  908.0 11.8 %collective-permute-done.3 = bf16[2,128,128]{2,1,0:T(8,128)(2,1)S(1)} collective-permute-done((bf16[2,128,128]{2,1,0:T(8,128)(2,1)}, bf16[2,128,128]{2,1,0:T(8,128)(2,1)S(1)}, u32[]{:S(2)}, u32[]{:S(2)}) %collective-permute-start.3) | collective-permute-done | bytes 65568 | tf_op jit(solution)/shard_map/while/body/eval_jaxpr/ppermute | solution.py:18
  928.1 5.8 collective-permute-done.4
  940.5 9.9 collective-permute-done.5
  957.1 6.3 collective-permute-done.6
  969.1 10.9 collective-permute-done.3
  998.1 7.4 collective-permute-done.5
  1011.1 4.9 collective-permute-done.6
  1017.0 5.2 conditional.17
  1026.1 6.6 collective-permute-done.3
  1035.3 87.0 %all-gather = bf16[256,1152]{1,0:T(8,128)(2,1)S(1)} all-gather(bf16[32,1152]{1,0:T(8,128)(2,1)S(1)} %pad_maximum_fusion), channel_id=2, replica_groups=mesh['ctx'=64,'section'=2,'dp'=4] {'section','dp'}, dimensions={0}, use_global_device_ids=true | all-gather | bytes 663552 | tf_op jit(solution)/shard_map/all_gather | solution.py:149
  1126.8 30.8 %reduce-scatter.2.cloned.1.call-done = bf16[16,2560]{1,0:T(8,128)(2,1)} async-done(((bf16[128,2560]{1,0:T(8,128)(2,1)}), bf16[16,2560]{1,0:T(8,128)(2,1)}) %reduce-scatter.2.cloned.1.call-update) | async-done | bytes 81936 | tf_op jit(solution)/shard_map/reduce_scatter | solution.py:162
  (472 shorter events, 421.5 us)
Async XLA Ops:
  7.2 89.2 %all-gather.3.cloned.1.call-start = ((), (), s32[]{:S(2)}) async-start(), calls=%async_computation.1 | async-start | bytes 2129920 | tf_op jit(solution)/shard_map/all_gather | solution.py:65
  7.9 1149.7 %reduce-scatter.2.cloned.1.call-start = ((), (), s32[]{:S(2)}) async-start(), calls=%async_computation.2 | async-start | bytes 737280 | tf_op jit(solution)/shard_map/reduce_scatter | solution.py:162
  170.0 12.3 %collective-permute-start.7 = (f32[2,128,128]{2,1,0:T(8,128)}, f32[2,128,128]{2,1,0:T(8,128)S(1)}, u32[]{:S(2)}, u32[]{:S(2)}) collective-permute-start(f32[2,128,128]{2,1,0:T(8,128)} %get-tuple-element.764), channel_id=1, source_target_pairs={{0,8},{8,16},{16,24},{24,32},{32,40},{40,48},{48,56},{56,64},{64,7... | collective-permute-start | bytes 393224 | tf_op jit(solution)/shard_map/while/body/eval_jaxpr/ppermute | solution.py:18
  196.0 11.9 %collective-permute-start.5 = (f32[2,128,128]{2,1,0:T(8,128)}, f32[2,128,128]{2,1,0:T(8,128)}, u32[]{:S(2)}, u32[]{:S(2)}) collective-permute-start(f32[2,128,128]{2,1,0:T(8,128)} %get-tuple-element.760), channel_id=1, source_target_pairs={{0,8},{8,16},{16,24},{24,32},{32,40},{40,48},{48,56},{56,64},{64,7... | collective-permute-start | bytes 393224 | tf_op jit(solution)/shard_map/while/body/eval_jaxpr/ppermute | solution.py:18
  220.3 14.2 %collective-permute-start.7 = (f32[2,128,128]{2,1,0:T(8,128)}, f32[2,128,128]{2,1,0:T(8,128)S(1)}, u32[]{:S(2)}, u32[]{:S(2)}) collective-permute-start(f32[2,128,128]{2,1,0:T(8,128)} %get-tuple-element.764), channel_id=1, source_target_pairs={{0,8},{8,16},{16,24},{24,32},{32,40},{40,48},{48,56},{56,64},{64,7... | collective-permute-start | bytes 393224 | tf_op jit(solution)/shard_map/while/body/eval_jaxpr/ppermute | solution.py:18
  222.2 12.3 %collective-permute-start.3 = (bf16[2,128,128]{2,1,0:T(8,128)(2,1)}, bf16[2,128,128]{2,1,0:T(8,128)(2,1)S(1)}, u32[]{:S(2)}, u32[]{:S(2)}) collective-permute-start(bf16[2,128,128]{2,1,0:T(8,128)(2,1)} %collective-permute-done.2), channel_id=1, source_target_pairs={{0,8},{8,16},{16,24},{24,32},{32,40},{40,48},{48,56},{56,64},{64,7... | collective-permute-start | bytes 196616 | tf_op jit(solution)/shard_map/while/body/eval_jaxpr/ppermute | solution.py:18
  248.8 12.8 %collective-permute-start.5 = (f32[2,128,128]{2,1,0:T(8,128)}, f32[2,128,128]{2,1,0:T(8,128)}, u32[]{:S(2)}, u32[]{:S(2)}) collective-permute-start(f32[2,128,128]{2,1,0:T(8,128)} %get-tuple-element.760), channel_id=1, source_target_pairs={{0,8},{8,16},{16,24},{24,32},{32,40},{40,48},{48,56},{56,64},{64,7... | collective-permute-start | bytes 393224 | tf_op jit(solution)/shard_map/while/body/eval_jaxpr/ppermute | solution.py:18
  250.7 12.3 %collective-permute-start.1 = (bf16[2,128,128]{2,1,0:T(8,128)(2,1)}, bf16[2,128,128]{2,1,0:T(8,128)(2,1)S(1)}, u32[]{:S(2)}, u32[]{:S(2)}) collective-permute-start(bf16[2,128,128]{2,1,0:T(8,128)(2,1)} %collective-permute-done), channel_id=1, source_target_pairs={{0,8},{8,16},{16,24},{24,32},{32,40},{40,48},{48,56},{56,64},{64,7... | collective-permute-start | bytes 196616 | tf_op jit(solution)/shard_map/while/body/eval_jaxpr/ppermute | solution.py:18
  274.2 14.1 %collective-permute-start.7 = (f32[2,128,128]{2,1,0:T(8,128)}, f32[2,128,128]{2,1,0:T(8,128)S(1)}, u32[]{:S(2)}, u32[]{:S(2)}) collective-permute-start(f32[2,128,128]{2,1,0:T(8,128)} %get-tuple-element.764), channel_id=1, source_target_pairs={{0,8},{8,16},{16,24},{24,32},{32,40},{40,48},{48,56},{56,64},{64,7... | collective-permute-start | bytes 393224 | tf_op jit(solution)/shard_map/while/body/eval_jaxpr/ppermute | solution.py:18
  276.1 12.1 %collective-permute-start.3 = (bf16[2,128,128]{2,1,0:T(8,128)(2,1)}, bf16[2,128,128]{2,1,0:T(8,128)(2,1)S(1)}, u32[]{:S(2)}, u32[]{:S(2)}) collective-permute-start(bf16[2,128,128]{2,1,0:T(8,128)(2,1)} %collective-permute-done.2), channel_id=1, source_target_pairs={{0,8},{8,16},{16,24},{24,32},{32,40},{40,48},{48,56},{56,64},{64,7... | collective-permute-start | bytes 196616 | tf_op jit(solution)/shard_map/while/body/eval_jaxpr/ppermute | solution.py:18
  302.0 12.8 %collective-permute-start.5 = (f32[2,128,128]{2,1,0:T(8,128)}, f32[2,128,128]{2,1,0:T(8,128)}, u32[]{:S(2)}, u32[]{:S(2)}) collective-permute-start(f32[2,128,128]{2,1,0:T(8,128)} %get-tuple-element.760), channel_id=1, source_target_pairs={{0,8},{8,16},{16,24},{24,32},{32,40},{40,48},{48,56},{56,64},{64,7... | collective-permute-start | bytes 393224 | tf_op jit(solution)/shard_map/while/body/eval_jaxpr/ppermute | solution.py:18
  303.9 12.0 %collective-permute-start.1 = (bf16[2,128,128]{2,1,0:T(8,128)(2,1)}, bf16[2,128,128]{2,1,0:T(8,128)(2,1)S(1)}, u32[]{:S(2)}, u32[]{:S(2)}) collective-permute-start(bf16[2,128,128]{2,1,0:T(8,128)(2,1)} %collective-permute-done), channel_id=1, source_target_pairs={{0,8},{8,16},{16,24},{24,32},{32,40},{40,48},{48,56},{56,64},{64,7... | collective-permute-start | bytes 196616 | tf_op jit(solution)/shard_map/while/body/eval_jaxpr/ppermute | solution.py:18
  327.1 13.6 %collective-permute-start.7 = (f32[2,128,128]{2,1,0:T(8,128)}, f32[2,128,128]{2,1,0:T(8,128)S(1)}, u32[]{:S(2)}, u32[]{:S(2)}) collective-permute-start(f32[2,128,128]{2,1,0:T(8,128)} %get-tuple-element.764), channel_id=1, source_target_pairs={{0,8},{8,16},{16,24},{24,32},{32,40},{40,48},{48,56},{56,64},{64,7... | collective-permute-start | bytes 393224 | tf_op jit(solution)/shard_map/while/body/eval_jaxpr/ppermute | solution.py:18
  329.0 11.7 %collective-permute-start.3 = (bf16[2,128,128]{2,1,0:T(8,128)(2,1)}, bf16[2,128,128]{2,1,0:T(8,128)(2,1)S(1)}, u32[]{:S(2)}, u32[]{:S(2)}) collective-permute-start(bf16[2,128,128]{2,1,0:T(8,128)(2,1)} %collective-permute-done.2), channel_id=1, source_target_pairs={{0,8},{8,16},{16,24},{24,32},{32,40},{40,48},{48,56},{56,64},{64,7... | collective-permute-start | bytes 196616 | tf_op jit(solution)/shard_map/while/body/eval_jaxpr/ppermute | solution.py:18
  354.9 14.9 %collective-permute-start.5 = (f32[2,128,128]{2,1,0:T(8,128)}, f32[2,128,128]{2,1,0:T(8,128)}, u32[]{:S(2)}, u32[]{:S(2)}) collective-permute-start(f32[2,128,128]{2,1,0:T(8,128)} %get-tuple-element.760), channel_id=1, source_target_pairs={{0,8},{8,16},{16,24},{24,32},{32,40},{40,48},{48,56},{56,64},{64,7... | collective-permute-start | bytes 393224 | tf_op jit(solution)/shard_map/while/body/eval_jaxpr/ppermute | solution.py:18
  356.8 14.1 %collective-permute-start.1 = (bf16[2,128,128]{2,1,0:T(8,128)(2,1)}, bf16[2,128,128]{2,1,0:T(8,128)(2,1)S(1)}, u32[]{:S(2)}, u32[]{:S(2)}) collective-permute-start(bf16[2,128,128]{2,1,0:T(8,128)(2,1)} %collective-permute-done), channel_id=1, source_target_pairs={{0,8},{8,16},{16,24},{24,32},{32,40},{40,48},{48,56},{56,64},{64,7... | collective-permute-start | bytes 196616 | tf_op jit(solution)/shard_map/while/body/eval_jaxpr/ppermute | solution.py:18
  383.2 13.6 %collective-permute-start.7 = (f32[2,128,128]{2,1,0:T(8,128)}, f32[2,128,128]{2,1,0:T(8,128)S(1)}, u32[]{:S(2)}, u32[]{:S(2)}) collective-permute-start(f32[2,128,128]{2,1,0:T(8,128)} %get-tuple-element.764), channel_id=1, source_target_pairs={{0,8},{8,16},{16,24},{24,32},{32,40},{40,48},{48,56},{56,64},{64,7... | collective-permute-start | bytes 393224 | tf_op jit(solution)/shard_map/while/body/eval_jaxpr/ppermute | solution.py:18
  385.2 11.6 collective-permute-start.3
  411.0 13.8 %collective-permute-start.5 = (f32[2,128,128]{2,1,0:T(8,128)}, f32[2,128,128]{2,1,0:T(8,128)}, u32[]{:S(2)}, u32[]{:S(2)}) collective-permute-start(f32[2,128,128]{2,1,0:T(8,128)} %get-tuple-element.760), channel_id=1, source_target_pairs={{0,8},{8,16},{16,24},{24,32},{32,40},{40,48},{48,56},{56,64},{64,7... | collective-permute-start | bytes 393224 | tf_op jit(solution)/shard_map/while/body/eval_jaxpr/ppermute | solution.py:18
  412.9 13.0 %collective-permute-start.1 = (bf16[2,128,128]{2,1,0:T(8,128)(2,1)}, bf16[2,128,128]{2,1,0:T(8,128)(2,1)S(1)}, u32[]{:S(2)}, u32[]{:S(2)}) collective-permute-start(bf16[2,128,128]{2,1,0:T(8,128)(2,1)} %collective-permute-done), channel_id=1, source_target_pairs={{0,8},{8,16},{16,24},{24,32},{32,40},{40,48},{48,56},{56,64},{64,7... | collective-permute-start | bytes 196616 | tf_op jit(solution)/shard_map/while/body/eval_jaxpr/ppermute | solution.py:18
  425.8 12.5 %collective-permute-start.6 = (f32[2,128,128]{2,1,0:T(8,128)}, f32[2,128,128]{2,1,0:T(8,128)}, u32[]{:S(2)}, u32[]{:S(2)}) collective-permute-start(f32[2,128,128]{2,1,0:T(8,128)} %get-tuple-element.762), channel_id=1, source_target_pairs={{0,8},{8,16},{16,24},{24,32},{32,40},{40,48},{48,56},{56,64},{64,7... | collective-permute-start | bytes 393224 | tf_op jit(solution)/shard_map/while/body/eval_jaxpr/ppermute | solution.py:18
  438.8 16.0 %collective-permute-start.7 = (f32[2,128,128]{2,1,0:T(8,128)}, f32[2,128,128]{2,1,0:T(8,128)S(1)}, u32[]{:S(2)}, u32[]{:S(2)}) collective-permute-start(f32[2,128,128]{2,1,0:T(8,128)} %get-tuple-element.764), channel_id=1, source_target_pairs={{0,8},{8,16},{16,24},{24,32},{32,40},{40,48},{48,56},{56,64},{64,7... | collective-permute-start | bytes 393224 | tf_op jit(solution)/shard_map/while/body/eval_jaxpr/ppermute | solution.py:18
  440.8 14.1 %collective-permute-start.3 = (bf16[2,128,128]{2,1,0:T(8,128)(2,1)}, bf16[2,128,128]{2,1,0:T(8,128)(2,1)S(1)}, u32[]{:S(2)}, u32[]{:S(2)}) collective-permute-start(bf16[2,128,128]{2,1,0:T(8,128)(2,1)} %collective-permute-done.2), channel_id=1, source_target_pairs={{0,8},{8,16},{16,24},{24,32},{32,40},{40,48},{48,56},{56,64},{64,7... | collective-permute-start | bytes 196616 | tf_op jit(solution)/shard_map/while/body/eval_jaxpr/ppermute | solution.py:18
  458.0 12.0 %collective-permute-start.4 = (f32[2,128,128]{2,1,0:T(8,128)S(1)}, f32[2,128,128]{2,1,0:T(8,128)}, u32[]{:S(2)}, u32[]{:S(2)}) collective-permute-start(f32[2,128,128]{2,1,0:T(8,128)S(1)} %get-tuple-element.758), channel_id=1, source_target_pairs={{0,8},{8,16},{16,24},{24,32},{32,40},{40,48},{48,56},{56,64},{64,7... | collective-permute-start | bytes 393224 | tf_op jit(solution)/shard_map/while/body/eval_jaxpr/ppermute | solution.py:18
  470.7 15.4 %collective-permute-start.5 = (f32[2,128,128]{2,1,0:T(8,128)}, f32[2,128,128]{2,1,0:T(8,128)}, u32[]{:S(2)}, u32[]{:S(2)}) collective-permute-start(f32[2,128,128]{2,1,0:T(8,128)} %get-tuple-element.760), channel_id=1, source_target_pairs={{0,8},{8,16},{16,24},{24,32},{32,40},{40,48},{48,56},{56,64},{64,7... | collective-permute-start | bytes 393224 | tf_op jit(solution)/shard_map/while/body/eval_jaxpr/ppermute | solution.py:18
  472.6 14.1 %collective-permute-start.1 = (bf16[2,128,128]{2,1,0:T(8,128)(2,1)}, bf16[2,128,128]{2,1,0:T(8,128)(2,1)S(1)}, u32[]{:S(2)}, u32[]{:S(2)}) collective-permute-start(bf16[2,128,128]{2,1,0:T(8,128)(2,1)} %collective-permute-done), channel_id=1, source_target_pairs={{0,8},{8,16},{16,24},{24,32},{32,40},{40,48},{48,56},{56,64},{64,7... | collective-permute-start | bytes 196616 | tf_op jit(solution)/shard_map/while/body/eval_jaxpr/ppermute | solution.py:18
  498.9 14.6 %collective-permute-start.7 = (f32[2,128,128]{2,1,0:T(8,128)}, f32[2,128,128]{2,1,0:T(8,128)S(1)}, u32[]{:S(2)}, u32[]{:S(2)}) collective-permute-start(f32[2,128,128]{2,1,0:T(8,128)} %get-tuple-element.764), channel_id=1, source_target_pairs={{0,8},{8,16},{16,24},{24,32},{32,40},{40,48},{48,56},{56,64},{64,7... | collective-permute-start | bytes 393224 | tf_op jit(solution)/shard_map/while/body/eval_jaxpr/ppermute | solution.py:18
  500.9 12.7 %collective-permute-start.3 = (bf16[2,128,128]{2,1,0:T(8,128)(2,1)}, bf16[2,128,128]{2,1,0:T(8,128)(2,1)S(1)}, u32[]{:S(2)}, u32[]{:S(2)}) collective-permute-start(bf16[2,128,128]{2,1,0:T(8,128)(2,1)} %collective-permute-done.2), channel_id=1, source_target_pairs={{0,8},{8,16},{16,24},{24,32},{32,40},{40,48},{48,56},{56,64},{64,7... | collective-permute-start | bytes 196616 | tf_op jit(solution)/shard_map/while/body/eval_jaxpr/ppermute | solution.py:18
  529.2 12.7 %collective-permute-start.5 = (f32[2,128,128]{2,1,0:T(8,128)}, f32[2,128,128]{2,1,0:T(8,128)}, u32[]{:S(2)}, u32[]{:S(2)}) collective-permute-start(f32[2,128,128]{2,1,0:T(8,128)} %get-tuple-element.760), channel_id=1, source_target_pairs={{0,8},{8,16},{16,24},{24,32},{32,40},{40,48},{48,56},{56,64},{64,7... | collective-permute-start | bytes 393224 | tf_op jit(solution)/shard_map/while/body/eval_jaxpr/ppermute | solution.py:18
  531.1 11.9 %collective-permute-start.1 = (bf16[2,128,128]{2,1,0:T(8,128)(2,1)}, bf16[2,128,128]{2,1,0:T(8,128)(2,1)S(1)}, u32[]{:S(2)}, u32[]{:S(2)}) collective-permute-start(bf16[2,128,128]{2,1,0:T(8,128)(2,1)} %collective-permute-done), channel_id=1, source_target_pairs={{0,8},{8,16},{16,24},{24,32},{32,40},{40,48},{48,56},{56,64},{64,7... | collective-permute-start | bytes 196616 | tf_op jit(solution)/shard_map/while/body/eval_jaxpr/ppermute | solution.py:18
  554.2 14.4 %collective-permute-start.7 = (f32[2,128,128]{2,1,0:T(8,128)}, f32[2,128,128]{2,1,0:T(8,128)S(1)}, u32[]{:S(2)}, u32[]{:S(2)}) collective-permute-start(f32[2,128,128]{2,1,0:T(8,128)} %get-tuple-element.764), channel_id=1, source_target_pairs={{0,8},{8,16},{16,24},{24,32},{32,40},{40,48},{48,56},{56,64},{64,7... | collective-permute-start | bytes 393224 | tf_op jit(solution)/shard_map/while/body/eval_jaxpr/ppermute | solution.py:18
  556.1 12.5 %collective-permute-start.3 = (bf16[2,128,128]{2,1,0:T(8,128)(2,1)}, bf16[2,128,128]{2,1,0:T(8,128)(2,1)S(1)}, u32[]{:S(2)}, u32[]{:S(2)}) collective-permute-start(bf16[2,128,128]{2,1,0:T(8,128)(2,1)} %collective-permute-done.2), channel_id=1, source_target_pairs={{0,8},{8,16},{16,24},{24,32},{32,40},{40,48},{48,56},{56,64},{64,7... | collective-permute-start | bytes 196616 | tf_op jit(solution)/shard_map/while/body/eval_jaxpr/ppermute | solution.py:18
  583.8 13.9 %collective-permute-start.5 = (f32[2,128,128]{2,1,0:T(8,128)}, f32[2,128,128]{2,1,0:T(8,128)}, u32[]{:S(2)}, u32[]{:S(2)}) collective-permute-start(f32[2,128,128]{2,1,0:T(8,128)} %get-tuple-element.760), channel_id=1, source_target_pairs={{0,8},{8,16},{16,24},{24,32},{32,40},{40,48},{48,56},{56,64},{64,7... | collective-permute-start | bytes 393224 | tf_op jit(solution)/shard_map/while/body/eval_jaxpr/ppermute | solution.py:18
  585.7 13.1 %collective-permute-start.1 = (bf16[2,128,128]{2,1,0:T(8,128)(2,1)}, bf16[2,128,128]{2,1,0:T(8,128)(2,1)S(1)}, u32[]{:S(2)}, u32[]{:S(2)}) collective-permute-start(bf16[2,128,128]{2,1,0:T(8,128)(2,1)} %collective-permute-done), channel_id=1, source_target_pairs={{0,8},{8,16},{16,24},{24,32},{32,40},{40,48},{48,56},{56,64},{64,7... | collective-permute-start | bytes 196616 | tf_op jit(solution)/shard_map/while/body/eval_jaxpr/ppermute | solution.py:18
  611.0 14.5 %collective-permute-start.7 = (f32[2,128,128]{2,1,0:T(8,128)}, f32[2,128,128]{2,1,0:T(8,128)S(1)}, u32[]{:S(2)}, u32[]{:S(2)}) collective-permute-start(f32[2,128,128]{2,1,0:T(8,128)} %get-tuple-element.764), channel_id=1, source_target_pairs={{0,8},{8,16},{16,24},{24,32},{32,40},{40,48},{48,56},{56,64},{64,7... | collective-permute-start | bytes 393224 | tf_op jit(solution)/shard_map/while/body/eval_jaxpr/ppermute | solution.py:18
  612.9 12.5 %collective-permute-start.3 = (bf16[2,128,128]{2,1,0:T(8,128)(2,1)}, bf16[2,128,128]{2,1,0:T(8,128)(2,1)S(1)}, u32[]{:S(2)}, u32[]{:S(2)}) collective-permute-start(bf16[2,128,128]{2,1,0:T(8,128)(2,1)} %collective-permute-done.2), channel_id=1, source_target_pairs={{0,8},{8,16},{16,24},{24,32},{32,40},{40,48},{48,56},{56,64},{64,7... | collective-permute-start | bytes 196616 | tf_op jit(solution)/shard_map/while/body/eval_jaxpr/ppermute | solution.py:18
  640.9 14.5 %collective-permute-start.5 = (f32[2,128,128]{2,1,0:T(8,128)}, f32[2,128,128]{2,1,0:T(8,128)}, u32[]{:S(2)}, u32[]{:S(2)}) collective-permute-start(f32[2,128,128]{2,1,0:T(8,128)} %get-tuple-element.760), channel_id=1, source_target_pairs={{0,8},{8,16},{16,24},{24,32},{32,40},{40,48},{48,56},{56,64},{64,7... | collective-permute-start | bytes 393224 | tf_op jit(solution)/shard_map/while/body/eval_jaxpr/ppermute | solution.py:18
  642.9 13.7 %collective-permute-start.1 = (bf16[2,128,128]{2,1,0:T(8,128)(2,1)}, bf16[2,128,128]{2,1,0:T(8,128)(2,1)S(1)}, u32[]{:S(2)}, u32[]{:S(2)}) collective-permute-start(bf16[2,128,128]{2,1,0:T(8,128)(2,1)} %collective-permute-done), channel_id=1, source_target_pairs={{0,8},{8,16},{16,24},{24,32},{32,40},{40,48},{48,56},{56,64},{64,7... | collective-permute-start | bytes 196616 | tf_op jit(solution)/shard_map/while/body/eval_jaxpr/ppermute | solution.py:18
  656.6 12.4 %collective-permute-start.6 = (f32[2,128,128]{2,1,0:T(8,128)}, f32[2,128,128]{2,1,0:T(8,128)}, u32[]{:S(2)}, u32[]{:S(2)}) collective-permute-start(f32[2,128,128]{2,1,0:T(8,128)} %get-tuple-element.762), channel_id=1, source_target_pairs={{0,8},{8,16},{16,24},{24,32},{32,40},{40,48},{48,56},{56,64},{64,7... | collective-permute-start | bytes 393224 | tf_op jit(solution)/shard_map/while/body/eval_jaxpr/ppermute | solution.py:18
  658.5 11.9 %collective-permute-start.2 = (bf16[2,128,128]{2,1,0:T(8,128)(2,1)S(1)}, bf16[2,128,128]{2,1,0:T(8,128)(2,1)}, u32[]{:S(2)}, u32[]{:S(2)}) collective-permute-start(bf16[2,128,128]{2,1,0:T(8,128)(2,1)S(1)} %collective-permute-done.1), channel_id=1, source_target_pairs={{0,8},{8,16},{16,24},{24,32},{32,40},{40,48},{48,56},{56,64},{64,7... | collective-permute-start | bytes 196616 | tf_op jit(solution)/shard_map/while/body/eval_jaxpr/ppermute | solution.py:18
  670.4 15.4 %collective-permute-start.7 = (f32[2,128,128]{2,1,0:T(8,128)}, f32[2,128,128]{2,1,0:T(8,128)S(1)}, u32[]{:S(2)}, u32[]{:S(2)}) collective-permute-start(f32[2,128,128]{2,1,0:T(8,128)} %get-tuple-element.764), channel_id=1, source_target_pairs={{0,8},{8,16},{16,24},{24,32},{32,40},{40,48},{48,56},{56,64},{64,7... | collective-permute-start | bytes 393224 | tf_op jit(solution)/shard_map/while/body/eval_jaxpr/ppermute | solution.py:18
  672.3 13.5 %collective-permute-start.3 = (bf16[2,128,128]{2,1,0:T(8,128)(2,1)}, bf16[2,128,128]{2,1,0:T(8,128)(2,1)S(1)}, u32[]{:S(2)}, u32[]{:S(2)}) collective-permute-start(bf16[2,128,128]{2,1,0:T(8,128)(2,1)} %collective-permute-done.2), channel_id=1, source_target_pairs={{0,8},{8,16},{16,24},{24,32},{32,40},{40,48},{48,56},{56,64},{64,7... | collective-permute-start | bytes 196616 | tf_op jit(solution)/shard_map/while/body/eval_jaxpr/ppermute | solution.py:18
  701.5 16.1 %collective-permute-start.5 = (f32[2,128,128]{2,1,0:T(8,128)}, f32[2,128,128]{2,1,0:T(8,128)}, u32[]{:S(2)}, u32[]{:S(2)}) collective-permute-start(f32[2,128,128]{2,1,0:T(8,128)} %get-tuple-element.760), channel_id=1, source_target_pairs={{0,8},{8,16},{16,24},{24,32},{32,40},{40,48},{48,56},{56,64},{64,7... | collective-permute-start | bytes 393224 | tf_op jit(solution)/shard_map/while/body/eval_jaxpr/ppermute | solution.py:18
  703.4 14.6 %collective-permute-start.1 = (bf16[2,128,128]{2,1,0:T(8,128)(2,1)}, bf16[2,128,128]{2,1,0:T(8,128)(2,1)S(1)}, u32[]{:S(2)}, u32[]{:S(2)}) collective-permute-start(bf16[2,128,128]{2,1,0:T(8,128)(2,1)} %collective-permute-done), channel_id=1, source_target_pairs={{0,8},{8,16},{16,24},{24,32},{32,40},{40,48},{48,56},{56,64},{64,7... | collective-permute-start | bytes 196616 | tf_op jit(solution)/shard_map/while/body/eval_jaxpr/ppermute | solution.py:18
  729.2 14.9 %collective-permute-start.7 = (f32[2,128,128]{2,1,0:T(8,128)}, f32[2,128,128]{2,1,0:T(8,128)S(1)}, u32[]{:S(2)}, u32[]{:S(2)}) collective-permute-start(f32[2,128,128]{2,1,0:T(8,128)} %get-tuple-element.764), channel_id=1, source_target_pairs={{0,8},{8,16},{16,24},{24,32},{32,40},{40,48},{48,56},{56,64},{64,7... | collective-permute-start | bytes 393224 | tf_op jit(solution)/shard_map/while/body/eval_jaxpr/ppermute | solution.py:18
  731.1 13.0 %collective-permute-start.3 = (bf16[2,128,128]{2,1,0:T(8,128)(2,1)}, bf16[2,128,128]{2,1,0:T(8,128)(2,1)S(1)}, u32[]{:S(2)}, u32[]{:S(2)}) collective-permute-start(bf16[2,128,128]{2,1,0:T(8,128)(2,1)} %collective-permute-done.2), channel_id=1, source_target_pairs={{0,8},{8,16},{16,24},{24,32},{32,40},{40,48},{48,56},{56,64},{64,7... | collective-permute-start | bytes 196616 | tf_op jit(solution)/shard_map/while/body/eval_jaxpr/ppermute | solution.py:18
  758.4 13.9 %collective-permute-start.5 = (f32[2,128,128]{2,1,0:T(8,128)}, f32[2,128,128]{2,1,0:T(8,128)}, u32[]{:S(2)}, u32[]{:S(2)}) collective-permute-start(f32[2,128,128]{2,1,0:T(8,128)} %get-tuple-element.760), channel_id=1, source_target_pairs={{0,8},{8,16},{16,24},{24,32},{32,40},{40,48},{48,56},{56,64},{64,7... | collective-permute-start | bytes 393224 | tf_op jit(solution)/shard_map/while/body/eval_jaxpr/ppermute | solution.py:18
  760.3 13.1 %collective-permute-start.1 = (bf16[2,128,128]{2,1,0:T(8,128)(2,1)}, bf16[2,128,128]{2,1,0:T(8,128)(2,1)S(1)}, u32[]{:S(2)}, u32[]{:S(2)}) collective-permute-start(bf16[2,128,128]{2,1,0:T(8,128)(2,1)} %collective-permute-done), channel_id=1, source_target_pairs={{0,8},{8,16},{16,24},{24,32},{32,40},{40,48},{48,56},{56,64},{64,7... | collective-permute-start | bytes 196616 | tf_op jit(solution)/shard_map/while/body/eval_jaxpr/ppermute | solution.py:18
  784.6 13.9 %collective-permute-start.7 = (f32[2,128,128]{2,1,0:T(8,128)}, f32[2,128,128]{2,1,0:T(8,128)S(1)}, u32[]{:S(2)}, u32[]{:S(2)}) collective-permute-start(f32[2,128,128]{2,1,0:T(8,128)} %get-tuple-element.764), channel_id=1, source_target_pairs={{0,8},{8,16},{16,24},{24,32},{32,40},{40,48},{48,56},{56,64},{64,7... | collective-permute-start | bytes 393224 | tf_op jit(solution)/shard_map/while/body/eval_jaxpr/ppermute | solution.py:18
  786.5 12.0 %collective-permute-start.3 = (bf16[2,128,128]{2,1,0:T(8,128)(2,1)}, bf16[2,128,128]{2,1,0:T(8,128)(2,1)S(1)}, u32[]{:S(2)}, u32[]{:S(2)}) collective-permute-start(bf16[2,128,128]{2,1,0:T(8,128)(2,1)} %collective-permute-done.2), channel_id=1, source_target_pairs={{0,8},{8,16},{16,24},{24,32},{32,40},{40,48},{48,56},{56,64},{64,7... | collective-permute-start | bytes 196616 | tf_op jit(solution)/shard_map/while/body/eval_jaxpr/ppermute | solution.py:18
  813.6 14.0 %collective-permute-start.5 = (f32[2,128,128]{2,1,0:T(8,128)}, f32[2,128,128]{2,1,0:T(8,128)}, u32[]{:S(2)}, u32[]{:S(2)}) collective-permute-start(f32[2,128,128]{2,1,0:T(8,128)} %get-tuple-element.760), channel_id=1, source_target_pairs={{0,8},{8,16},{16,24},{24,32},{32,40},{40,48},{48,56},{56,64},{64,7... | collective-permute-start | bytes 393224 | tf_op jit(solution)/shard_map/while/body/eval_jaxpr/ppermute | solution.py:18
  815.5 13.2 %collective-permute-start.1 = (bf16[2,128,128]{2,1,0:T(8,128)(2,1)}, bf16[2,128,128]{2,1,0:T(8,128)(2,1)S(1)}, u32[]{:S(2)}, u32[]{:S(2)}) collective-permute-start(bf16[2,128,128]{2,1,0:T(8,128)(2,1)} %collective-permute-done), channel_id=1, source_target_pairs={{0,8},{8,16},{16,24},{24,32},{32,40},{40,48},{48,56},{56,64},{64,7... | collective-permute-start | bytes 196616 | tf_op jit(solution)/shard_map/while/body/eval_jaxpr/ppermute | solution.py:18
  828.7 11.8 %collective-permute-start.6 = (f32[2,128,128]{2,1,0:T(8,128)}, f32[2,128,128]{2,1,0:T(8,128)}, u32[]{:S(2)}, u32[]{:S(2)}) collective-permute-start(f32[2,128,128]{2,1,0:T(8,128)} %get-tuple-element.762), channel_id=1, source_target_pairs={{0,8},{8,16},{16,24},{24,32},{32,40},{40,48},{48,56},{56,64},{64,7... | collective-permute-start | bytes 393224 | tf_op jit(solution)/shard_map/while/body/eval_jaxpr/ppermute | solution.py:18
  841.2 16.8 %collective-permute-start.7 = (f32[2,128,128]{2,1,0:T(8,128)}, f32[2,128,128]{2,1,0:T(8,128)S(1)}, u32[]{:S(2)}, u32[]{:S(2)}) collective-permute-start(f32[2,128,128]{2,1,0:T(8,128)} %get-tuple-element.764), channel_id=1, source_target_pairs={{0,8},{8,16},{16,24},{24,32},{32,40},{40,48},{48,56},{56,64},{64,7... | collective-permute-start | bytes 393224 | tf_op jit(solution)/shard_map/while/body/eval_jaxpr/ppermute | solution.py:18
  843.1 14.9 %collective-permute-start.3 = (bf16[2,128,128]{2,1,0:T(8,128)(2,1)}, bf16[2,128,128]{2,1,0:T(8,128)(2,1)S(1)}, u32[]{:S(2)}, u32[]{:S(2)}) collective-permute-start(bf16[2,128,128]{2,1,0:T(8,128)(2,1)} %collective-permute-done.2), channel_id=1, source_target_pairs={{0,8},{8,16},{16,24},{24,32},{32,40},{40,48},{48,56},{56,64},{64,7... | collective-permute-start | bytes 196616 | tf_op jit(solution)/shard_map/while/body/eval_jaxpr/ppermute | solution.py:18
  874.2 14.7 %collective-permute-start.5 = (f32[2,128,128]{2,1,0:T(8,128)}, f32[2,128,128]{2,1,0:T(8,128)}, u32[]{:S(2)}, u32[]{:S(2)}) collective-permute-start(f32[2,128,128]{2,1,0:T(8,128)} %get-tuple-element.760), channel_id=1, source_target_pairs={{0,8},{8,16},{16,24},{24,32},{32,40},{40,48},{48,56},{56,64},{64,7... | collective-permute-start | bytes 393224 | tf_op jit(solution)/shard_map/while/body/eval_jaxpr/ppermute | solution.py:18
  876.1 14.9 %collective-permute-start.1 = (bf16[2,128,128]{2,1,0:T(8,128)(2,1)}, bf16[2,128,128]{2,1,0:T(8,128)(2,1)S(1)}, u32[]{:S(2)}, u32[]{:S(2)}) collective-permute-start(bf16[2,128,128]{2,1,0:T(8,128)(2,1)} %collective-permute-done), channel_id=1, source_target_pairs={{0,8},{8,16},{16,24},{24,32},{32,40},{40,48},{48,56},{56,64},{64,7... | collective-permute-start | bytes 196616 | tf_op jit(solution)/shard_map/while/body/eval_jaxpr/ppermute | solution.py:18
  904.2 15.6 %collective-permute-start.7 = (f32[2,128,128]{2,1,0:T(8,128)}, f32[2,128,128]{2,1,0:T(8,128)S(1)}, u32[]{:S(2)}, u32[]{:S(2)}) collective-permute-start(f32[2,128,128]{2,1,0:T(8,128)} %get-tuple-element.764), channel_id=1, source_target_pairs={{0,8},{8,16},{16,24},{24,32},{32,40},{40,48},{48,56},{56,64},{64,7... | collective-permute-start | bytes 393224 | tf_op jit(solution)/shard_map/while/body/eval_jaxpr/ppermute | solution.py:18
  906.1 13.7 %collective-permute-start.3 = (bf16[2,128,128]{2,1,0:T(8,128)(2,1)}, bf16[2,128,128]{2,1,0:T(8,128)(2,1)S(1)}, u32[]{:S(2)}, u32[]{:S(2)}) collective-permute-start(bf16[2,128,128]{2,1,0:T(8,128)(2,1)} %collective-permute-done.2), channel_id=1, source_target_pairs={{0,8},{8,16},{16,24},{24,32},{32,40},{40,48},{48,56},{56,64},{64,7... | collective-permute-start | bytes 196616 | tf_op jit(solution)/shard_map/while/body/eval_jaxpr/ppermute | solution.py:18
  936.1 14.4 %collective-permute-start.5 = (f32[2,128,128]{2,1,0:T(8,128)}, f32[2,128,128]{2,1,0:T(8,128)}, u32[]{:S(2)}, u32[]{:S(2)}) collective-permute-start(f32[2,128,128]{2,1,0:T(8,128)} %get-tuple-element.760), channel_id=1, source_target_pairs={{0,8},{8,16},{16,24},{24,32},{32,40},{40,48},{48,56},{56,64},{64,7... | collective-permute-start | bytes 393224 | tf_op jit(solution)/shard_map/while/body/eval_jaxpr/ppermute | solution.py:18
  938.0 14.7 %collective-permute-start.1 = (bf16[2,128,128]{2,1,0:T(8,128)(2,1)}, bf16[2,128,128]{2,1,0:T(8,128)(2,1)S(1)}, u32[]{:S(2)}, u32[]{:S(2)}) collective-permute-start(bf16[2,128,128]{2,1,0:T(8,128)(2,1)} %collective-permute-done), channel_id=1, source_target_pairs={{0,8},{8,16},{16,24},{24,32},{32,40},{40,48},{48,56},{56,64},{64,7... | collective-permute-start | bytes 196616 | tf_op jit(solution)/shard_map/while/body/eval_jaxpr/ppermute | solution.py:18
  965.3 14.7 %collective-permute-start.7 = (f32[2,128,128]{2,1,0:T(8,128)}, f32[2,128,128]{2,1,0:T(8,128)S(1)}, u32[]{:S(2)}, u32[]{:S(2)}) collective-permute-start(f32[2,128,128]{2,1,0:T(8,128)} %get-tuple-element.764), channel_id=1, source_target_pairs={{0,8},{8,16},{16,24},{24,32},{32,40},{40,48},{48,56},{56,64},{64,7... | collective-permute-start | bytes 393224 | tf_op jit(solution)/shard_map/while/body/eval_jaxpr/ppermute | solution.py:18
  967.2 12.8 %collective-permute-start.3 = (bf16[2,128,128]{2,1,0:T(8,128)(2,1)}, bf16[2,128,128]{2,1,0:T(8,128)(2,1)S(1)}, u32[]{:S(2)}, u32[]{:S(2)}) collective-permute-start(bf16[2,128,128]{2,1,0:T(8,128)(2,1)} %collective-permute-done.2), channel_id=1, source_target_pairs={{0,8},{8,16},{16,24},{24,32},{32,40},{40,48},{48,56},{56,64},{64,7... | collective-permute-start | bytes 196616 | tf_op jit(solution)/shard_map/while/body/eval_jaxpr/ppermute | solution.py:18
  993.6 11.9 %collective-permute-start.5 = (f32[2,128,128]{2,1,0:T(8,128)}, f32[2,128,128]{2,1,0:T(8,128)}, u32[]{:S(2)}, u32[]{:S(2)}) collective-permute-start(f32[2,128,128]{2,1,0:T(8,128)} %get-tuple-element.760), channel_id=1, source_target_pairs={{0,8},{8,16},{16,24},{24,32},{32,40},{40,48},{48,56},{56,64},{64,7... | collective-permute-start | bytes 393224 | tf_op jit(solution)/shard_map/while/body/eval_jaxpr/ppermute | solution.py:18
  (87 other events, 1980.2 us)
Sparse Core Ops, SparseCore 0:
  11.1 85.2 all-gather.2
  1126.9 30.6 reduce-scatter.1
where the time goes:
time: 1180 us; the launch traced here: 1170 us
  waiting for transfers between devices  659 us (56%)
  starting transfers between devices  257 us (22%)
  blocking collectives  87 us (7%)
  loops' own time  49.9 us (4%)
  other arithmetic  46.4 us (4%)
  local copies, waits for them, and re-layouts  32.6 us (3%)
  matrix products  20.3 us (2%)
  between operations  15.4 us (1%)
    ppermute x128, waiting for transfers between devices, shifted(): return lax.ppermute(value, axis, pairs)  549 us
    ppermute x128, starting transfers between devices, shifted(): return lax.ppermute(value, axis, pairs)  257 us
    all_gather x1, blocking collectives, shards(): lax.all_gather(chosen[None], ('section', 'dp'), axis=0, tiled=True)  87 us
    all_gather x1, waiting for transfers between devices, shards(): key_block = lax.all_gather(key_vectors, 'ctx', axis=1, tiled=True)[0]  78.3 us
    another operation x1, loops' own time, shards(): carried = lax.fori_loop(0, rounds, four_turns, carried)  49.8 us
    reduce_scatter x1, waiting for transfers between devices, shards(): lax.psum_scatter(jnp.dot(visual_grad, projector_weight, preferred_element...  30.8 us
  transfers between devices with their start and end apart: 130, of which 114 were waited for; matrix products, arithmetic and copies ran while one was open for 1% of the time, Pallas kernels for 0%

commit v1 on v0

v1 whole, which is shorter than its diff:
```python
import math

import jax
import jax.numpy as jnp
from jax import lax
from jax.sharding import PartitionSpec as P

HEAD_DIM = 128
GROUP = 7


MASKED = -1e30


def shards(
    query_vectors,
    key_vectors,
    value_vectors,
    grad_output,
    output_dots,
    frame_ids,
    visual_rows,
    shuffle_source,
    qkv_weight,
    projector_weight,
):
    position = lax.axis_index("ctx")
    local_rows = query_vectors.shape[1]
    scale_factor = 1.0 / math.sqrt(HEAD_DIM)
    query_heads = query_vectors[0].reshape(local_rows, GROUP, HEAD_DIM)
    grad_heads = grad_output[0].reshape(local_rows, GROUP, HEAD_DIM)
    corrections = output_dots[0]
    frame_line = frame_ids[0]
    seq_total = frame_line.shape[0]
    query_first = position * local_rows
    query_pos = query_first + jnp.arange(local_rows, dtype=jnp.int32)
    query_frames = lax.dynamic_slice_in_dim(frame_line, query_first, local_rows)

    own_pair = jnp.concatenate([key_vectors[0], value_vectors[0]], axis=1)
    all_pairs = lax.all_gather(own_pair, "ctx", axis=0, tiled=True)
    key_all = all_pairs[:, :HEAD_DIM]
    value_all = all_pairs[:, HEAD_DIM:]

    key_pos = jnp.arange(seq_total, dtype=jnp.int32)
    allowed = (key_pos[None, :] <= query_pos[:, None]) | (frame_line[None, :] == query_frames[:, None])

    scores = (
        jnp.einsum("qhd,kd->hqk", query_heads, key_all, preferred_element_type=jnp.float32)
        * scale_factor
    )
    masked_scores = jnp.where(allowed[None], scores, MASKED)
    running = masked_scores.max(axis=-1)
    summed = jnp.exp(masked_scores - running[:, :, None]).sum(axis=-1)
    log_total = running + jnp.log(summed)

    probability = jnp.exp(jnp.where(allowed[None], scores - log_total[:, :, None], MASKED))
    probs_low = probability.astype(jnp.bfloat16)
    grad_probs = jnp.einsum(
        "qhd,kd->hqk", grad_heads, value_all, preferred_element_type=jnp.float32
    )
    grad_scores = (probability * (grad_probs - corrections[:, :, None])).astype(jnp.bfloat16)
    grad_query = (
        jnp.einsum("hqk,kd->qhd", grad_scores, key_all, preferred_element_type=jnp.float32)
        * scale_factor
    )
    key_part = (
        jnp.einsum("hqk,qhd->kd", grad_scores, query_heads, preferred_element_type=jnp.float32)
        * scale_factor
    )
    value_part = jnp.einsum(
        "hqk,qhd->kd", probs_low, grad_heads, preferred_element_type=jnp.float32
    )
    summed_grads = lax.psum_scatter(
        jnp.concatenate([key_part, value_part], axis=1), "ctx", scatter_dimension=0, tiled=True
    )
    grad_keys_low = summed_grads[:, :HEAD_DIM].astype(jnp.bfloat16)
    grad_values_low = summed_grads[:, HEAD_DIM:].astype(jnp.bfloat16)
    grad_query_low = grad_query.astype(jnp.bfloat16).reshape(local_rows, GROUP * HEAD_DIM)
    visual_picks = visual_rows[0, 0]
    chosen = jnp.concatenate(
        [grad_query_low[visual_picks], grad_keys_low[visual_picks], grad_values_low[visual_picks]],
        axis=1,
    )
    everyone = lax.all_gather(chosen[None], ("section", "dp"), axis=0, tiled=True)
    groups = lax.axis_size("section")
    replicas = lax.axis_size("dp")
    half_rows = visual_picks.shape[0] // 2
    width_in = chosen.shape[1]
    arranged = (
        everyone.reshape(groups, replicas, 2, half_rows, width_in)
        .transpose(2, 1, 3, 0, 4)
        .reshape(2 * replicas * half_rows, groups * width_in)
    )
    visual_grad = jnp.dot(arranged, qkv_weight, preferred_element_type=jnp.float32).astype(
        jnp.bfloat16
    )
    shuffled = lax.psum_scatter(
        jnp.dot(visual_grad, projector_weight, preferred_element_type=jnp.float32).astype(
            jnp.bfloat16
        ),
        ("section", "dp"),
        scatter_dimension=0,
        tiled=True,
    ).astype(jnp.float32)
    slot_rows = shuffled.reshape(half_rows * 4, projector_weight.shape[1] // 4)
    patches = slot_rows[shuffle_source[0, 0]].astype(jnp.bfloat16)
    return (grad_keys_low[None], grad_values_low[None], patches[None])


def solution(mesh):
    placed = (
        P("dp", "ctx", "section"),
        P("dp", "ctx", "section"),
        P("dp", "ctx", "section"),
        P("dp", "ctx", "section"),
        P("dp", "section", "ctx"),
        P("dp", None),
        P("dp", "ctx", None),
        P("dp", ("ctx", "section"), None),
        P(None, ("section", "dp")),
        P(("section", "dp"), None),
    )
    return jax.shard_map(
        shards,
        mesh=mesh,
        in_specs=placed,
        out_specs=(
            P("dp", "ctx", "section"),
            P("dp", "ctx", "section"),
            P("dp", ("ctx", "section"), None),
        ),
        check_vma=False,
    )
```

time: 1180 us -> 489 us (0.41)
  waiting for transfers between devices: 659 us -> 351 us
  starting transfers between devices: 257 us -> 0.12 us
  blocking collectives: 87 us -> 18.8 us
  loops' own time: 49.9 us -> 0 us
  matrix products: 20.3 us -> 67.7 us
  other arithmetic: 46.4 us -> 23.6 us
  local copies, waits for them, and re-layouts: 32.6 us -> 11.6 us
    ppermute x128 -> x0, waiting for transfers between devices: 549 us -> none  [shifted(): return lax.ppermute(value, axis, pairs)]
    ppermute x128 -> x0, starting transfers between devices: 257 us -> none  [shifted(): return lax.ppermute(value, axis, pairs)]
    reduce_scatter x0 -> x1, waiting for transfers between devices: none -> 239 us  [shards(): lax.psum_scatter(jnp.concatenate([key_part, value_part], axis=1), 'ctx',...]
    all_gather x1, blocking collectives: 87 us -> 18.8 us  [shards(): lax.all_gather(chosen[None], ('section', 'dp'), axis=0, tiled=True)]
    another operation x66 -> x0, loops' own time: 49.9 us -> none  [the longest x1 49.8 us: shards(): carried = lax.fori_loop(0, rounds, four_turns, carried)]
    dot_general x11 -> x5, matrix products: 16.5 us -> 64 us  [the longest x1 19.4 us: shards(): jnp.einsum('qhd,kd->hqk', grad_heads, value_all, preferred_element_type=j...]
    dynamic_slice x16 -> x0, other arithmetic: 23 us -> none  [key_mask(): key_frames = lax.dynamic_slice_in_dim(frame_line, key_first, row_count)]
  transfers between devices with their start and end apart: 130 -> 3, of which waited for: 114 -> 3; matrix products, arithmetic and copies ran while one was open for 1% -> 4% of each run, Pallas kernels for 0% -> 0%
where the time goes in v1:
time: 489 us; the launch traced here: 487 us
  waiting for transfers between devices  351 us (72%)
  matrix products  67.7 us (14%)
  other arithmetic  23.6 us (5%)
  blocking collectives  18.8 us (4%)
  between operations  13.9 us (3%)
  local copies, waits for them, and re-layouts  11.6 us (2%)
    reduce_scatter x1, waiting for transfers between devices, shards(): lax.psum_scatter(jnp.concatenate([key_part, value_part], axis=1), 'ctx',...  239 us
    all_gather x1, waiting for transfers between devices, shards(): all_pairs = lax.all_gather(own_pair, 'ctx', axis=0, tiled=True)  82.4 us
    reduce_scatter x1, waiting for transfers between devices, shards(): lax.psum_scatter(jnp.dot(visual_grad, projector_weight, preferred_element...  29.6 us
    dot_general x1, matrix products, shards(): jnp.einsum('qhd,kd->hqk', grad_heads, value_all, preferred_element_type=j...  19.4 us
    all_gather x1, blocking collectives, shards(): lax.all_gather(chosen[None], ('section', 'dp'), axis=0, tiled=True)  18.8 us
    dot_general x1, matrix products, shards(): jnp.einsum('hqk,qhd->kd', probs_low, grad_heads, preferred_element_type=j...  13.4 us
    dot_general x1, matrix products, shards(): jnp.einsum('qhd,kd->hqk', query_heads, key_all, preferred_element_type=jn...  13.1 us
    reduce_sum x1, other arithmetic, shards(): summed = jnp.exp(masked_scores - running[:, :, None]).sum(axis=-1)  12.7 us
  transfers between devices with their start and end apart: 3, of which 3 were waited for; matrix products, arithmetic and copies ran while one was open for 4% of the time, Pallas kernels for 0%

profile of v1, /device:TPU:1, one launch (start us, length us, event | category | flops | bytes accessed | tf_op | source)
XLA Modules:
  0.0 487.2 jit_solution(14910348359824243187)
XLA Ops:
  7.2 0.0 copy-start
  7.2 0.0 all-gather.3.cloned.1.call-start
  7.2 1.6 pad_maximum_fusion.2
  8.8 0.0 all-gather.3.cloned.1.call-update
  8.8 0.0 reduce-scatter.3.cloned.1.call-start
  8.9 1.8 copy.28
  10.6 1.8 copy.26
  12.4 0.7 copy.50
  13.1 0.7 dynamic-slice_bitcast_fusion
  13.8 4.3 fusion.13
  18.0 82.4 %all-gather.3.cloned.1.call-done = bf16[8192,256]{1,0:T(8,128)(2,1)} async-done(((bf16[128,256]{1,0:T(8,128)(2,1)}), bf16[8192,256]{1,0:T(8,128)(2,1)}) %all-gather.3.cloned.1.call-update) | async-done | bytes 4194320 | tf_op jit(solution)/shard_map/all_gather | solution.py:40
  100.4 13.1 %fusion.4 = (f32[7,128]{1,0:T(8,128)S(1)}, f32[8192,128,7]{1,0,2:T(8,128)}) fusion(pred[128,8192]{0,1:T(8,128)(4,1)S(1)} %fusion.13, bf16[128,7,128]{0,2,1:T(8,128)(2,1)} %bitcast.90, bf16[8192,256]{1,0:T(8,128)(2,1)} %all-gather.3.cloned.1.call-done), kind=kOutput, calls=%fused_computation.12 | convolution fusion | flops 1901067392 | bytes 32738816 | tf_op jit(solution)/shard_map/qhd,kd->hqk/dot_general | solution.py:48
  113.5 0.0 copy-start.3
  113.5 12.7 %exponential_reduce_fusion = f32[7,128]{1,0:T(8,128)S(1)} fusion(f32[8192,128,7]{1,0,2:T(8,128)} %get-tuple-element.14, f32[7,128]{1,0:T(8,128)S(1)} %get-tuple-element.13, pred[128,8192]{0,1:T(8,128)(4,1)S(1)} %fusion.13), kind=kLoop, calls=%fused_computation.11 | loop fusion | flops 29359232 | bytes 30415872 | tf_op jit(solution)/shard_map/reduce_sum | solution.py:53
  126.3 0.0 copy-done.3
  126.3 0.0 copy-start.1
  126.3 13.4 %fusion.9 = f32[8192,128]{0,1:T(8,128)S(1)} fusion(bf16[128,7,128]{0,2,1:T(8,128)(2,1)S(1)} %bitcast.92, f32[8192,128,7]{1,0,2:T(8,128)} %get-tuple-element.14, f32[7,128]{1,0:T(8,128)S(1)} %log_add_fusion, pred[128,8192]{0,1:T(8,128)(4,1)S(1)} %fusion.13), kind=kOutput, calls=%fused_computation.17 | convolution fusion | flops 1908408320 | bytes 34835968 | tf_op jit(solution)/shard_map/hqk,qhd->kd/dot_general | solution.py:70
  139.7 0.0 copy-done.1
  139.7 0.0 copy-start.2
  139.7 19.4 %fusion.1 = bf16[7,128,8192]{1,2,0:T(8,128)(2,1)} fusion(f32[8192,128,7]{1,0,2:T(8,128)} %get-tuple-element.14, bf16[128,7,128]{0,2,1:T(8,128)(2,1)S(1)} %bitcast.93, f32[7,128]{1,0:T(8,128)S(1)} %bitcast.98, f32[7,128]{1,0:T(8,128)S(1)} %log_add_fusion, pred[128,8192]{0,1:T(8,128)(4,1)S(1)} %fusion.13, bf16[8192,256]{1,0:T(8,128)(2,1)S(1)} %copy-done.1), kind=kOutput, calls=%fused_computation.6 | convolution fusion | flops 1923088384 | bytes 47423488 | tf_op jit(solution)/shard_map/qhd,kd->hqk/dot_general | solution.py:58
  159.1 0.0 copy-done.2
  159.1 9.9 %fusion.12 = f32[8192,128]{0,1:T(8,128)S(1)} fusion(bf16[7,128,8192]{1,2,0:T(8,128)(2,1)} %fusion.1, bf16[128,7,128]{0,2,1:T(8,128)(2,1)S(1)} %bitcast.91), kind=kOutput, calls=%fused_computation.18 | convolution fusion | flops 1880096768 | bytes 19103744 | tf_op jit(solution)/shard_map/hqk,qhd->kd/dot_general | solution.py:67
  169.0 0.0 copy-start.4
  169.0 4.1 pad_maximum_fusion
  173.1 0.0 reduce-scatter.3.cloned.1.call-update
  173.2 0.0 reduce-scatter.5.cloned.1.call-start
  173.2 0.0 copy-done.4
  173.2 0.0 copy-start.5
  173.3 8.2 %fusion.17 = bf16[128,7,128]{2,0,1:T(8,128)(2,1)S(1)} fusion(bf16[7,128,8192]{1,2,0:T(8,128)(2,1)} %fusion.1, bf16[8192,256]{1,0:T(8,128)(2,1)} %all-gather.3.cloned.1.call-done), kind=kOutput, calls=%fused_computation.28 | convolution fusion | flops 1879277568 | bytes 17006592 | tf_op jit(solution)/shard_map/hqk,kd->qhd/dot_general | solution.py:63
  181.5 0.2 copy.34
  181.6 0.6 gather_fusion
  182.3 239.3 %reduce-scatter.3.cloned.1.call-done = f32[128,256]{0,1:T(8,128)} async-done(((f32[8192,256]{0,1:T(8,128)}), f32[128,256]{0,1:T(8,128)}) %reduce-scatter.3.cloned.1.call-update) | async-done | bytes 131088 | tf_op jit(solution)/shard_map/reduce_scatter | solution.py:73
  421.5 0.9 convert.5
  422.5 0.1 copy.36
  422.6 0.6 gather_fusion.2
  423.2 0.1 copy.35
  423.3 0.6 gather_fusion.1
  423.9 18.8 %all-gather = bf16[256,1152]{1,0:T(8,128)(2,1)S(1)} all-gather(bf16[32,1152]{1,0:T(8,128)(2,1)S(1)} %pad_maximum_fusion.1), channel_id=2, replica_groups=mesh['ctx'=64,'section'=2,'dp'=4] {'section','dp'}, dimensions={0}, use_global_device_ids=true | all-gather | bytes 663552 | tf_op jit(solution)/shard_map/all_gather | solution.py:84
  442.7 0.6 copy.37
  443.4 0.1 copy.48
  443.4 0.0 copy-done
  443.4 3.8 convolution_convert_fusion
  447.2 0.0 reduce-scatter.5.cloned.1.call-update
  447.2 0.0 copy-done.5
  447.3 0.7 copy.38
  448.0 0.7 copy.39
  448.7 29.6 %reduce-scatter.5.cloned.1.call-done = bf16[16,2560]{1,0:T(8,128)(2,1)} async-done(((bf16[128,2560]{1,0:T(8,128)(2,1)}), bf16[16,2560]{1,0:T(8,128)(2,1)}) %reduce-scatter.5.cloned.1.call-update) | async-done | bytes 81936 | tf_op jit(solution)/shard_map/reduce_scatter | solution.py:97
  478.3 0.9 reshape.155
  479.3 1.3 gather_fusion.3
  (8 shorter events, 0.1 us)
Async XLA Ops:
  7.2 436.3 %copy-start = (bf16[448,2560]{1,0:T(8,128)(2,1)S(1)}, bf16[448,2560]{1,0:T(8,128)(2,1)}, u32[]{:S(2)}) copy-start(bf16[448,2560]{1,0:T(8,128)(2,1)} %param.19) | copy-start | bytes 6881284
  7.2 93.2 %all-gather.3.cloned.1.call-start = ((), (), s32[]{:S(2)}) async-start(), calls=%async_computation.2 | async-start | bytes 4259840 | tf_op jit(solution)/shard_map/all_gather | solution.py:40
  8.8 412.7 %reduce-scatter.3.cloned.1.call-start = ((), (), s32[]{:S(2)}) async-start(), calls=%async_computation.3 | async-start | bytes 8519680 | tf_op jit(solution)/shard_map/reduce_scatter | solution.py:73
  113.5 12.7 %copy-start.3 = (bf16[1,128,896]{1,2,0:T(8,128)(2,1)S(1)}, bf16[1,128,896]{1,2,0:T(8,128)(2,1)}, u32[]{:S(2)}) copy-start(bf16[1,128,896]{1,2,0:T(8,128)(2,1)} %copy.28) | copy-start | bytes 688132
  126.3 13.4 %copy-start.1 = (bf16[8192,256]{1,0:T(8,128)(2,1)S(1)}, bf16[8192,256]{1,0:T(8,128)(2,1)}, u32[]{:S(2)}) copy-start(bf16[8192,256]{1,0:T(8,128)(2,1)} %all-gather.3.cloned.1.call-done) | copy-start | bytes 12582916
  139.7 19.4 %copy-start.2 = (bf16[1,128,896]{1,2,0:T(8,128)(2,1)S(1)}, bf16[1,128,896]{1,2,0:T(8,128)(2,1)}, u32[]{:S(2)}) copy-start(bf16[1,128,896]{1,2,0:T(8,128)(2,1)} %copy.26) | copy-start | bytes 688132
  169.0 4.2 copy-start.4
  173.2 305.2 %reduce-scatter.5.cloned.1.call-start = ((), (), s32[]{:S(2)}) async-start(), calls=%async_computation.4 | async-start | bytes 737280 | tf_op jit(solution)/shard_map/reduce_scatter | solution.py:97
  173.2 274.0 %copy-start.5 = (s32[1,1,64]{2,1,0:T(1,128)S(1)}, s32[1,1,64]{2,1,0:T(1,128)}, u32[]{:S(2)}) copy-start(s32[1,1,64]{2,1,0:T(1,128)} %param.17) | copy-start | bytes 772
Sparse Core Ops, SparseCore 0:
  11.7 88.7 all-gather.2
  173.3 248.2 reduce-scatter.2
  447.3 30.9 reduce-scatter.4

commit v2 on v1

--- a/solution.py
+++ b/solution.py
@@ -24,7 +24,9 @@
     qkv_weight,
     projector_weight,
 ):
-    position = lax.axis_index("ctx")
+    ring_z = lax.axis_size("cz")
+    ring_y = lax.axis_size("cy")
+    position = lax.axis_index("cz") * ring_y + lax.axis_index("cy")
     local_rows = query_vectors.shape[1]
     scale_factor = 1.0 / math.sqrt(HEAD_DIM)
     query_heads = query_vectors[0].reshape(local_rows, GROUP, HEAD_DIM)
@@ -37,12 +39,22 @@
     query_frames = lax.dynamic_slice_in_dim(frame_line, query_first, local_rows)
 
     own_pair = jnp.concatenate([key_vectors[0], value_vectors[0]], axis=1)
-    all_pairs = lax.all_gather(own_pair, "ctx", axis=0, tiled=True)
+    all_pairs = lax.all_gather(
+        lax.all_gather(own_pair, "cz", axis=0, tiled=True), "cy", axis=0, tiled=True
+    )
     key_all = all_pairs[:, :HEAD_DIM]
     value_all = all_pairs[:, HEAD_DIM:]
 
-    key_pos = jnp.arange(seq_total, dtype=jnp.int32)
-    allowed = (key_pos[None, :] <= query_pos[:, None]) | (frame_line[None, :] == query_frames[:, None])
+    key_pos = (
+        jnp.arange(seq_total, dtype=jnp.int32)
+        .reshape(ring_z, ring_y, local_rows)
+        .transpose(1, 0, 2)
+        .reshape(seq_total)
+    )
+    key_frames = (
+        frame_line.reshape(ring_z, ring_y, local_rows).transpose(1, 0, 2).reshape(seq_total)
+    )
+    allowed = (key_pos[None, :] <= query_pos[:, None]) | (key_frames[None, :] == query_frames[:, None])
 
     scores = (
         jnp.einsum("qhd,kd->hqk", query_heads, key_all, preferred_element_type=jnp.float32)
@@ -71,7 +83,15 @@
         "hqk,qhd->kd", probs_low, grad_heads, preferred_element_type=jnp.float32
     )
     summed_grads = lax.psum_scatter(
-        jnp.concatenate([key_part, value_part], axis=1), "ctx", scatter_dimension=0, tiled=True
+        lax.psum_scatter(
+            jnp.concatenate([key_part, value_part], axis=1),
+            "cy",
+            scatter_dimension=0,
+            tiled=True,
+        ),
+        "cz",
+        scatter_dimension=0,
+        tiled=True,
     )
     grad_keys_low = summed_grads[:, :HEAD_DIM].astype(jnp.bfloat16)
     grad_values_low = summed_grads[:, HEAD_DIM:].astype(jnp.bfloat16)
@@ -108,26 +128,35 @@
 
 
 def solution(mesh):
+    ctx_size = mesh.shape["ctx"]
+    ring_y = 8 if ctx_size % 8 == 0 else 1
+    split_mesh = jax.sharding.Mesh(
+        mesh.devices.reshape(
+            ctx_size // ring_y, ring_y, mesh.shape["section"], mesh.shape["dp"]
+        ),
+        ("cz", "cy", "section", "dp"),
+    )
+    ctx = ("cz", "cy")
     placed = (
-        P("dp", "ctx", "section"),
-        P("dp", "ctx", "section"),
-        P("dp", "ctx", "section"),
-        P("dp", "ctx", "section"),
-        P("dp", "section", "ctx"),
+        P("dp", ctx, "section"),
+        P("dp", ctx, "section"),
+        P("dp", ctx, "section"),
+        P("dp", ctx, "section"),
+        P("dp", "section", ctx),
         P("dp", None),
-        P("dp", "ctx", None),
-        P("dp", ("ctx", "section"), None),
+        P("dp", ctx, None),
+        P("dp", ("cz", "cy", "section"), None),
         P(None, ("section", "dp")),
         P(("section", "dp"), None),
     )
     return jax.shard_map(
         shards,
-        mesh=mesh,
+        mesh=split_mesh,
         in_specs=placed,
         out_specs=(
-            P("dp", "ctx", "section"),
-            P("dp", "ctx", "section"),
-            P("dp", ("ctx", "section"), None),
+            P("dp", ctx, "section"),
+            P("dp", ctx, "section"),
+            P("dp", ("cz", "cy", "section"), None),
         ),
         check_vma=False,
     )

time: 489 us -> 375 us (0.77)
  waiting for transfers between devices: 351 us -> 211 us
  blocking collectives: 18.8 us -> 46.9 us
    reduce_scatter x1 -> x2, waiting for transfers between devices: 239 us -> 127 us  [the longest x1 96.4 us: shards(): lax.psum_scatter(jnp.concatenate([key_part, value_part], axis=1), 'cy', s...]
    all_gather x1, waiting for transfers between devices: 82.4 us -> 53.1 us  [shards(): lax.all_gather(lax.all_gather(own_pair, 'cz', axis=0, tiled=True), 'cy',...]
    all_gather x0 -> x1, blocking collectives: none -> 28.4 us  [shards(): lax.all_gather(own_pair, 'cz', axis=0, tiled=True)]
  transfers between devices with their start and end apart: 3 -> 4, of which waited for: 3 -> 4; matrix products, arithmetic and copies ran while one was open for 4% -> 5% of each run, Pallas kernels for 0% -> 0%
where the time goes in v2:
time: 375 us; the launch traced here: 374 us
  waiting for transfers between devices  211 us (56%)
  matrix products  68.2 us (18%)
  blocking collectives  46.9 us (13%)
  other arithmetic  22.3 us (6%)
  between operations  14 us (4%)
  local copies, waits for them, and re-layouts  11.6 us (3%)
    reduce_scatter x1, waiting for transfers between devices, shards(): lax.psum_scatter(jnp.concatenate([key_part, value_part], axis=1), 'cy', s...  96.4 us
    all_gather x1, waiting for transfers between devices, shards(): lax.all_gather(lax.all_gather(own_pair, 'cz', axis=0, tiled=True), 'cy',...  53.1 us
    reduce_scatter x1, waiting for transfers between devices, shards(): lax.psum_scatter(jnp.dot(visual_grad, projector_weight, preferred_element...  30.8 us
    reduce_scatter x1, waiting for transfers between devices, shards(): lax.psum_scatter(lax.psum_scatter(jnp.concatenate([key_part, value_part],...  30.5 us
    all_gather x1, blocking collectives, shards(): lax.all_gather(own_pair, 'cz', axis=0, tiled=True)  28.4 us
    dot_general x1, matrix products, shards(): jnp.einsum('qhd,kd->hqk', grad_heads, value_all, preferred_element_type=j...  19.4 us
    all_gather x1, blocking collectives, shards(): lax.all_gather(chosen[None], ('section', 'dp'), axis=0, tiled=True)  18.5 us
    dot_general x1, matrix products, shards(): jnp.einsum('hqk,qhd->kd', probs_low, grad_heads, preferred_element_type=j...  13.4 us
  transfers between devices with their start and end apart: 4, of which 4 were waited for; matrix products, arithmetic and copies ran while one was open for 5% of the time, Pallas kernels for 0%

profile of v2, /device:TPU:1, one launch (start us, length us, event | category | flops | bytes accessed | tf_op | source)
XLA Modules:
  0.0 373.9 jit_solution(5285974721121662468)
XLA Ops:
  7.2 0.0 copy-start
  7.2 0.0 all-gather.3.cloned.1.call-start
  7.2 0.9 pad_maximum_fusion.2
  8.2 28.4 %all_gather.9 = bf16[1024,256]{1,0:T(8,128)(2,1)} all-gather(bf16[128,256]{1,0:T(8,128)(2,1)S(1)} %pad_maximum_fusion.2), channel_id=1, replica_groups=mesh['cz'=8,'cy'=8,'section'=2,'dp'=4] {'cz'}, dimensions={0}, use_global_device_ids=true | all-gather | bytes 589824 | tf_op jit(solution)/shard_map/all_gather | solution.py:43
  36.6 0.0 all-gather.3.cloned.1.call-update
  36.6 0.0 reduce-scatter.4.cloned.1.call-start
  36.7 1.8 copy.43
  38.5 1.8 copy.41
  40.2 0.7 copy.66
  40.9 0.7 dynamic-slice_bitcast_fusion
  41.6 0.8 copy_bitcast_fusion
  42.4 2.8 compare_or_fusion
  45.1 53.1 %all-gather.3.cloned.1.call-done = bf16[8192,256]{1,0:T(8,128)(2,1)} async-done(((bf16[1024,256]{1,0:T(8,128)(2,1)}), bf16[8192,256]{1,0:T(8,128)(2,1)}) %all-gather.3.cloned.1.call-update) | async-done | bytes 4194320 | tf_op jit(solution)/shard_map/all_gather | solution.py:42
  98.2 13.1 %fusion.4 = (f32[7,128]{1,0:T(8,128)S(1)}, f32[8192,128,7]{1,0,2:T(8,128)}) fusion(pred[128,8192]{0,1:T(8,128)(4,1)S(1)} %compare_or_fusion, bf16[128,7,128]{0,2,1:T(8,128)(2,1)} %bitcast.96, bf16[8192,256]{1,0:T(8,128)(2,1)} %all-gather.3.cloned.1.call-done), kind=kOutput, calls=%fused_computation.12 | convolution fusion | flops 1901067392 | bytes 32738816 | tf_op jit(solution)/shard_map/qhd,kd->hqk/dot_general | solution.py:60
  111.3 0.0 copy-start.3
  111.3 12.7 %exponential_reduce_fusion = f32[7,128]{1,0:T(8,128)S(1)} fusion(f32[8192,128,7]{1,0,2:T(8,128)} %get-tuple-element.17, f32[7,128]{1,0:T(8,128)S(1)} %get-tuple-element.16, pred[128,8192]{0,1:T(8,128)(4,1)S(1)} %compare_or_fusion), kind=kLoop, calls=%fused_computation.11 | loop fusion | flops 29359232 | bytes 30415872 | tf_op jit(solution)/shard_map/reduce_sum | solution.py:65
  124.1 0.0 copy-done.3
  124.1 0.0 copy-start.1
  124.1 13.4 %fusion.9 = f32[8192,128]{0,1:T(8,128)S(1)} fusion(bf16[128,7,128]{0,2,1:T(8,128)(2,1)S(1)} %bitcast.98, f32[8192,128,7]{1,0,2:T(8,128)} %get-tuple-element.17, f32[7,128]{1,0:T(8,128)S(1)} %log_add_fusion, pred[128,8192]{0,1:T(8,128)(4,1)S(1)} %compare_or_fusion), kind=kOutput, calls=%fused_computation.17 | convolution fusion | flops 1908408320 | bytes 34835968 | tf_op jit(solution)/shard_map/hqk,qhd->kd/dot_general | solution.py:82
  137.5 0.0 copy-done.1
  137.5 0.0 copy-start.2
  137.5 19.4 %fusion.1 = bf16[7,128,8192]{1,2,0:T(8,128)(2,1)} fusion(f32[8192,128,7]{1,0,2:T(8,128)} %get-tuple-element.17, bf16[128,7,128]{0,2,1:T(8,128)(2,1)S(1)} %bitcast.99, f32[7,128]{1,0:T(8,128)S(1)} %bitcast.104, f32[7,128]{1,0:T(8,128)S(1)} %log_add_fusion, pred[128,8192]{0,1:T(8,128)(4,1)S(1)} %compare_or_fusion, bf16[8192,256]{1,0:T(8,128)(2,1)S(1)} %copy-done.1), kind=kOutput, calls=%fused_computation.6 | convolution fusion | flops 1923088384 | bytes 47423488 | tf_op jit(solution)/shard_map/qhd,kd->hqk/dot_general | solution.py:70
  156.9 0.0 copy-done.2
  156.9 9.9 %fusion.12 = f32[8192,128]{0,1:T(8,128)S(1)} fusion(bf16[7,128,8192]{1,2,0:T(8,128)(2,1)} %fusion.1, bf16[128,7,128]{0,2,1:T(8,128)(2,1)S(1)} %bitcast.97), kind=kOutput, calls=%fused_computation.18 | convolution fusion | flops 1880096768 | bytes 19103744 | tf_op jit(solution)/shard_map/hqk,qhd->kd/dot_general | solution.py:79
  166.8 0.0 copy-start.4
  166.8 4.1 %pad_maximum_fusion = f32[8192,256]{0,1:T(8,128)} fusion(f32[8192,128]{0,1:T(8,128)S(1)} %fusion.9, f32[8192,128]{0,1:T(8,128)S(1)} %fusion.12), kind=kLoop, calls=%fused_computation.19 | loop fusion | flops 2097152 | bytes 16777216 | tf_op jit(solution)/shard_map/concatenate | solution.py:87
  170.9 0.0 reduce-scatter.4.cloned.1.call-update
  171.0 0.0 reduce-scatter.6.cloned.1.call-start
  171.0 96.4 %reduce-scatter.4.cloned.1.call-done = f32[1024,256]{0,1:T(8,128)} async-done(((f32[8192,256]{0,1:T(8,128)}), f32[1024,256]{0,1:T(8,128)}) %reduce-scatter.4.cloned.1.call-update) | async-done | bytes 1048592 | tf_op jit(solution)/shard_map/reduce_scatter | solution.py:86
  267.4 0.0 reduce-scatter.6.cloned.1.call-update
  267.5 0.0 reduce-scatter.8.cloned.1.call-start
  267.5 0.0 copy-done.4
  267.5 0.0 copy-start.5
  267.6 8.2 %fusion.16 = bf16[128,7,128]{2,0,1:T(8,128)(2,1)S(1)} fusion(bf16[7,128,8192]{1,2,0:T(8,128)(2,1)} %fusion.1, bf16[8192,256]{1,0:T(8,128)(2,1)} %all-gather.3.cloned.1.call-done), kind=kOutput, calls=%fused_computation.27 | convolution fusion | flops 1879277568 | bytes 17006592 | tf_op jit(solution)/shard_map/hqk,kd->qhd/dot_general | solution.py:75
  275.8 0.2 copy.49
  275.9 0.6 gather_fusion
  276.6 30.5 %reduce-scatter.6.cloned.1.call-done = f32[128,256]{0,1:T(8,128)} async-done(((f32[1024,256]{0,1:T(8,128)}), f32[128,256]{0,1:T(8,128)}) %reduce-scatter.6.cloned.1.call-update) | async-done | bytes 131088 | tf_op jit(solution)/shard_map/reduce_scatter | solution.py:85
  307.0 0.9 convert.5
  308.0 0.1 copy.51
  308.1 0.6 gather_fusion.2
  308.7 0.1 copy.50
  308.8 0.6 gather_fusion.1
  309.4 18.5 %all-gather = bf16[256,1152]{1,0:T(8,128)(2,1)S(1)} all-gather(bf16[32,1152]{1,0:T(8,128)(2,1)S(1)} %pad_maximum_fusion.1), channel_id=2, replica_groups=mesh['cz'=8,'cy'=8,'section'=2,'dp'=4] {'section','dp'}, dimensions={0}, use_global_device_ids=true | all-gather | bytes 663552 | tf_op jit(solution)/shard_map/all_gather | solution.py:104
  327.9 0.6 copy.52
  328.5 0.1 copy.63
  328.6 0.0 copy-done
  328.6 4.2 %convolution_convert_fusion = bf16[128,2560]{1,0:T(8,128)(2,1)} fusion(bf16[448,2560]{1,0:T(8,128)(2,1)S(1)} %copy-done, bf16[128,2304]{1,0:T(8,128)(2,1)S(1)} %bitcast.94, bf16[2304,448]{0,1:T(8,128)(2,1)} %param.18), kind=kOutput, calls=%fused_computation.21 | convolution fusion | flops 558227456 | bytes 5603328 | tf_op jit(solution)/shard_map/dot_general | solution.py:118
  332.8 0.0 reduce-scatter.8.cloned.1.call-update
  332.8 0.0 copy-done.5
  332.9 0.7 copy.53
  333.6 0.7 copy.54
  334.3 30.8 %reduce-scatter.8.cloned.1.call-done = bf16[16,2560]{1,0:T(8,128)(2,1)} async-done(((bf16[128,2560]{1,0:T(8,128)(2,1)}), bf16[16,2560]{1,0:T(8,128)(2,1)}) %reduce-scatter.8.cloned.1.call-update) | async-done | bytes 81936 | tf_op jit(solution)/shard_map/reduce_scatter | solution.py:117
  365.1 0.9 reshape.215
  366.1 1.3 gather_fusion.3
  (8 shorter events, 0.1 us)
Async XLA Ops:
  7.2 321.4 %copy-start = (bf16[448,2560]{1,0:T(8,128)(2,1)S(1)}, bf16[448,2560]{1,0:T(8,128)(2,1)}, u32[]{:S(2)}) copy-start(bf16[448,2560]{1,0:T(8,128)(2,1)} %param.19) | copy-start | bytes 6881284
  7.2 91.0 %all-gather.3.cloned.1.call-start = ((), (), s32[]{:S(2)}) async-start(), calls=%async_computation.3 | async-start | bytes 4718592 | tf_op jit(solution)/shard_map/all_gather | solution.py:42
  36.6 230.8 %reduce-scatter.4.cloned.1.call-start = ((), (), s32[]{:S(2)}) async-start(), calls=%async_computation.4 | async-start | bytes 9437184 | tf_op jit(solution)/shard_map/reduce_scatter | solution.py:86
  111.3 12.7 %copy-start.3 = (bf16[1,128,896]{1,2,0:T(8,128)(2,1)S(1)}, bf16[1,128,896]{1,2,0:T(8,128)(2,1)}, u32[]{:S(2)}) copy-start(bf16[1,128,896]{1,2,0:T(8,128)(2,1)} %copy.43) | copy-start | bytes 688132
  124.1 13.4 %copy-start.1 = (bf16[8192,256]{1,0:T(8,128)(2,1)S(1)}, bf16[8192,256]{1,0:T(8,128)(2,1)}, u32[]{:S(2)}) copy-start(bf16[8192,256]{1,0:T(8,128)(2,1)} %all-gather.3.cloned.1.call-done) | copy-start | bytes 12582916
  137.5 19.4 %copy-start.2 = (bf16[1,128,896]{1,2,0:T(8,128)(2,1)S(1)}, bf16[1,128,896]{1,2,0:T(8,128)(2,1)}, u32[]{:S(2)}) copy-start(bf16[1,128,896]{1,2,0:T(8,128)(2,1)} %copy.41) | copy-start | bytes 688132
  166.8 100.7 %copy-start.4 = (s32[1,1,32]{2,1,0:T(1,128)S(1)}, s32[1,1,32]{2,1,0:T(1,128)}, u32[]{:S(2)}) copy-start(s32[1,1,32]{2,1,0:T(1,128)} %param.16) | copy-start | bytes 388
  171.0 136.1 %reduce-scatter.6.cloned.1.call-start = ((), (), s32[]{:S(2)}) async-start(), calls=%async_computation.5 | async-start | bytes 1179648 | tf_op jit(solution)/shard_map/reduce_scatter | solution.py:85
  267.5 97.7 %reduce-scatter.8.cloned.1.call-start = ((), (), s32[]{:S(2)}) async-start(), calls=%async_computation.6 | async-start | bytes 737280 | tf_op jit(solution)/shard_map/reduce_scatter | solution.py:117
  267.5 65.3 %copy-start.5 = (s32[1,1,64]{2,1,0:T(1,128)S(1)}, s32[1,1,64]{2,1,0:T(1,128)}, u32[]{:S(2)}) copy-start(s32[1,1,64]{2,1,0:T(1,128)} %param.17) | copy-start | bytes 772
Sparse Core Ops, SparseCore 0:
  36.8 61.4 all-gather.2
  171.1 96.3 reduce-scatter.3
  270.3 36.7 reduce-scatter.5
  333.0 32.1 reduce-scatter.7

commit v3 on v2

--- a/solution.py
+++ b/solution.py
@@ -65,47 +65,74 @@
     summed = jnp.exp(masked_scores - running[:, :, None]).sum(axis=-1)
     log_total = running + jnp.log(summed)
 
-    probability = jnp.exp(jnp.where(allowed[None], scores - log_total[:, :, None], MASKED))
-    probs_low = probability.astype(jnp.bfloat16)
-    grad_probs = jnp.einsum(
-        "qhd,kd->hqk", grad_heads, value_all, preferred_element_type=jnp.float32
-    )
-    grad_scores = (probability * (grad_probs - corrections[:, :, None])).astype(jnp.bfloat16)
-    grad_query = (
-        jnp.einsum("hqk,kd->qhd", grad_scores, key_all, preferred_element_type=jnp.float32)
-        * scale_factor
-    )
-    key_part = (
-        jnp.einsum("hqk,qhd->kd", grad_scores, query_heads, preferred_element_type=jnp.float32)
-        * scale_factor
-    )
-    value_part = jnp.einsum(
-        "hqk,qhd->kd", probs_low, grad_heads, preferred_element_type=jnp.float32
-    )
-    summed_grads = lax.psum_scatter(
-        lax.psum_scatter(
+    def chunk_grads(chunk_keys, chunk_values, chunk_allowed, chunk_scores):
+        probability = jnp.exp(
+            jnp.where(chunk_allowed[None], chunk_scores - log_total[:, :, None], MASKED)
+        )
+        probs_low = probability.astype(jnp.bfloat16)
+        grad_probs = jnp.einsum(
+            "qhd,kd->hqk", grad_heads, chunk_values, preferred_element_type=jnp.float32
+        )
+        grad_scores = (probability * (grad_probs - corrections[:, :, None])).astype(jnp.bfloat16)
+        query_term = (
+            jnp.einsum("hqk,kd->qhd", grad_scores, chunk_keys, preferred_element_type=jnp.float32)
+            * scale_factor
+        )
+        key_part = (
+            jnp.einsum(
+                "hqk,qhd->kd", grad_scores, query_heads, preferred_element_type=jnp.float32
+            )
+            * scale_factor
+        )
+        value_part = jnp.einsum(
+            "hqk,qhd->kd", probs_low, grad_heads, preferred_element_type=jnp.float32
+        )
+        partial = lax.psum_scatter(
             jnp.concatenate([key_part, value_part], axis=1),
             "cy",
             scatter_dimension=0,
             tiled=True,
-        ),
-        "cz",
-        scatter_dimension=0,
-        tiled=True,
+        )
+        return query_term, partial
+
+    def chunk_of(array, lo, hi):
+        lead = array.reshape((ring_y, ring_z, local_rows) + array.shape[1:])[:, lo:hi]
+        return lead.reshape((ring_y * (hi - lo) * local_rows,) + array.shape[1:])
+
+    half_z = ring_z // 2
+    query_terms = []
+    partials = []
+    for lo, hi in ((0, half_z), (half_z, ring_z)):
+        chunk_allowed = chunk_of(allowed.T, lo, hi).T
+        chunk_scores = chunk_of(scores.transpose(2, 0, 1), lo, hi).transpose(1, 2, 0)
+        query_term, partial = chunk_grads(
+            chunk_of(key_all, lo, hi), chunk_of(value_all, lo, hi), chunk_allowed, chunk_scores
+        )
+        query_terms.append(query_term)
+        partials.append(partial)
+    grad_query = query_terms[0] + query_terms[1]
+    summed_grads = lax.psum_scatter(
+        jnp.concatenate(partials, axis=0), "cz", scatter_dimension=0, tiled=True
     )
     grad_keys_low = summed_grads[:, :HEAD_DIM].astype(jnp.bfloat16)
     grad_values_low = summed_grads[:, HEAD_DIM:].astype(jnp.bfloat16)
     grad_query_low = grad_query.astype(jnp.bfloat16).reshape(local_rows, GROUP * HEAD_DIM)
     visual_picks = visual_rows[0, 0]
-    chosen = jnp.concatenate(
-        [grad_query_low[visual_picks], grad_keys_low[visual_picks], grad_values_low[visual_picks]],
-        axis=1,
+    query_chosen = grad_query_low[visual_picks]
+    pair_chosen = jnp.concatenate(
+        [grad_keys_low[visual_picks], grad_values_low[visual_picks]], axis=1
     )
-    everyone = lax.all_gather(chosen[None], ("section", "dp"), axis=0, tiled=True)
+    everyone = jnp.concatenate(
+        [
+            lax.all_gather(query_chosen[None], ("section", "dp"), axis=0, tiled=True),
+            lax.all_gather(pair_chosen[None], ("section", "dp"), axis=0, tiled=True),
+        ],
+        axis=2,
+    )
     groups = lax.axis_size("section")
     replicas = lax.axis_size("dp")
     half_rows = visual_picks.shape[0] // 2
-    width_in = chosen.shape[1]
+    width_in = everyone.shape[2]
     arranged = (
         everyone.reshape(groups, replicas, 2, half_rows, width_in)
         .transpose(2, 1, 3, 0, 4)

time: 375 us -> 400 us (1.067)
  local copies, waits for them, and re-layouts: 11.6 us -> 40 us
  waiting for transfers between devices: 211 us -> 190 us
  other arithmetic: 22.3 us -> 38.1 us
  blocking collectives: 46.9 us -> 60.4 us
  matrix products: 68.2 us -> 56.3 us
    slice x0 -> x5, local copies, waits for them, and re-layouts: none -> 25.4 us  [the longest x4 23.7 us: chunk_of(): array.reshape((ring_y, ring_z, local_rows) + array.shape[1:])[:, lo:hi]]
    reduce_scatter x2 -> x3, waiting for transfers between devices: 127 us -> 110 us  [the longest x2 95.3 us: chunk_grads(): lax.psum_scatter(jnp.concatenate([key_part, value_part], axis=1), 'cy', s...]
    all_gather x1 -> x2, blocking collectives: 18.5 us -> 31.9 us  [the longest x1 18.1 us: shards(): lax.all_gather(pair_chosen[None], ('section', 'dp'), axis=0, tiled=True)]
    dot_general x4 -> x8, matrix products: 50.8 us -> 39 us  [the longest x2 16.6 us: chunk_grads(): jnp.einsum('qhd,kd->hqk', grad_heads, chunk_values, preferred_element_typ...]
    convert_element_type x0 -> x1, other arithmetic: none -> 10.5 us  [chunk_grads(): probs_low = probability.astype(jnp.bfloat16)]
    unnamed x18 -> x42, local copies, waits for them, and re-layouts: 5.78 us -> 8.8 us
  transfers between devices with their start and end apart: 4 -> 5, of which waited for: 4 -> 5; matrix products, arithmetic and copies ran while one was open for 5% -> 10% of each run, Pallas kernels for 0% -> 0%
where the time goes in v3:
time: 400 us; the launch traced here: 399 us
  waiting for transfers between devices  190 us (48%)
  blocking collectives  60.4 us (15%)
  matrix products  56.3 us (14%)
  local copies, waits for them, and re-layouts  40 us (10%)
  other arithmetic  38.1 us (10%)
  between operations  14.2 us (4%)
    reduce_scatter x2, waiting for transfers between devices, chunk_grads(): lax.psum_scatter(jnp.concatenate([key_part, value_part], axis=1), 'cy', s...  95.3 us
    all_gather x1, waiting for transfers between devices, shards(): lax.all_gather(lax.all_gather(own_pair, 'cz', axis=0, tiled=True), 'cy',...  49.3 us
    reduce_scatter x1, waiting for transfers between devices, shards(): lax.psum_scatter(jnp.dot(visual_grad, projector_weight, preferred_element...  30.7 us
    all_gather x1, blocking collectives, shards(): lax.all_gather(own_pair, 'cz', axis=0, tiled=True)  28.4 us
    slice x4, local copies, waits for them, and re-layouts, chunk_of(): array.reshape((ring_y, ring_z, local_rows) + array.shape[1:])[:, lo:hi]  23.7 us
    all_gather x1, blocking collectives, shards(): lax.all_gather(pair_chosen[None], ('section', 'dp'), axis=0, tiled=True)  18.1 us
    dot_general x2, matrix products, chunk_grads(): jnp.einsum('qhd,kd->hqk', grad_heads, chunk_values, preferred_element_typ...  16.6 us
    reduce_scatter x1, waiting for transfers between devices, shards(): lax.psum_scatter(jnp.concatenate(partials, axis=0), 'cz', scatter_dimensi...  14.5 us
  transfers between devices with their start and end apart: 5, of which 5 were waited for; matrix products, arithmetic and copies ran while one was open for 10% of the time, Pallas kernels for 0%

profile of v3, /device:TPU:1, one launch (start us, length us, event | category | flops | bytes accessed | tf_op | source)
XLA Modules:
  0.0 399.2 jit_solution(16075960261216749493)
XLA Ops:
  7.2 0.0 copy-start
  7.2 0.0 all-gather.4.cloned.1.call-start
  7.2 0.9 pad_maximum_fusion.4
  8.2 28.4 %all_gather.12 = bf16[1024,256]{1,0:T(8,128)(2,1)} all-gather(bf16[128,256]{1,0:T(8,128)(2,1)S(1)} %pad_maximum_fusion.4), channel_id=1, replica_groups=mesh['cz'=8,'cy'=8,'section'=2,'dp'=4] {'cz'}, dimensions={0}, use_global_device_ids=true | all-gather | bytes 589824 | tf_op jit(solution)/shard_map/all_gather | solution.py:43
  36.6 0.0 all-gather.4.cloned.1.call-update
  36.6 0.0 reduce-scatter.5.cloned.1.call-start
  36.7 1.8 copy.53
  38.5 1.8 copy.56
  40.2 0.7 copy.89
  40.9 0.7 dynamic-slice_bitcast_fusion
  41.6 0.8 fusion.24
  42.3 2.8 compare_or_fusion.1
  45.1 1.1 fusion.22
  46.2 2.8 compare_or_fusion
  49.0 49.3 %all-gather.4.cloned.1.call-done = bf16[8192,256]{1,0:T(8,128)(2,1)} async-done(((bf16[1024,256]{1,0:T(8,128)(2,1)}), bf16[8192,256]{1,0:T(8,128)(2,1)}) %all-gather.4.cloned.1.call-update) | async-done | bytes 4194320 | tf_op jit(solution)/shard_map/all_gather | solution.py:42
  98.2 13.1 %fusion = (f32[7,128]{1,0:T(8,128)S(1)}, f32[8192,128,7]{1,0,2:T(8,128)}) fusion(pred[128,8192]{0,1:T(8,128)(4,1)S(1)} %compare_or_fusion, bf16[128,7,128]{0,2,1:T(8,128)(2,1)} %bitcast.170, bf16[8192,256]{1,0:T(8,128)(2,1)} %all-gather.4.cloned.1.call-done), kind=kOutput, calls=%fused_computation.6 | convolution fusion | flops 1901067392 | bytes 32738816 | tf_op jit(solution)/shard_map/qhd,kd->hqk/dot_general | solution.py:60
  111.3 12.2 %exponential_reduce_fusion = f32[7,128]{1,0:T(8,128)S(1)} fusion(f32[8192,128,7]{1,0,2:T(8,128)} %get-tuple-element.31, f32[7,128]{1,0:T(8,128)S(1)} %get-tuple-element.30, pred[128,8192]{0,1:T(8,128)(4,1)S(1)} %compare_or_fusion), kind=kLoop, calls=%fused_computation.5 | loop fusion | flops 22019200 | bytes 30415872 | tf_op jit(solution)/shard_map/reduce_sum | solution.py:65
  123.6 19.6 %fusion.18 = (f32[8,4,128,7,128]{4,2,1,0,3:T(8,128)}, f32[8,4,128,7,128]{4,2,1,0,3:T(8,128)}) fusion(f32[8,8,128,7,128]{4,2,1,0,3:T(8,128)} %bitcast.154), kind=kLoop, calls=%fused_computation.59 | loop fusion | bytes 58720256 | tf_op jit(solution)/shard_map/slice | solution.py:99
  143.2 1.7 fusion.19
  144.9 1.2 fusion.21
  146.1 9.3 %fusion.5 = bf16[7,128,4096]{1,2,0:T(8,128)(2,1)} fusion(f32[8,4,128,7,128]{4,2,1,0,3:T(8,128)} %get-tuple-element.12, bf16[4096,128,1]{1,0,2:T(8,128)(2,1)S(1)} %bitcast.180, bf16[128,7,128]{0,2,1:T(8,128)(2,1)S(1)} %bitcast.173, f32[7,128]{1,0:T(8,128)S(1)} %bitcast.186, f32[7,128]{1,0:T(8,128)S(1)} %log_add_fusion, pred[128,4096]{0,1:T(8,128)(4,1)S(1)} %bitcast.168), kind=kOutput, calls=%fused_computation.15 | convolution fusion | flops 957874176 | bytes 23829504 | tf_op jit(solution)/shard_map/qhd,kd->hqk/dot_general | solution.py:73
  155.4 6.1 %fusion.10 = f32[4096,128]{0,1:T(8,128)S(1)} fusion(bf16[7,128,4096]{1,2,0:T(8,128)(2,1)} %fusion.5, bf16[128,7,128]{0,2,1:T(8,128)(2,1)} %bitcast.171), kind=kOutput, calls=%fused_computation.27 | convolution fusion | flops 940048384 | bytes 9666560 | tf_op jit(solution)/shard_map/hqk,qhd->kd/dot_general | solution.py:82
  161.6 10.5 %fusion.7 = (bf16[7,128,4096]{1,2,0:T(8,128)(2,1)S(1)}, bf16[7,128,4096]{1,2,0:T(8,128)(2,1)}) fusion(f32[8,4,128,7,128]{4,2,1,0,3:T(8,128)} %get-tuple-element.12, f32[7,128]{1,0:T(8,128)S(1)} %log_add_fusion, pred[128,4096]{0,1:T(8,128)(4,1)S(1)} %bitcast.169, f32[8,4,128,7,128]{4,2,1,0,3:T(8,128)S(1)} %bitcast.156, pred[128,4096]{0,1:T(8,128)(4,1)S(1)} %bitcast.166), kind=kLoop, calls=%fused_computation.20 | loop fusion | flops 22020096 | bytes 45092352 | tf_op jit(solution)/shard_map/convert_element_type | solution.py:72
  172.0 2.4 convolution_bitcast_fusion.2
  174.5 2.4 pad_maximum_fusion
  176.8 0.0 reduce-scatter.5.cloned.1.call-update
  176.9 0.2 reduce-scatter.7.cloned.1.call-start
  177.1 5.6 %convolution_bitcast_fusion = f32[4096,128]{0,1:T(8,128)S(1)} fusion(bf16[7,128,4096]{1,2,0:T(8,128)(2,1)} %get-tuple-element.29, bf16[128,7,128]{0,2,1:T(8,128)(2,1)S(1)} %bitcast.175), kind=kOutput, calls=%fused_computation.22 | convolution fusion | flops 939524096 | bytes 9666560 | tf_op jit(solution)/shard_map/hqk,qhd->kd/dot_general | solution.py:87
  182.7 7.3 %fusion.2 = bf16[7,128,4096]{1,2,0:T(8,128)(2,1)S(1)} fusion(f32[8,4,128,7,128]{4,2,1,0,3:T(8,128)} %get-tuple-element.13, bf16[4096,128,1]{1,0,2:T(8,128)(2,1)S(1)} %bitcast.179, bf16[128,7,128]{0,2,1:T(8,128)(2,1)S(1)} %bitcast.176, f32[7,128]{1,0:T(8,128)S(1)} %bitcast.187, f32[7,128]{1,0:T(8,128)S(1)} %log_add_fusion, pred[128,4096]{0,1:T(8,128)(4,1)S(1)} %bitcast.167), kind=kOutput, calls=%fused_computation.9 | convolution fusion | flops 957874176 | bytes 23829504 | tf_op jit(solution)/shard_map/qhd,kd->hqk/dot_general | solution.py:73
  190.1 3.0 copy-done.1
  193.1 2.4 fusion.9
  195.5 0.0 copy-start.10
  195.5 2.5 pad_maximum_fusion.1
  198.0 0.0 reduce-scatter.7.cloned.1.call-update
  198.0 0.0 reduce-scatter.9.cloned.1.call-start
  198.0 35.7 %reduce-scatter.5.cloned.1.call-done = f32[512,256]{0,1:T(8,128)} async-done(((f32[4096,256]{0,1:T(8,128)}), f32[512,256]{0,1:T(8,128)}) %reduce-scatter.5.cloned.1.call-update) | async-done | bytes 524304 | tf_op jit(solution)/shard_map/reduce_scatter | solution.py:90
  233.7 59.6 %reduce-scatter.7.cloned.1.call-done = f32[512,256]{0,1:T(8,128)} async-done(((f32[4096,256]{0,1:T(8,128)}), f32[512,256]{0,1:T(8,128)}) %reduce-scatter.7.cloned.1.call-update) | async-done | bytes 524304 | tf_op jit(solution)/shard_map/reduce_scatter | solution.py:90
  293.3 2.3 pad_maximum_fusion.2
  295.6 0.0 reduce-scatter.9.cloned.1.call-update
  295.7 0.0 reduce-scatter.11.cloned.1.call-start
  295.8 1.8 fusion.20
  297.6 4.5 %fusion.25 = f32[128,7,128]{2,0,1:T(8,128)S(1)} fusion(bf16[4096,128,1]{1,0,2:T(8,128)(2,1)S(1)} %bitcast.162, bf16[7,128,4096]{1,2,0:T(8,128)(2,1)} %fusion.5), kind=kOutput, calls=%fused_computation.66 | convolution fusion | flops 939524096 | bytes 8847360 | tf_op jit(solution)/shard_map/hqk,kd->qhd/dot_general | solution.py:78
  302.2 1.3 fusion.13
  303.5 0.0 copy-start.11
  303.5 0.2 copy.67
  303.7 0.6 gather_fusion
  304.3 13.8 %all-gather = bf16[256,896]{1,0:T(8,128)(2,1)S(1)} all-gather(bf16[32,896]{1,0:T(8,128)(2,1)S(1)} %gather_fusion), channel_id=2, replica_groups=mesh['cz'=8,'cy'=8,'section'=2,'dp'=4] {'section','dp'}, dimensions={0}, use_global_device_ids=true | all-gather | bytes 516096 | tf_op jit(solution)/shard_map/all_gather | solution.py:127
  318.1 14.5 %reduce-scatter.9.cloned.1.call-done = f32[128,256]{0,1:T(8,128)} async-done(((f32[1024,256]{0,1:T(8,128)}), f32[128,256]{0,1:T(8,128)}) %reduce-scatter.9.cloned.1.call-update) | async-done | bytes 131088 | tf_op jit(solution)/shard_map/reduce_scatter | solution.py:114
  332.6 0.9 convert.5
  333.5 0.1 copy.68
  333.7 0.6 gather_fusion.1
  334.3 0.1 copy.69
  334.4 0.6 gather_fusion.2
  335.0 18.1 %all-gather.1 = bf16[256,256]{1,0:T(8,128)(2,1)S(1)} all-gather(bf16[32,256]{1,0:T(8,128)(2,1)S(1)} %pad_maximum_fusion.5), channel_id=3, replica_groups=mesh['cz'=8,'cy'=8,'section'=2,'dp'=4] {'section','dp'}, dimensions={0}, use_global_device_ids=true | all-gather | bytes 147456 | tf_op jit(solution)/shard_map/all_gather | solution.py:128
  353.1 0.1 pad_maximum_fusion.3
  353.2 0.6 copy.70
  353.8 0.1 copy.85
  353.9 4.2 %convolution_convert_fusion = bf16[128,2560]{1,0:T(8,128)(2,1)} fusion(bf16[448,2560]{1,0:T(8,128)(2,1)S(1)} %copy-done, bf16[128,2304]{1,0:T(8,128)(2,1)S(1)} %bitcast.165, bf16[2304,448]{0,1:T(8,128)(2,1)} %param.18), kind=kOutput, calls=%fused_computation.32 | convolution fusion | flops 558227456 | bytes 5603328 | tf_op jit(solution)/shard_map/dot_general | solution.py:145
  358.1 0.0 reduce-scatter.11.cloned.1.call-update
  358.2 0.7 copy.71
  358.9 0.7 copy.72
  359.6 30.7 %reduce-scatter.11.cloned.1.call-done = bf16[16,2560]{1,0:T(8,128)(2,1)} async-done(((bf16[128,2560]{1,0:T(8,128)(2,1)}), bf16[16,2560]{1,0:T(8,128)(2,1)}) %reduce-scatter.11.cloned.1.call-update) | async-done | bytes 81936 | tf_op jit(solution)/shard_map/reduce_scatter | solution.py:144
  390.4 0.9 reshape.294
  391.3 1.3 gather_fusion.3
  (43 shorter events, 0.1 us)
Async XLA Ops:
  7.2 346.7 %copy-start = (bf16[448,2560]{1,0:T(8,128)(2,1)S(1)}, bf16[448,2560]{1,0:T(8,128)(2,1)}, u32[]{:S(2)}) copy-start(bf16[448,2560]{1,0:T(8,128)(2,1)} %param.19) | copy-start | bytes 6881284
  7.2 91.1 %all-gather.4.cloned.1.call-start = ((), (), s32[]{:S(2)}) async-start(), calls=%async_computation.4 | async-start | bytes 4718592 | tf_op jit(solution)/shard_map/all_gather | solution.py:42
  36.6 197.1 %reduce-scatter.5.cloned.1.call-start = ((), (), s32[]{:S(2)}) async-start(), calls=%async_computation.5 | async-start | bytes 4718592 | tf_op jit(solution)/shard_map/reduce_scatter | solution.py:90
  123.6 19.6 %copy-start.2 = (bf16[8192,256]{1,0:T(8,128)(2,1)S(1)}, bf16[8192,256]{1,0:T(8,128)(2,1)}, u32[]{:S(2)}) copy-start(bf16[8192,256]{1,0:T(8,128)(2,1)} %all-gather.4.cloned.1.call-done) | copy-start | bytes 12582916
  143.2 2.9 copy-start.4
  143.2 2.9 copy-start.6
  146.1 15.4 %slice-start = ((s8[14680064]{0:T(1024)(128)(4,1)}), s8[4194304]{0:T(1024)(128)(4,1)S(1)}, s32[]{:S(2)}) async-start(s8[14680064]{0:T(1024)(128)(4,1)} %bitcast.155), calls=%async_computation.9 | async-start | bytes 8388608
  146.1 15.4 %slice-start.1 = ((s8[14680064]{0:T(1024)(128)(4,1)}), s8[4194304]{0:T(1024)(128)(4,1)S(1)}, s32[]{:S(2)}) async-start(s8[14680064]{0:T(1024)(128)(4,1)} %bitcast.155), calls=%async_computation.10 | async-start | bytes 8388608
  146.1 15.4 %slice-start.2 = ((s8[14680064]{0:T(1024)(128)(4,1)}), s8[2097152]{0:T(1024)(128)(4,1)S(1)}, s32[]{:S(2)}) async-start(s8[14680064]{0:T(1024)(128)(4,1)} %bitcast.155), calls=%async_computation.11 | async-start | bytes 4194304
  155.4 6.2 %slice-start.3 = ((s8[14680064]{0:T(1024)(128)(4,1)}), s8[4194304]{0:T(1024)(128)(4,1)S(1)}, s32[]{:S(2)}) async-start(s8[14680064]{0:T(1024)(128)(4,1)} %bitcast.155), calls=%async_computation.12 | async-start | bytes 8388608
  155.4 6.2 %copy-start.3 = (pred[8,4,128,128]{3,2,1,0:T(8,128)(4,1)S(1)}, pred[8,4,128,128]{3,2,1,0:T(8,128)(4,1)}, u32[]{:S(2)}) copy-start(pred[8,4,128,128]{3,2,1,0:T(8,128)(4,1)} %get-tuple-element.21) | copy-start | bytes 1572868
  161.5 10.5 %copy-start.7 = (bf16[1,128,896]{1,2,0:T(8,128)(2,1)S(1)}, bf16[1,128,896]{1,2,0:T(8,128)(2,1)}, u32[]{:S(2)}) copy-start(bf16[1,128,896]{1,2,0:T(8,128)(2,1)} %copy.56) | copy-start | bytes 688132
  174.5 2.6 copy-start.8
  176.9 116.5 %reduce-scatter.7.cloned.1.call-start = ((), (), s32[]{:S(2)}) async-start(), calls=%async_computation.6 | async-start | bytes 4718592 | tf_op jit(solution)/shard_map/reduce_scatter | solution.py:90
  177.1 5.6 %copy-start.9 = (bf16[8,4,128,128]{3,2,1,0:T(8,128)(2,1)S(1)}, bf16[8,4,128,128]{3,2,1,0:T(8,128)(2,1)}, u32[]{:S(2)}) copy-start(bf16[8,4,128,128]{3,2,1,0:T(8,128)(2,1)} %get-tuple-element.19) | copy-start | bytes 3145732
  182.7 10.3 %copy-start.5 = (bf16[1,128,896]{1,2,0:T(8,128)(2,1)S(1)}, bf16[1,128,896]{1,2,0:T(8,128)(2,1)}, u32[]{:S(2)}) copy-start(bf16[1,128,896]{1,2,0:T(8,128)(2,1)} %copy.53) | copy-start | bytes 688132
  190.1 3.0 copy-start.1
  195.5 100.2 %copy-start.10 = (s32[1,1,32]{2,1,0:T(1,128)S(1)}, s32[1,1,32]{2,1,0:T(1,128)}, u32[]{:S(2)}) copy-start(s32[1,1,32]{2,1,0:T(1,128)} %param.16) | copy-start | bytes 388
  198.0 134.6 %reduce-scatter.9.cloned.1.call-start = ((), (), s32[]{:S(2)}) async-start(), calls=%async_computation.7 | async-start | bytes 1179648 | tf_op jit(solution)/shard_map/reduce_scatter | solution.py:114
  295.7 94.7 %reduce-scatter.11.cloned.1.call-start = ((), (), s32[]{:S(2)}) async-start(), calls=%async_computation.8 | async-start | bytes 737280 | tf_op jit(solution)/shard_map/reduce_scatter | solution.py:144
  295.8 6.4 %slice-start.4 = ((s8[7340032]{0:T(1024)(128)(4,1)}), s8[4194304]{0:T(1024)(128)(4,1)S(1)}, s32[]{:S(2)}) async-start(s8[7340032]{0:T(1024)(128)(4,1)} %bitcast.157), calls=%async_computation.13 | async-start | bytes 8388608
  297.6 4.6 %slice-start.5 = ((s8[7340032]{0:T(1024)(128)(4,1)}), s8[3145728]{0:T(1024)(128)(4,1)S(1)}, s32[]{:S(2)}) async-start(s8[7340032]{0:T(1024)(128)(4,1)} %bitcast.157), calls=%async_computation.14 | async-start | bytes 6291456
  303.5 54.6 %copy-start.11 = (s32[1,1,64]{2,1,0:T(1,128)S(1)}, s32[1,1,64]{2,1,0:T(1,128)}, u32[]{:S(2)}) copy-start(s32[1,1,64]{2,1,0:T(1,128)} %param.17) | copy-start | bytes 772
Sparse Core Ops, SparseCore 0:
  36.8 61.4 all-gather.3
  177.0 56.6 reduce-scatter.4
  236.6 56.7 reduce-scatter.6
  296.0 36.5 reduce-scatter.8
  358.2 32.0 reduce-scatter.10

commit v4 on v2

--- a/solution.py
+++ b/solution.py
@@ -84,11 +84,11 @@
     )
     summed_grads = lax.psum_scatter(
         lax.psum_scatter(
-            jnp.concatenate([key_part, value_part], axis=1),
+            jnp.concatenate([key_part, value_part], axis=1).astype(jnp.bfloat16),
             "cy",
             scatter_dimension=0,
             tiled=True,
-        ),
+        ).astype(jnp.float32),
         "cz",
         scatter_dimension=0,
         tiled=True,

time: 375 us -> 332 us (0.89)
  waiting for transfers between devices: 211 us -> 169 us
    reduce_scatter x1, waiting for transfers between devices: 96.4 us -> 56.8 us  [shards(): lax.psum_scatter(jnp.concatenate([key_part, value_part], axis=1).astype(j...]
  transfers between devices with their start and end apart: 4 -> 4, of which waited for: 4 -> 4; matrix products, arithmetic and copies ran while one was open for 5% -> 6% of each run, Pallas kernels for 0% -> 0%
where the time goes in v4:
time: 332 us; the launch traced here: 331 us
  waiting for transfers between devices  169 us (51%)
  matrix products  68.2 us (21%)
  blocking collectives  47.2 us (14%)
  other arithmetic  19.6 us (6%)
  between operations  14 us (4%)
  local copies, waits for them, and re-layouts  12.4 us (4%)
    reduce_scatter x1, waiting for transfers between devices, shards(): lax.psum_scatter(jnp.concatenate([key_part, value_part], axis=1).astype(j...  56.8 us
    all_gather x1, waiting for transfers between devices, shards(): lax.all_gather(lax.all_gather(own_pair, 'cz', axis=0, tiled=True), 'cy',...  53.1 us
    reduce_scatter x1, waiting for transfers between devices, shards(): lax.psum_scatter(jnp.dot(visual_grad, projector_weight, preferred_element...  30.7 us
    reduce_scatter x1, waiting for transfers between devices, shards(): lax.psum_scatter(lax.psum_scatter(jnp.concatenate([key_part, value_part],...  28.7 us
    all_gather x1, blocking collectives, shards(): lax.all_gather(own_pair, 'cz', axis=0, tiled=True)  28.4 us
    dot_general x1, matrix products, shards(): jnp.einsum('qhd,kd->hqk', grad_heads, value_all, preferred_element_type=j...  19.4 us
    all_gather x1, blocking collectives, shards(): lax.all_gather(chosen[None], ('section', 'dp'), axis=0, tiled=True)  18.8 us
    dot_general x1, matrix products, shards(): jnp.einsum('hqk,qhd->kd', probs_low, grad_heads, preferred_element_type=j...  13.4 us
  transfers between devices with their start and end apart: 4, of which 4 were waited for; matrix products, arithmetic and copies ran while one was open for 6% of the time, Pallas kernels for 0%

profile of v4, /device:TPU:1, one launch (start us, length us, event | category | flops | bytes accessed | tf_op | source)
XLA Modules:
  0.0 330.8 jit_solution(16535619733414794945)
XLA Ops:
  7.2 0.0 copy-start
  7.2 0.0 all-gather.3.cloned.1.call-start
  7.2 0.9 pad_maximum_fusion.2
  8.2 28.4 %all_gather.9 = bf16[1024,256]{1,0:T(8,128)(2,1)} all-gather(bf16[128,256]{1,0:T(8,128)(2,1)S(1)} %pad_maximum_fusion.2), channel_id=1, replica_groups=mesh['cz'=8,'cy'=8,'section'=2,'dp'=4] {'cz'}, dimensions={0}, use_global_device_ids=true | all-gather | bytes 589824 | tf_op jit(solution)/shard_map/all_gather | solution.py:43
  36.6 0.0 all-gather.3.cloned.1.call-update
  36.6 0.0 reduce-scatter.4.cloned.1.call-start
  36.7 1.8 copy.43
  38.5 1.8 copy.41
  40.2 0.7 copy.66
  40.9 0.7 dynamic-slice_bitcast_fusion
  41.6 0.8 copy_bitcast_fusion
  42.4 2.8 compare_or_fusion
  45.1 53.1 %all-gather.3.cloned.1.call-done = bf16[8192,256]{1,0:T(8,128)(2,1)} async-done(((bf16[1024,256]{1,0:T(8,128)(2,1)}), bf16[8192,256]{1,0:T(8,128)(2,1)}) %all-gather.3.cloned.1.call-update) | async-done | bytes 4194320 | tf_op jit(solution)/shard_map/all_gather | solution.py:42
  98.2 13.1 %fusion.4 = (f32[7,128]{1,0:T(8,128)S(1)}, f32[8192,128,7]{1,0,2:T(8,128)}) fusion(pred[128,8192]{0,1:T(8,128)(4,1)S(1)} %compare_or_fusion, bf16[128,7,128]{0,2,1:T(8,128)(2,1)} %bitcast.104, bf16[8192,256]{1,0:T(8,128)(2,1)} %all-gather.3.cloned.1.call-done), kind=kOutput, calls=%fused_computation.12 | convolution fusion | flops 1901067392 | bytes 32738816 | tf_op jit(solution)/shard_map/qhd,kd->hqk/dot_general | solution.py:60
  111.3 0.0 copy-start.2
  111.3 12.7 %exponential_reduce_fusion = f32[7,128]{1,0:T(8,128)S(1)} fusion(f32[8192,128,7]{1,0,2:T(8,128)} %get-tuple-element.17, f32[7,128]{1,0:T(8,128)S(1)} %get-tuple-element.16, pred[128,8192]{0,1:T(8,128)(4,1)S(1)} %compare_or_fusion), kind=kLoop, calls=%fused_computation.11 | loop fusion | flops 29359232 | bytes 30415872 | tf_op jit(solution)/shard_map/reduce_sum | solution.py:65
  124.1 0.0 copy-done.2
  124.1 0.0 copy-start.1
  124.1 13.4 %fusion.13 = bf16[8192,128]{0,1:T(8,128)(2,1)S(1)} fusion(bf16[128,7,128]{0,2,1:T(8,128)(2,1)S(1)} %bitcast.102, f32[8192,128,7]{1,0,2:T(8,128)} %get-tuple-element.17, f32[7,128]{1,0:T(8,128)S(1)} %log_add_fusion, pred[128,8192]{0,1:T(8,128)(4,1)S(1)} %compare_or_fusion), kind=kOutput, calls=%fused_computation.19 | convolution fusion | flops 1909456896 | bytes 32738816 | tf_op jit(solution)/shard_map/hqk,qhd->kd/dot_general | solution.py:82
  137.5 0.0 copy-done.1
  137.5 0.0 copy-start.3
  137.5 19.4 %fusion.1 = bf16[7,128,8192]{1,2,0:T(8,128)(2,1)} fusion(f32[8192,128,7]{1,0,2:T(8,128)} %get-tuple-element.17, bf16[128,7,128]{0,2,1:T(8,128)(2,1)S(1)} %bitcast.103, f32[7,128]{1,0:T(8,128)S(1)} %bitcast.110, f32[7,128]{1,0:T(8,128)S(1)} %log_add_fusion, pred[128,8192]{0,1:T(8,128)(4,1)S(1)} %compare_or_fusion, bf16[8192,256]{1,0:T(8,128)(2,1)S(1)} %copy-done.1), kind=kOutput, calls=%fused_computation.6 | convolution fusion | flops 1923088384 | bytes 47423488 | tf_op jit(solution)/shard_map/qhd,kd->hqk/dot_general | solution.py:70
  156.9 0.0 copy-done.3
  156.9 9.9 %fusion.16 = bf16[8192,128]{0,1:T(8,128)(2,1)S(1)} fusion(bf16[7,128,8192]{1,2,0:T(8,128)(2,1)} %fusion.1, bf16[128,7,128]{0,2,1:T(8,128)(2,1)S(1)} %bitcast.105), kind=kOutput, calls=%fused_computation.20 | convolution fusion | flops 1881145344 | bytes 17006592 | tf_op jit(solution)/shard_map/hqk,qhd->kd/dot_general | solution.py:79
  166.8 0.0 copy-start.4
  166.8 2.4 pad_maximum_fusion
  169.2 0.0 reduce-scatter.4.cloned.1.call-update
  169.2 0.0 reduce-scatter.6.cloned.1.call-start
  169.3 0.0 copy-done.4
  169.3 56.8 %reduce-scatter.4.cloned.1.call-done = bf16[1024,256]{0,1:T(8,128)(2,1)} async-done(((bf16[8192,256]{0,1:T(8,128)(2,1)}), bf16[1024,256]{0,1:T(8,128)(2,1)}) %reduce-scatter.4.cloned.1.call-update) | async-done | bytes 524304 | tf_op jit(solution)/shard_map/reduce_scatter | solution.py:86
  226.1 0.0 reduce-scatter.6.cloned.1.call-update
  226.1 0.0 reduce-scatter.8.cloned.1.call-start
  226.2 8.2 %fusion.20 = bf16[128,7,128]{2,0,1:T(8,128)(2,1)S(1)} fusion(bf16[7,128,8192]{1,2,0:T(8,128)(2,1)} %fusion.1, bf16[8192,256]{1,0:T(8,128)(2,1)} %all-gather.3.cloned.1.call-done), kind=kOutput, calls=%fused_computation.29 | convolution fusion | flops 1879277568 | bytes 17006592 | tf_op jit(solution)/shard_map/hqk,kd->qhd/dot_general | solution.py:75
  234.4 0.0 copy-start.5
  234.4 0.2 copy.49
  234.5 0.6 gather_fusion
  235.2 28.7 %reduce-scatter.6.cloned.1.call-done = bf16[128,256]{0,1:T(8,128)(2,1)} async-done(((bf16[1024,256]{0,1:T(8,128)(2,1)}), bf16[128,256]{0,1:T(8,128)(2,1)}) %reduce-scatter.6.cloned.1.call-update) | async-done | bytes 65552 | tf_op jit(solution)/shard_map/reduce_scatter | solution.py:85
  263.9 0.8 fusion.25
  264.7 0.1 copy.51
  264.8 0.6 gather_fusion.2
  265.4 0.1 copy.50
  265.5 0.6 gather_fusion.1
  266.2 18.8 %all-gather = bf16[256,1152]{1,0:T(8,128)(2,1)S(1)} all-gather(bf16[32,1152]{1,0:T(8,128)(2,1)S(1)} %pad_maximum_fusion.1), channel_id=2, replica_groups=mesh['cz'=8,'cy'=8,'section'=2,'dp'=4] {'section','dp'}, dimensions={0}, use_global_device_ids=true | all-gather | bytes 663552 | tf_op jit(solution)/shard_map/all_gather | solution.py:104
  284.9 0.6 copy.52
  285.5 0.1 copy.63
  285.6 0.0 copy-done
  285.6 4.2 %convolution_convert_fusion = bf16[128,2560]{1,0:T(8,128)(2,1)} fusion(bf16[448,2560]{1,0:T(8,128)(2,1)S(1)} %copy-done, bf16[128,2304]{1,0:T(8,128)(2,1)S(1)} %bitcast.100, bf16[2304,448]{0,1:T(8,128)(2,1)} %param.18), kind=kOutput, calls=%fused_computation.23 | convolution fusion | flops 558227456 | bytes 5603328 | tf_op jit(solution)/shard_map/dot_general | solution.py:118
  289.8 0.0 reduce-scatter.8.cloned.1.call-update
  289.9 0.0 copy-done.5
  289.9 0.7 copy.53
  290.6 0.7 copy.54
  291.3 30.7 %reduce-scatter.8.cloned.1.call-done = bf16[16,2560]{1,0:T(8,128)(2,1)} async-done(((bf16[128,2560]{1,0:T(8,128)(2,1)}), bf16[16,2560]{1,0:T(8,128)(2,1)}) %reduce-scatter.8.cloned.1.call-update) | async-done | bytes 81936 | tf_op jit(solution)/shard_map/reduce_scatter | solution.py:117
  322.0 0.9 reshape.215
  322.9 1.3 gather_fusion.3
  (7 shorter events, 0.0 us)
Async XLA Ops:
  7.2 278.5 %copy-start = (bf16[448,2560]{1,0:T(8,128)(2,1)S(1)}, bf16[448,2560]{1,0:T(8,128)(2,1)}, u32[]{:S(2)}) copy-start(bf16[448,2560]{1,0:T(8,128)(2,1)} %param.19) | copy-start | bytes 6881284
  7.2 91.0 %all-gather.3.cloned.1.call-start = ((), (), s32[]{:S(2)}) async-start(), calls=%async_computation.3 | async-start | bytes 4718592 | tf_op jit(solution)/shard_map/all_gather | solution.py:42
  36.6 189.4 %reduce-scatter.4.cloned.1.call-start = ((), (), s32[]{:S(2)}) async-start(), calls=%async_computation.4 | async-start | bytes 4718592 | tf_op jit(solution)/shard_map/reduce_scatter | solution.py:86
  111.3 12.7 %copy-start.2 = (bf16[1,128,896]{1,2,0:T(8,128)(2,1)S(1)}, bf16[1,128,896]{1,2,0:T(8,128)(2,1)}, u32[]{:S(2)}) copy-start(bf16[1,128,896]{1,2,0:T(8,128)(2,1)} %copy.43) | copy-start | bytes 688132
  124.1 13.4 %copy-start.1 = (bf16[8192,256]{1,0:T(8,128)(2,1)S(1)}, bf16[8192,256]{1,0:T(8,128)(2,1)}, u32[]{:S(2)}) copy-start(bf16[8192,256]{1,0:T(8,128)(2,1)} %all-gather.3.cloned.1.call-done) | copy-start | bytes 12582916
  137.5 19.4 %copy-start.3 = (bf16[1,128,896]{1,2,0:T(8,128)(2,1)S(1)}, bf16[1,128,896]{1,2,0:T(8,128)(2,1)}, u32[]{:S(2)}) copy-start(bf16[1,128,896]{1,2,0:T(8,128)(2,1)} %copy.41) | copy-start | bytes 688132
  166.8 2.5 copy-start.4
  169.2 94.7 %reduce-scatter.6.cloned.1.call-start = ((), (), s32[]{:S(2)}) async-start(), calls=%async_computation.5 | async-start | bytes 589824 | tf_op jit(solution)/shard_map/reduce_scatter | solution.py:85
  226.1 95.9 %reduce-scatter.8.cloned.1.call-start = ((), (), s32[]{:S(2)}) async-start(), calls=%async_computation.6 | async-start | bytes 737280 | tf_op jit(solution)/shard_map/reduce_scatter | solution.py:117
  234.4 55.5 %copy-start.5 = (s32[1,1,64]{2,1,0:T(1,128)S(1)}, s32[1,1,64]{2,1,0:T(1,128)}, u32[]{:S(2)}) copy-start(s32[1,1,64]{2,1,0:T(1,128)} %param.17) | copy-start | bytes 772
Sparse Core Ops, SparseCore 0:
  36.8 61.4 all-gather.2
  169.3 56.6 reduce-scatter.3
  228.9 34.9 reduce-scatter.5
  290.0 31.9 reduce-scatter.7

commit v5 on v4

--- a/solution.py
+++ b/solution.py
@@ -114,14 +114,16 @@
     visual_grad = jnp.dot(arranged, qkv_weight, preferred_element_type=jnp.float32).astype(
         jnp.bfloat16
     )
-    shuffled = lax.psum_scatter(
+    pieces = lax.all_to_all(
         jnp.dot(visual_grad, projector_weight, preferred_element_type=jnp.float32).astype(
             jnp.bfloat16
         ),
         ("section", "dp"),
-        scatter_dimension=0,
+        0,
+        0,
         tiled=True,
-    ).astype(jnp.float32)
+    )
+    shuffled = pieces.astype(jnp.float32).reshape(groups * replicas, -1, pieces.shape[1]).sum(0)
     slot_rows = shuffled.reshape(half_rows * 4, projector_weight.shape[1] // 4)
     patches = slot_rows[shuffle_source[0, 0]].astype(jnp.bfloat16)
     return (grad_keys_low[None], grad_values_low[None], patches[None])

time: 332 us -> 313 us (0.943)
  waiting for transfers between devices: 169 us -> 148 us
  starting transfers between devices: 0.16 us -> 3.93 us
    reduce_scatter x1 -> x0, waiting for transfers between devices: 30.7 us -> none  [shards(): lax.psum_scatter(jnp.dot(visual_grad, projector_weight, preferred_element...]
    all_to_all x0 -> x1, waiting for transfers between devices: none -> 9.42 us  [shards(): lax.all_to_all(jnp.dot(visual_grad, projector_weight, preferred_element_t...]
    all_to_all x0 -> x1, starting transfers between devices: none -> 3.81 us  [shards(): lax.all_to_all(jnp.dot(visual_grad, projector_weight, preferred_element_t...]
where the time goes in v5:
time: 313 us
  waiting for transfers between devices  148 us (47%)
  matrix products  68.2 us (22%)
  blocking collectives  47.3 us (15%)
  other arithmetic  19.7 us (6%)
  between operations  13.9 us (4%)
  local copies, waits for them, and re-layouts  11.5 us (4%)
  starting transfers between devices  3.93 us (1%)
    reduce_scatter x1, waiting for transfers between devices, shards(): lax.psum_scatter(jnp.concatenate([key_part, value_part], axis=1).astype(j...  56.8 us
    all_gather x1, waiting for transfers between devices, shards(): lax.all_gather(lax.all_gather(own_pair, 'cz', axis=0, tiled=True), 'cy',...  53.1 us
    reduce_scatter x1, waiting for transfers between devices, shards(): lax.psum_scatter(lax.psum_scatter(jnp.concatenate([key_part, value_part],...  28.7 us
    all_gather x1, blocking collectives, shards(): lax.all_gather(own_pair, 'cz', axis=0, tiled=True)  28.4 us
    dot_general x1, matrix products, shards(): jnp.einsum('qhd,kd->hqk', grad_heads, value_all, preferred_element_type=j...  19.4 us
    all_gather x1, blocking collectives, shards(): lax.all_gather(chosen[None], ('section', 'dp'), axis=0, tiled=True)  18.9 us
    dot_general x1, matrix products, shards(): jnp.einsum('hqk,qhd->kd', probs_low, grad_heads, preferred_element_type=j...  13.4 us
    dot_general x1, matrix products, shards(): jnp.einsum('qhd,kd->hqk', query_heads, key_all, preferred_element_type=jn...  13.1 us
  transfers between devices with their start and end apart: 4, of which 4 were waited for; matrix products, arithmetic and copies ran while one was open for 6% of the time, Pallas kernels for 0%

profile of v5, /device:TPU:1, one launch (start us, length us, event | category | flops | bytes accessed | tf_op | source)
XLA Modules:
  0.0 312.6 jit_solution(2415836253007539415)
XLA Ops:
  7.2 0.0 copy-start
  7.2 0.0 all-gather.3.cloned.1.call-start
  7.2 0.9 pad_maximum_fusion.2
  8.2 28.4 %all_gather.9 = bf16[1024,256]{1,0:T(8,128)(2,1)} all-gather(bf16[128,256]{1,0:T(8,128)(2,1)S(1)} %pad_maximum_fusion.2), channel_id=1, replica_groups=mesh['cz'=8,'cy'=8,'section'=2,'dp'=4] {'cz'}, dimensions={0}, use_global_device_ids=true | all-gather | bytes 589824 | tf_op jit(solution)/shard_map/all_gather | solution.py:43
  36.6 0.0 all-gather.3.cloned.1.call-update
  36.6 0.0 reduce-scatter.3.cloned.1.call-start
  36.7 1.8 copy.43
  38.5 1.8 copy.41
  40.2 0.7 copy.66
  40.9 0.7 dynamic-slice_bitcast_fusion
  41.6 0.8 copy_bitcast_fusion
  42.3 2.8 compare_or_fusion
  45.1 53.1 %all-gather.3.cloned.1.call-done = bf16[8192,256]{1,0:T(8,128)(2,1)} async-done(((bf16[1024,256]{1,0:T(8,128)(2,1)}), bf16[8192,256]{1,0:T(8,128)(2,1)}) %all-gather.3.cloned.1.call-update) | async-done | bytes 4194320 | tf_op jit(solution)/shard_map/all_gather | solution.py:42
  98.2 13.1 %fusion.4 = (f32[7,128]{1,0:T(8,128)S(1)}, f32[8192,128,7]{1,0,2:T(8,128)}) fusion(pred[128,8192]{0,1:T(8,128)(4,1)S(1)} %compare_or_fusion, bf16[128,7,128]{0,2,1:T(8,128)(2,1)} %bitcast.106, bf16[8192,256]{1,0:T(8,128)(2,1)} %all-gather.3.cloned.1.call-done), kind=kOutput, calls=%fused_computation.12 | convolution fusion | flops 1901067392 | bytes 32738816 | tf_op jit(solution)/shard_map/qhd,kd->hqk/dot_general | solution.py:60
  111.3 0.0 copy-start.2
  111.4 12.7 %exponential_reduce_fusion = f32[7,128]{1,0:T(8,128)S(1)} fusion(f32[8192,128,7]{1,0,2:T(8,128)} %get-tuple-element.17, f32[7,128]{1,0:T(8,128)S(1)} %get-tuple-element.16, pred[128,8192]{0,1:T(8,128)(4,1)S(1)} %compare_or_fusion), kind=kLoop, calls=%fused_computation.11 | loop fusion | flops 29359232 | bytes 30415872 | tf_op jit(solution)/shard_map/reduce_sum | solution.py:65
  124.1 0.0 copy-done.2
  124.1 0.0 copy-start.1
  124.1 13.4 %fusion.13 = bf16[8192,128]{0,1:T(8,128)(2,1)S(1)} fusion(bf16[128,7,128]{0,2,1:T(8,128)(2,1)S(1)} %bitcast.104, f32[8192,128,7]{1,0,2:T(8,128)} %get-tuple-element.17, f32[7,128]{1,0:T(8,128)S(1)} %log_add_fusion, pred[128,8192]{0,1:T(8,128)(4,1)S(1)} %compare_or_fusion), kind=kOutput, calls=%fused_computation.19 | convolution fusion | flops 1909456896 | bytes 32738816 | tf_op jit(solution)/shard_map/hqk,qhd->kd/dot_general | solution.py:82
  137.5 0.0 copy-done.1
  137.5 0.0 copy-start.3
  137.5 19.4 %fusion.1 = bf16[7,128,8192]{1,2,0:T(8,128)(2,1)} fusion(f32[8192,128,7]{1,0,2:T(8,128)} %get-tuple-element.17, bf16[128,7,128]{0,2,1:T(8,128)(2,1)S(1)} %bitcast.105, f32[7,128]{1,0:T(8,128)S(1)} %bitcast.112, f32[7,128]{1,0:T(8,128)S(1)} %log_add_fusion, pred[128,8192]{0,1:T(8,128)(4,1)S(1)} %compare_or_fusion, bf16[8192,256]{1,0:T(8,128)(2,1)S(1)} %copy-done.1), kind=kOutput, calls=%fused_computation.6 | convolution fusion | flops 1923088384 | bytes 47423488 | tf_op jit(solution)/shard_map/qhd,kd->hqk/dot_general | solution.py:70
  156.9 0.0 copy-done.3
  156.9 9.9 %fusion.16 = bf16[8192,128]{0,1:T(8,128)(2,1)S(1)} fusion(bf16[7,128,8192]{1,2,0:T(8,128)(2,1)} %fusion.1, bf16[128,7,128]{0,2,1:T(8,128)(2,1)S(1)} %bitcast.107), kind=kOutput, calls=%fused_computation.20 | convolution fusion | flops 1881145344 | bytes 17006592 | tf_op jit(solution)/shard_map/hqk,qhd->kd/dot_general | solution.py:79
  166.8 0.0 copy-start.4
  166.8 2.4 pad_maximum_fusion
  169.2 0.0 reduce-scatter.3.cloned.1.call-update
  169.2 0.0 reduce-scatter.5.cloned.1.call-start
  169.3 0.0 copy-done.4
  169.3 56.8 %reduce-scatter.3.cloned.1.call-done = bf16[1024,256]{0,1:T(8,128)(2,1)} async-done(((bf16[8192,256]{0,1:T(8,128)(2,1)}), bf16[1024,256]{0,1:T(8,128)(2,1)}) %reduce-scatter.3.cloned.1.call-update) | async-done | bytes 524304 | tf_op jit(solution)/shard_map/reduce_scatter | solution.py:86
  226.1 0.0 reduce-scatter.5.cloned.1.call-update
  226.1 8.2 %fusion.20 = bf16[128,7,128]{2,0,1:T(8,128)(2,1)S(1)} fusion(bf16[7,128,8192]{1,2,0:T(8,128)(2,1)} %fusion.1, bf16[8192,256]{1,0:T(8,128)(2,1)} %all-gather.3.cloned.1.call-done), kind=kOutput, calls=%fused_computation.30 | convolution fusion | flops 1879277568 | bytes 17006592 | tf_op jit(solution)/shard_map/hqk,kd->qhd/dot_general | solution.py:75
  234.3 0.0 copy-start.5
  234.3 0.2 copy.49
  234.5 0.6 gather_fusion
  235.1 28.7 %reduce-scatter.5.cloned.1.call-done = bf16[128,256]{0,1:T(8,128)(2,1)} async-done(((bf16[1024,256]{0,1:T(8,128)(2,1)}), bf16[128,256]{0,1:T(8,128)(2,1)}) %reduce-scatter.5.cloned.1.call-update) | async-done | bytes 65552 | tf_op jit(solution)/shard_map/reduce_scatter | solution.py:85
  263.8 0.8 fusion.25
  264.6 0.1 copy.51
  264.7 0.6 gather_fusion.2
  265.3 0.1 copy.50
  265.4 0.6 gather_fusion.1
  266.1 18.9 %all-gather = bf16[256,1152]{1,0:T(8,128)(2,1)S(1)} all-gather(bf16[32,1152]{1,0:T(8,128)(2,1)S(1)} %pad_maximum_fusion.1), channel_id=2, replica_groups=mesh['cz'=8,'cy'=8,'section'=2,'dp'=4] {'section','dp'}, dimensions={0}, use_global_device_ids=true | all-gather | bytes 663552 | tf_op jit(solution)/shard_map/all_gather | solution.py:104
  284.9 0.6 copy.52
  285.5 0.1 copy.63
  285.6 0.0 copy-done
  285.6 4.2 %convolution_convert_fusion = bf16[128,2560]{1,0:T(8,128)(2,1)} fusion(bf16[448,2560]{1,0:T(8,128)(2,1)S(1)} %copy-done, bf16[128,2304]{1,0:T(8,128)(2,1)S(1)} %bitcast.102, bf16[2304,448]{0,1:T(8,128)(2,1)} %param.18), kind=kOutput, calls=%fused_computation.23 | convolution fusion | flops 558227456 | bytes 5603328 | tf_op jit(solution)/shard_map/dot_general | solution.py:118
  289.8 3.8 %all-to-all-start = ((bf16[8,16,2560]{2,1,0:T(8,128)(2,1)}), bf16[8,16,2560]{2,1,0:T(8,128)(2,1)S(1)}, u32[]{:S(2)}, u32[]{:S(2)}) async-start(bf16[8,16,2560]{2,1,0:T(8,128)(2,1)} %bitcast.99), calls=%async_computation.2 | async-start | bytes 1310720 | tf_op jit(solution)/shard_map/all_to_all | solution.py:117
  293.6 0.0 copy-done.5
  293.7 0.7 copy.53
  294.4 0.7 copy.54
  295.1 9.4 %all-to-all-done = bf16[8,16,2560]{2,1,0:T(8,128)(2,1)S(1)} async-done(((bf16[8,16,2560]{2,1,0:T(8,128)(2,1)}), bf16[8,16,2560]{2,1,0:T(8,128)(2,1)S(1)}, u32[]{:S(2)}, u32[]{:S(2)}) %all-to-all-start) | async-done | bytes 655392 | tf_op jit(solution)/shard_map/all_to_all | solution.py:117
  304.5 0.1 convert_reduce_fusion
  304.6 0.1 reshape.212
  304.7 1.3 gather_fusion.3
  (7 shorter events, 0.0 us)
Async XLA Ops:
  7.2 278.4 %copy-start = (bf16[448,2560]{1,0:T(8,128)(2,1)S(1)}, bf16[448,2560]{1,0:T(8,128)(2,1)}, u32[]{:S(2)}) copy-start(bf16[448,2560]{1,0:T(8,128)(2,1)} %param.19) | copy-start | bytes 6881284
  7.2 91.0 %all-gather.3.cloned.1.call-start = ((), (), s32[]{:S(2)}) async-start(), calls=%async_computation.3 | async-start | bytes 4718592 | tf_op jit(solution)/shard_map/all_gather | solution.py:42
  36.6 189.4 %reduce-scatter.3.cloned.1.call-start = ((), (), s32[]{:S(2)}) async-start(), calls=%async_computation.4 | async-start | bytes 4718592 | tf_op jit(solution)/shard_map/reduce_scatter | solution.py:86
  111.3 12.7 %copy-start.2 = (bf16[1,128,896]{1,2,0:T(8,128)(2,1)S(1)}, bf16[1,128,896]{1,2,0:T(8,128)(2,1)}, u32[]{:S(2)}) copy-start(bf16[1,128,896]{1,2,0:T(8,128)(2,1)} %copy.43) | copy-start | bytes 688132
  124.1 13.4 %copy-start.1 = (bf16[8192,256]{1,0:T(8,128)(2,1)S(1)}, bf16[8192,256]{1,0:T(8,128)(2,1)}, u32[]{:S(2)}) copy-start(bf16[8192,256]{1,0:T(8,128)(2,1)} %all-gather.3.cloned.1.call-done) | copy-start | bytes 12582916
  137.5 19.4 %copy-start.3 = (bf16[1,128,896]{1,2,0:T(8,128)(2,1)S(1)}, bf16[1,128,896]{1,2,0:T(8,128)(2,1)}, u32[]{:S(2)}) copy-start(bf16[1,128,896]{1,2,0:T(8,128)(2,1)} %copy.41) | copy-start | bytes 688132
  166.8 2.5 copy-start.4
  169.2 94.6 %reduce-scatter.5.cloned.1.call-start = ((), (), s32[]{:S(2)}) async-start(), calls=%async_computation.5 | async-start | bytes 589824 | tf_op jit(solution)/shard_map/reduce_scatter | solution.py:85
  234.3 59.3 %copy-start.5 = (s32[1,1,64]{2,1,0:T(1,128)S(1)}, s32[1,1,64]{2,1,0:T(1,128)}, u32[]{:S(2)}) copy-start(s32[1,1,64]{2,1,0:T(1,128)} %param.17) | copy-start | bytes 772
  289.8 14.7 %all-to-all-start = ((bf16[8,16,2560]{2,1,0:T(8,128)(2,1)}), bf16[8,16,2560]{2,1,0:T(8,128)(2,1)S(1)}, u32[]{:S(2)}, u32[]{:S(2)}) async-start(bf16[8,16,2560]{2,1,0:T(8,128)(2,1)} %bitcast.99), calls=%async_computation.2 | async-start | bytes 1310720 | tf_op jit(solution)/shard_map/all_to_all | solution.py:117
Sparse Core Ops, SparseCore 0:
  36.8 61.4 all-gather.2
  169.3 56.6 reduce-scatter.2
  228.9 34.8 reduce-scatter.4

commit v6 on v5

--- a/solution.py
+++ b/solution.py
@@ -40,7 +40,10 @@
 
     own_pair = jnp.concatenate([key_vectors[0], value_vectors[0]], axis=1)
     all_pairs = lax.all_gather(
-        lax.all_gather(own_pair, "cz", axis=0, tiled=True), "cy", axis=0, tiled=True
+        lax.all_to_all(jnp.tile(own_pair, (ring_z, 1)), "cz", 0, 0, tiled=True),
+        "cy",
+        axis=0,
+        tiled=True,
     )
     key_all = all_pairs[:, :HEAD_DIM]
     value_all = all_pairs[:, HEAD_DIM:]
@@ -82,16 +85,15 @@
     value_part = jnp.einsum(
         "hqk,qhd->kd", probs_low, grad_heads, preferred_element_type=jnp.float32
     )
-    summed_grads = lax.psum_scatter(
-        lax.psum_scatter(
-            jnp.concatenate([key_part, value_part], axis=1).astype(jnp.bfloat16),
-            "cy",
-            scatter_dimension=0,
-            tiled=True,
-        ).astype(jnp.float32),
-        "cz",
+    stage_one = lax.psum_scatter(
+        jnp.concatenate([key_part, value_part], axis=1).astype(jnp.bfloat16),
+        "cy",
         scatter_dimension=0,
         tiled=True,
+    )
+    stage_two = lax.all_to_all(stage_one, "cz", 0, 0, tiled=True)
+    summed_grads = (
+        stage_two.astype(jnp.float32).reshape(ring_z, local_rows, stage_two.shape[1]).sum(0)
     )
     grad_keys_low = summed_grads[:, :HEAD_DIM].astype(jnp.bfloat16)
     grad_values_low = summed_grads[:, HEAD_DIM:].astype(jnp.bfloat16)

time: 313 us -> 289 us (0.923)
  waiting for transfers between devices: 148 us -> 123 us
  starting transfers between devices: 3.93 us -> 11 us
  blocking collectives: 47.3 us -> 40.6 us
    reduce_scatter x1 -> x0, waiting for transfers between devices: 28.7 us -> none  [shards(): lax.psum_scatter(lax.psum_scatter(jnp.concatenate([key_part, value_part],...]
    all_gather x1 -> x0, blocking collectives: 28.4 us -> none  [shards(): lax.all_gather(own_pair, 'cz', axis=0, tiled=True)]
    all_to_all x0 -> x1, blocking collectives: none -> 26.8 us  [shards(): lax.all_to_all(jnp.tile(own_pair, (ring_z, 1)), 'cz', 0, 0, tiled=True)]
    all_to_all x0 -> x1, waiting for transfers between devices: none -> 8.94 us  [shards(): stage_two = lax.all_to_all(stage_one, 'cz', 0, 0, tiled=True)]
    all_to_all x0 -> x1, starting transfers between devices: none -> 7.1 us  [shards(): stage_two = lax.all_to_all(stage_one, 'cz', 0, 0, tiled=True)]
    all_gather x1, waiting for transfers between devices: 53.1 us -> 46.8 us  [shards(): lax.all_gather(lax.all_to_all(jnp.tile(own_pair, (ring_z, 1)), 'cz', 0, 0...]
    all_gather x1, blocking collectives: 18.9 us -> 13.8 us  [shards(): lax.all_gather(chosen[None], ('section', 'dp'), axis=0, tiled=True)]
where the time goes in v6:
time: 289 us; the launch traced here: 288 us
  waiting for transfers between devices  123 us (43%)
  matrix products  68.2 us (24%)
  blocking collectives  40.6 us (14%)
  other arithmetic  19.8 us (7%)
  between operations  14.3 us (5%)
  local copies, waits for them, and re-layouts  11.2 us (4%)
  starting transfers between devices  11 us (4%)
    reduce_scatter x1, waiting for transfers between devices, shards(): lax.psum_scatter(jnp.concatenate([key_part, value_part], axis=1).astype(j...  56.8 us
    all_gather x1, waiting for transfers between devices, shards(): lax.all_gather(lax.all_to_all(jnp.tile(own_pair, (ring_z, 1)), 'cz', 0, 0...  46.8 us
    all_to_all x1, blocking collectives, shards(): lax.all_to_all(jnp.tile(own_pair, (ring_z, 1)), 'cz', 0, 0, tiled=True)  26.8 us
    dot_general x1, matrix products, shards(): jnp.einsum('qhd,kd->hqk', grad_heads, value_all, preferred_element_type=j...  19.4 us
    all_gather x1, blocking collectives, shards(): lax.all_gather(chosen[None], ('section', 'dp'), axis=0, tiled=True)  13.8 us
    dot_general x1, matrix products, shards(): jnp.einsum('hqk,qhd->kd', probs_low, grad_heads, preferred_element_type=j...  13.4 us
    dot_general x1, matrix products, shards(): jnp.einsum('qhd,kd->hqk', query_heads, key_all, preferred_element_type=jn...  13.1 us
    reduce_sum x1, other arithmetic, shards(): summed = jnp.exp(masked_scores - running[:, :, None]).sum(axis=-1)  12.7 us
  transfers between devices with their start and end apart: 4, of which 4 were waited for; matrix products, arithmetic and copies ran while one was open for 6% of the time, Pallas kernels for 0%

profile of v6, /device:TPU:1, one launch (start us, length us, event | category | flops | bytes accessed | tf_op | source)
XLA Modules:
  0.0 288.4 jit_solution(3191562445234428152)
XLA Ops:
  7.2 0.0 copy-start
  7.2 0.0 all-gather.3.cloned.1.call-start
  7.2 0.9 pad_maximum_fusion.2
  8.2 26.8 %all_to_all.27 = bf16[8,128,256]{2,1,0:T(8,128)(2,1)} all-to-all(bf16[8,128,256]{2,1,0:T(8,128)(2,1)S(1)} %tile.2), channel_id=1, replica_groups=mesh['cz'=8,'cy'=8,'section'=2,'dp'=4] {'cz'}, dimensions={0} | all-to-all | bytes 1048576 | tf_op jit(solution)/shard_map/all_to_all | solution.py:43
  35.0 0.0 all-gather.3.cloned.1.call-update
  35.0 0.0 reduce-scatter.2.cloned.1.call-start
  35.0 1.8 copy.46
  36.8 1.8 copy.44
  38.6 0.7 copy.74
  39.3 0.7 dynamic-slice_bitcast_fusion
  39.9 0.8 copy_bitcast_fusion.1
  40.7 2.8 compare_or_fusion
  43.5 46.8 %all-gather.3.cloned.1.call-done = bf16[8192,256]{1,0:T(8,128)(2,1)} async-done(((bf16[1024,256]{1,0:T(8,128)(2,1)}), bf16[8192,256]{1,0:T(8,128)(2,1)}) %all-gather.3.cloned.1.call-update) | async-done | bytes 4194320 | tf_op jit(solution)/shard_map/all_gather | solution.py:42
  90.2 13.1 %fusion.4 = (f32[7,128]{1,0:T(8,128)S(1)}, f32[8192,128,7]{1,0,2:T(8,128)}) fusion(pred[128,8192]{0,1:T(8,128)(4,1)S(1)} %compare_or_fusion, bf16[128,7,128]{0,2,1:T(8,128)(2,1)} %bitcast.113, bf16[8192,256]{1,0:T(8,128)(2,1)} %all-gather.3.cloned.1.call-done), kind=kOutput, calls=%fused_computation.12 | convolution fusion | flops 1901067392 | bytes 32738816 | tf_op jit(solution)/shard_map/qhd,kd->hqk/dot_general | solution.py:63
  103.4 0.0 copy-start.4
  103.4 12.7 %exponential_reduce_fusion = f32[7,128]{1,0:T(8,128)S(1)} fusion(f32[8192,128,7]{1,0,2:T(8,128)} %get-tuple-element.6, f32[7,128]{1,0:T(8,128)S(1)} %get-tuple-element.5, pred[128,8192]{0,1:T(8,128)(4,1)S(1)} %compare_or_fusion), kind=kLoop, calls=%fused_computation.11 | loop fusion | flops 29359232 | bytes 30415872 | tf_op jit(solution)/shard_map/reduce_sum | solution.py:68
  116.1 0.0 copy-done.4
  116.1 0.0 copy-start.1
  116.1 13.4 %fusion.13 = bf16[8192,128]{0,1:T(8,128)(2,1)S(1)} fusion(bf16[128,7,128]{0,2,1:T(8,128)(2,1)S(1)} %bitcast.111, f32[8192,128,7]{1,0,2:T(8,128)} %get-tuple-element.6, f32[7,128]{1,0:T(8,128)S(1)} %log_add_fusion, pred[128,8192]{0,1:T(8,128)(4,1)S(1)} %compare_or_fusion), kind=kOutput, calls=%fused_computation.19 | convolution fusion | flops 1909456896 | bytes 32738816 | tf_op jit(solution)/shard_map/hqk,qhd->kd/dot_general | solution.py:85
  129.5 0.0 copy-done.1
  129.5 0.0 copy-start.5
  129.5 19.4 %fusion.1 = bf16[7,128,8192]{1,2,0:T(8,128)(2,1)} fusion(f32[8192,128,7]{1,0,2:T(8,128)} %get-tuple-element.6, bf16[128,7,128]{0,2,1:T(8,128)(2,1)S(1)} %bitcast.112, f32[7,128]{1,0:T(8,128)S(1)} %bitcast.119, f32[7,128]{1,0:T(8,128)S(1)} %log_add_fusion, pred[128,8192]{0,1:T(8,128)(4,1)S(1)} %compare_or_fusion, bf16[8192,256]{1,0:T(8,128)(2,1)S(1)} %copy-done.1), kind=kOutput, calls=%fused_computation.6 | convolution fusion | flops 1923088384 | bytes 47423488 | tf_op jit(solution)/shard_map/qhd,kd->hqk/dot_general | solution.py:73
  148.9 0.0 copy-done.5
  148.9 9.9 %fusion.16 = bf16[8192,128]{0,1:T(8,128)(2,1)S(1)} fusion(bf16[7,128,8192]{1,2,0:T(8,128)(2,1)} %fusion.1, bf16[128,7,128]{0,2,1:T(8,128)(2,1)S(1)} %bitcast.114), kind=kOutput, calls=%fused_computation.20 | convolution fusion | flops 1881145344 | bytes 17006592 | tf_op jit(solution)/shard_map/hqk,qhd->kd/dot_general | solution.py:82
  158.8 0.0 copy-start.6
  158.8 2.4 pad_maximum_fusion
  161.2 0.0 reduce-scatter.2.cloned.1.call-update
  161.2 0.0 copy-done.6
  161.3 56.8 %reduce-scatter.2.cloned.1.call-done = bf16[1024,256]{0,1:T(8,128)(2,1)} async-done(((bf16[8192,256]{0,1:T(8,128)(2,1)}), bf16[1024,256]{0,1:T(8,128)(2,1)}) %reduce-scatter.2.cloned.1.call-update) | async-done | bytes 524304 | tf_op jit(solution)/shard_map/reduce_scatter | solution.py:88
  218.1 1.9 copy_bitcast_fusion
  220.0 7.1 %all-to-all-start.1 = ((bf16[8,128,256]{1,2,0:T(8,128)(2,1)}), bf16[8,128,256]{1,2,0:T(8,128)(2,1)S(1)}, u32[]{:S(2)}, u32[]{:S(2)}) async-start(bf16[8,128,256]{1,2,0:T(8,128)(2,1)} %copy_bitcast_fusion), calls=%async_computation.2 | async-start | bytes 1048576 | tf_op jit(solution)/shard_map/all_to_all | solution.py:94
  227.1 8.2 %fusion.20 = bf16[128,7,128]{2,0,1:T(8,128)(2,1)S(1)} fusion(bf16[7,128,8192]{1,2,0:T(8,128)(2,1)} %fusion.1, bf16[8192,256]{1,0:T(8,128)(2,1)} %all-gather.3.cloned.1.call-done), kind=kOutput, calls=%fused_computation.30 | convolution fusion | flops 1879277568 | bytes 17006592 | tf_op jit(solution)/shard_map/hqk,kd->qhd/dot_general | solution.py:78
  235.3 0.0 copy-start.7
  235.3 0.2 copy.56
  235.5 0.6 gather_fusion
  236.1 8.9 %all-to-all-done.1 = bf16[8,128,256]{1,2,0:T(8,128)(2,1)S(1)} async-done(((bf16[8,128,256]{1,2,0:T(8,128)(2,1)}), bf16[8,128,256]{1,2,0:T(8,128)(2,1)S(1)}, u32[]{:S(2)}, u32[]{:S(2)}) %all-to-all-start.1) | async-done | bytes 524320 | tf_op jit(solution)/shard_map/all_to_all | solution.py:94
  245.1 0.1 reduce
  245.2 0.1 copy.67
  245.3 0.0 copy-start.2
  245.3 0.1 copy.68
  245.4 0.0 copy-start.3
  245.4 0.6 gather_fusion.2
  246.0 0.6 gather_fusion.1
  246.6 13.8 %all-gather = bf16[256,1152]{1,0:T(8,128)(2,1)S(1)} all-gather(bf16[32,1152]{1,0:T(8,128)(2,1)S(1)} %pad_maximum_fusion.1), channel_id=2, replica_groups=mesh['cz'=8,'cy'=8,'section'=2,'dp'=4] {'section','dp'}, dimensions={0}, use_global_device_ids=true | all-gather | bytes 663552 | tf_op jit(solution)/shard_map/all_gather | solution.py:106
  260.4 0.6 copy.57
  261.1 0.1 copy.70
  261.1 0.0 copy-done
  261.1 4.2 %convolution_convert_fusion = bf16[128,2560]{1,0:T(8,128)(2,1)} fusion(bf16[448,2560]{1,0:T(8,128)(2,1)S(1)} %copy-done, bf16[128,2304]{1,0:T(8,128)(2,1)S(1)} %bitcast.106, bf16[2304,448]{0,1:T(8,128)(2,1)} %param.18), kind=kOutput, calls=%fused_computation.23 | convolution fusion | flops 558227456 | bytes 5603328 | tf_op jit(solution)/shard_map/dot_general | solution.py:120
  265.4 3.8 %all-to-all-start.2 = ((bf16[8,16,2560]{2,1,0:T(8,128)(2,1)}), bf16[8,16,2560]{2,1,0:T(8,128)(2,1)S(1)}, u32[]{:S(2)}, u32[]{:S(2)}) async-start(bf16[8,16,2560]{2,1,0:T(8,128)(2,1)} %bitcast.103), calls=%async_computation.3 | async-start | bytes 1310720 | tf_op jit(solution)/shard_map/all_to_all | solution.py:119
  269.2 0.0 copy-done.7
  269.2 10.9 %all-to-all-done.2 = bf16[8,16,2560]{2,1,0:T(8,128)(2,1)S(1)} async-done(((bf16[8,16,2560]{2,1,0:T(8,128)(2,1)}), bf16[8,16,2560]{2,1,0:T(8,128)(2,1)S(1)}, u32[]{:S(2)}, u32[]{:S(2)}) %all-to-all-start.2) | async-done | bytes 655392 | tf_op jit(solution)/shard_map/all_to_all | solution.py:119
  280.1 0.1 convert_reduce_fusion
  280.2 0.1 reshape.222
  280.2 1.3 gather_fusion.3
  281.6 0.0 copy-done.2
  281.6 0.0 copy-done.3
  (9 shorter events, 0.1 us)
Async XLA Ops:
  7.2 254.0 %copy-start = (bf16[448,2560]{1,0:T(8,128)(2,1)S(1)}, bf16[448,2560]{1,0:T(8,128)(2,1)}, u32[]{:S(2)}) copy-start(bf16[448,2560]{1,0:T(8,128)(2,1)} %param.19) | copy-start | bytes 6881284
  7.2 83.1 %all-gather.3.cloned.1.call-start = ((), (), s32[]{:S(2)}) async-start(), calls=%async_computation.4 | async-start | bytes 4718592 | tf_op jit(solution)/shard_map/all_gather | solution.py:42
  35.0 183.1 %reduce-scatter.2.cloned.1.call-start = ((), (), s32[]{:S(2)}) async-start(), calls=%async_computation.5 | async-start | bytes 4718592 | tf_op jit(solution)/shard_map/reduce_scatter | solution.py:88
  103.4 12.7 %copy-start.4 = (bf16[1,128,896]{1,2,0:T(8,128)(2,1)S(1)}, bf16[1,128,896]{1,2,0:T(8,128)(2,1)}, u32[]{:S(2)}) copy-start(bf16[1,128,896]{1,2,0:T(8,128)(2,1)} %copy.46) | copy-start | bytes 688132
  116.1 13.4 %copy-start.1 = (bf16[8192,256]{1,0:T(8,128)(2,1)S(1)}, bf16[8192,256]{1,0:T(8,128)(2,1)}, u32[]{:S(2)}) copy-start(bf16[8192,256]{1,0:T(8,128)(2,1)} %all-gather.3.cloned.1.call-done) | copy-start | bytes 12582916
  129.5 19.4 %copy-start.5 = (bf16[1,128,896]{1,2,0:T(8,128)(2,1)S(1)}, bf16[1,128,896]{1,2,0:T(8,128)(2,1)}, u32[]{:S(2)}) copy-start(bf16[1,128,896]{1,2,0:T(8,128)(2,1)} %copy.44) | copy-start | bytes 688132
  158.8 2.4 copy-start.6
  220.0 25.1 %all-to-all-start.1 = ((bf16[8,128,256]{1,2,0:T(8,128)(2,1)}), bf16[8,128,256]{1,2,0:T(8,128)(2,1)S(1)}, u32[]{:S(2)}, u32[]{:S(2)}) async-start(bf16[8,128,256]{1,2,0:T(8,128)(2,1)} %copy_bitcast_fusion), calls=%async_computation.2 | async-start | bytes 1048576 | tf_op jit(solution)/shard_map/all_to_all | solution.py:94
  235.3 33.9 %copy-start.7 = (s32[1,1,64]{2,1,0:T(1,128)S(1)}, s32[1,1,64]{2,1,0:T(1,128)}, u32[]{:S(2)}) copy-start(s32[1,1,64]{2,1,0:T(1,128)} %param.17) | copy-start | bytes 772
  245.3 36.3 %copy-start.2 = (bf16[128,128]{1,0:T(8,128)(2,1)}, bf16[128,128]{1,0:T(8,128)(2,1)S(1)}, u32[]{:S(2)}) copy-start(bf16[128,128]{1,0:T(8,128)(2,1)S(1)} %copy.67) | copy-start | bytes 98308
  245.4 36.2 %copy-start.3 = (bf16[128,128]{1,0:T(8,128)(2,1)}, bf16[128,128]{1,0:T(8,128)(2,1)S(1)}, u32[]{:S(2)}) copy-start(bf16[128,128]{1,0:T(8,128)(2,1)S(1)} %copy.68) | copy-start | bytes 98308
  265.4 14.7 %all-to-all-start.2 = ((bf16[8,16,2560]{2,1,0:T(8,128)(2,1)}), bf16[8,16,2560]{2,1,0:T(8,128)(2,1)S(1)}, u32[]{:S(2)}, u32[]{:S(2)}) async-start(bf16[8,16,2560]{2,1,0:T(8,128)(2,1)} %bitcast.103), calls=%async_computation.3 | async-start | bytes 1310720 | tf_op jit(solution)/shard_map/all_to_all | solution.py:119
Sparse Core Ops, SparseCore 0:
  35.1 55.0 all-gather.2
  161.4 56.6 reduce-scatter.1

commit v7 on v6

--- a/solution.py
+++ b/solution.py
@@ -3,6 +3,8 @@
 import jax
 import jax.numpy as jnp
 from jax import lax
+from jax.experimental import pallas as pl
+from jax.experimental.pallas import tpu as pltpu
 from jax.sharding import PartitionSpec as P
 
 HEAD_DIM = 128
@@ -10,6 +12,89 @@
 
 
 MASKED = -1e30
+KEY_TILE = 512
+INTERPRET = False
+
+
+def backward_kernel(
+    q_ref, g_ref, dots_ref, qpos_ref, qframe_ref, kv_ref, kpos_ref, kframe_ref, dq_ref, dkv_ref
+):
+    rows = q_ref.shape[0]
+    tiles = kpos_ref.shape[0]
+    scale_factor = 1.0 / math.sqrt(HEAD_DIM)
+    query_block = q_ref[...]
+    grad_block = g_ref[...]
+    qpos = qpos_ref[...]
+    qframe = qframe_ref[...]
+
+    def allowed_at(tile):
+        kpos = kpos_ref[pl.ds(tile, 1), :]
+        kframe = kframe_ref[pl.ds(tile, 1), :]
+        return (kpos <= qpos) | (kframe == qframe)
+
+    def scores_at(tile):
+        start = pl.multiple_of(tile * KEY_TILE, KEY_TILE)
+        keys = kv_ref[pl.ds(start, KEY_TILE), pl.ds(0, HEAD_DIM)]
+        return (
+            lax.dot_general(
+                query_block, keys, (((1,), (1,)), ((), ())), preferred_element_type=jnp.float32
+            )
+            * scale_factor
+        )
+
+    def statistics(tile, carried):
+        running, summed = carried
+        scores = jnp.where(allowed_at(tile), scores_at(tile), MASKED)
+        newest = jnp.maximum(running, scores.max(axis=1, keepdims=True))
+        summed = summed * jnp.exp(running - newest) + jnp.exp(scores - newest).sum(
+            axis=1, keepdims=True
+        )
+        return (newest, summed)
+
+    running, summed = lax.fori_loop(
+        0,
+        tiles,
+        statistics,
+        (jnp.full((rows, 1), MASKED, jnp.float32), jnp.zeros((rows, 1), jnp.float32)),
+    )
+    log_total = running + jnp.log(summed)
+    dots = dots_ref[...]
+
+    def gradients(tile, query_now):
+        start = pl.multiple_of(tile * KEY_TILE, KEY_TILE)
+        keys = kv_ref[pl.ds(start, KEY_TILE), pl.ds(0, HEAD_DIM)]
+        values = kv_ref[pl.ds(start, KEY_TILE), pl.ds(HEAD_DIM, HEAD_DIM)]
+        probability = jnp.exp(jnp.where(allowed_at(tile), scores_at(tile) - log_total, MASKED))
+        grad_probs = lax.dot_general(
+            grad_block, values, (((1,), (1,)), ((), ())), preferred_element_type=jnp.float32
+        )
+        grad_scores = (probability * (grad_probs - dots)).astype(jnp.bfloat16)
+        key_part = (
+            jnp.dot(grad_scores.T, query_block, preferred_element_type=jnp.float32) * scale_factor
+        )
+        value_part = jnp.dot(
+            probability.astype(jnp.bfloat16).T, grad_block, preferred_element_type=jnp.float32
+        )
+        dkv_ref[pl.ds(start, KEY_TILE), pl.ds(0, HEAD_DIM)] = key_part.astype(dkv_ref.dtype)
+        dkv_ref[pl.ds(start, KEY_TILE), pl.ds(HEAD_DIM, HEAD_DIM)] = value_part.astype(
+            dkv_ref.dtype
+        )
+        return query_now + jnp.dot(grad_scores, keys, preferred_element_type=jnp.float32)
+
+    query_now = lax.fori_loop(0, tiles, gradients, jnp.zeros((rows, HEAD_DIM), jnp.float32))
+    dq_ref[...] = query_now * scale_factor
+
+
+def attention_backward(q2, g2, dots2, qpos2, qframe2, kv, kpos2, kframe2):
+    rows = q2.shape[0]
+    return pl.pallas_call(
+        backward_kernel,
+        out_shape=(
+            jax.ShapeDtypeStruct((rows, HEAD_DIM), jnp.float32),
+            jax.ShapeDtypeStruct(kv.shape, jnp.bfloat16),
+        ),
+        interpret=INTERPRET,
+    )(q2, g2, dots2, qpos2, qframe2, kv, kpos2, kframe2)
 
 
 def shards(
@@ -45,8 +130,6 @@
         axis=0,
         tiled=True,
     )
-    key_all = all_pairs[:, :HEAD_DIM]
-    value_all = all_pairs[:, HEAD_DIM:]
 
     key_pos = (
         jnp.arange(seq_total, dtype=jnp.int32)
@@ -57,36 +140,26 @@
     key_frames = (
         frame_line.reshape(ring_z, ring_y, local_rows).transpose(1, 0, 2).reshape(seq_total)
     )
-    allowed = (key_pos[None, :] <= query_pos[:, None]) | (key_frames[None, :] == query_frames[:, None])
-
-    scores = (
-        jnp.einsum("qhd,kd->hqk", query_heads, key_all, preferred_element_type=jnp.float32)
-        * scale_factor
-    )
-    masked_scores = jnp.where(allowed[None], scores, MASKED)
-    running = masked_scores.max(axis=-1)
-    summed = jnp.exp(masked_scores - running[:, :, None]).sum(axis=-1)
-    log_total = running + jnp.log(summed)
-
-    probability = jnp.exp(jnp.where(allowed[None], scores - log_total[:, :, None], MASKED))
-    probs_low = probability.astype(jnp.bfloat16)
-    grad_probs = jnp.einsum(
-        "qhd,kd->hqk", grad_heads, value_all, preferred_element_type=jnp.float32
-    )
-    grad_scores = (probability * (grad_probs - corrections[:, :, None])).astype(jnp.bfloat16)
-    grad_query = (
-        jnp.einsum("hqk,kd->qhd", grad_scores, key_all, preferred_element_type=jnp.float32)
-        * scale_factor
-    )
-    key_part = (
-        jnp.einsum("hqk,qhd->kd", grad_scores, query_heads, preferred_element_type=jnp.float32)
-        * scale_factor
-    )
-    value_part = jnp.einsum(
-        "hqk,qhd->kd", probs_low, grad_heads, preferred_element_type=jnp.float32
-    )
+    rows = GROUP * local_rows
+    q2 = query_heads.transpose(1, 0, 2).reshape(rows, HEAD_DIM)
+    g2 = grad_heads.transpose(1, 0, 2).reshape(rows, HEAD_DIM)
+    dots2 = corrections.reshape(rows, 1)
+    qpos2 = jnp.tile(query_pos, GROUP).reshape(rows, 1)
+    qframe2 = jnp.tile(query_frames, GROUP).reshape(rows, 1)
+    tiles = seq_total // KEY_TILE
+    dq2, partials = attention_backward(
+        q2,
+        g2,
+        dots2,
+        qpos2,
+        qframe2,
+        all_pairs,
+        key_pos.reshape(tiles, KEY_TILE),
+        key_frames.reshape(tiles, KEY_TILE),
+    )
+    grad_query = dq2.reshape(GROUP, local_rows, HEAD_DIM).transpose(1, 0, 2)
     stage_one = lax.psum_scatter(
-        jnp.concatenate([key_part, value_part], axis=1).astype(jnp.bfloat16),
+        partials,
         "cy",
         scatter_dimension=0,
         tiled=True,

time: 289 us -> 269 us (0.931)
  matrix products: 68.2 us -> 3.76 us
  Pallas kernels: 0 us -> 53.1 us
  other arithmetic: 19.8 us -> 2.18 us
  waiting for transfers between devices: 123 us -> 132 us
    dot_general x5 -> x0, matrix products: 64 us -> none  [the longest x1 19.4 us: shards(): jnp.einsum('qhd,kd->hqk', grad_heads, value_all, preferred_element_type=j...]
    pallas_call x0 -> x1, Pallas kernels: none -> 53.1 us  [attention_backward(): pl.pallas_call(backward_kernel, out_shape=(jax.ShapeDtypeStruct((rows, HE...]
    reduce_sum x1 -> x0, other arithmetic: 12.7 us -> none  [shards(): summed = jnp.exp(masked_scores - running[:, :, None]).sum(axis=-1)]
    all_to_all x1, waiting for transfers between devices: 8.94 us -> 15.9 us  [shards(): stage_two = lax.all_to_all(stage_one, 'cz', 0, 0, tiled=True)]
  transfers between devices with their start and end apart: 4 -> 4, of which waited for: 4 -> 4; matrix products, arithmetic and copies ran while one was open for 6% -> 3% of each run, Pallas kernels for 0% -> 0%
where the time goes in v7:
time: 269 us
  waiting for transfers between devices  132 us (49%)
  Pallas kernels  53.1 us (20%)
  blocking collectives  40.7 us (15%)
  between operations  14.2 us (5%)
  local copies, waits for them, and re-layouts  11.3 us (4%)
  starting transfers between devices  11 us (4%)
  matrix products  3.76 us (1%)
    reduce_scatter x1, waiting for transfers between devices, shards(): lax.psum_scatter(partials, 'cy', scatter_dimension=0, tiled=True)  56.9 us
    pallas_call x1, Pallas kernels, attention_backward(): pl.pallas_call(backward_kernel, out_shape=(jax.ShapeDtypeStruct((rows, HE...  53.1 us
    all_gather x1, waiting for transfers between devices, shards(): lax.all_gather(lax.all_to_all(jnp.tile(own_pair, (ring_z, 1)), 'cz', 0, 0...  48.8 us
    all_to_all x1, blocking collectives, shards(): lax.all_to_all(jnp.tile(own_pair, (ring_z, 1)), 'cz', 0, 0, tiled=True)  26.9 us
    all_to_all x1, waiting for transfers between devices, shards(): stage_two = lax.all_to_all(stage_one, 'cz', 0, 0, tiled=True)  15.9 us
    all_gather x1, blocking collectives, shards(): lax.all_gather(chosen[None], ('section', 'dp'), axis=0, tiled=True)  13.8 us
    all_to_all x1, waiting for transfers between devices, shards(): lax.all_to_all(jnp.dot(visual_grad, projector_weight, preferred_element_t...  10.9 us
    all_to_all x1, starting transfers between devices, shards(): stage_two = lax.all_to_all(stage_one, 'cz', 0, 0, tiled=True)  7.1 us
  transfers between devices with their start and end apart: 4, of which 4 were waited for; matrix products, arithmetic and copies ran while one was open for 3% of the time, Pallas kernels for 0%

profile of v7, /device:TPU:1, one launch (start us, length us, event | category | flops | bytes accessed | tf_op | source)
XLA Modules:
  0.0 268.8 jit_solution(10178235353251022334)
XLA Ops:
  7.2 0.0 copy-start
  7.2 0.0 copy-start.3
  7.2 0.0 copy-start.1
  7.2 0.0 all-gather.3.cloned.1.call-start
  7.2 0.9 pad_maximum_fusion.1
  8.2 0.0 copy-start.2
  8.2 0.0 copy-start.4
  8.2 26.9 %all_to_all.27 = bf16[8,128,256]{2,1,0:T(8,128)(2,1)} all-to-all(bf16[8,128,256]{2,1,0:T(8,128)(2,1)S(1)} %tile.11), channel_id=1, replica_groups=mesh['cz'=8,'cy'=8,'section'=2,'dp'=4] {'cz'}, dimensions={0} | all-to-all | bytes 1048576 | tf_op jit(solution)/shard_map/all_to_all | solution.py:128
  35.1 0.0 all-gather.3.cloned.1.call-update
  35.2 0.0 reduce-scatter.2.cloned.1.call-start
  35.2 0.0 copy-done.3
  35.3 1.0 copy.31
  36.3 1.0 copy.29
  37.3 0.0 copy-done.1
  37.3 0.2 copy.17
  37.5 0.9 copy.18
  38.4 0.0 copy-done.2
  38.4 0.2 copy.19
  38.5 0.8 copy.20
  39.4 0.0 copy-done.4
  39.4 1.0 copy.22.dots_ref
  40.4 0.6 reshape.141.kpos_ref
  41.0 0.6 reshape_reshape.4.kframe_ref
  41.7 48.8 %all-gather.3.cloned.1.call-done.kv_ref = bf16[8192,256]{1,0:T(8,128)(2,1)} async-done(((bf16[1024,256]{1,0:T(8,128)(2,1)}), bf16[8192,256]{1,0:T(8,128)(2,1)}) %all-gather.3.cloned.1.call-update) | async-done | bytes 4194320 | tf_op jit(solution)/shard_map/all_gather | solution.py:127
  90.4 53.1 %shard_map.121 = (f32[896,128]{1,0:T(8,128)}, bf16[8192,256]{1,0:T(8,128)(2,1)}) custom-call(bf16[896,128]{1,0:T(8,128)(2,1)} %bitcast.71, bf16[896,128]{1,0:T(8,128)(2,1)} %bitcast.72, f32[896,1]{1,0:T(8,128)} %copy.22.dots_ref, s32[896,1]{1,0:T(8,128)} %bitcast.67, s32[896,1]{1,0:T(8,128)} %bitcast.66, ...), custom_call_target="tpu_custom_call" | custom-call | tf_op jit(solution)/shard_map/pallas_call | solution.py:90
  143.6 0.0 copy-start.5
  143.6 0.0 reduce-scatter.2.cloned.1.call-update
  143.6 56.9 %reduce-scatter.2.cloned.1.call-done = bf16[1024,256]{1,0:T(8,128)(2,1)} async-done(((bf16[8192,256]{1,0:T(8,128)(2,1)}), bf16[1024,256]{1,0:T(8,128)(2,1)}) %reduce-scatter.2.cloned.1.call-update) | async-done | bytes 524304 | tf_op jit(solution)/shard_map/reduce_scatter | solution.py:161
  200.5 7.1 %all-to-all-start.1 = ((bf16[8,128,256]{2,1,0:T(8,128)(2,1)}), bf16[8,128,256]{2,1,0:T(8,128)(2,1)S(1)}, u32[]{:S(2)}, u32[]{:S(2)}) async-start(bf16[8,128,256]{2,1,0:T(8,128)(2,1)} %bitcast.74), calls=%async_computation.2 | async-start | bytes 1048576 | tf_op jit(solution)/shard_map/all_to_all | solution.py:167
  207.6 0.0 copy-done.5
  207.6 1.0 convert_element_type.39
  208.7 0.2 copy.25
  208.8 0.2 copy.26
  209.0 0.6 gather_fusion
  209.6 15.9 %all-to-all-done.1 = bf16[8,128,256]{2,1,0:T(8,128)(2,1)S(1)} async-done(((bf16[8,128,256]{2,1,0:T(8,128)(2,1)}), bf16[8,128,256]{2,1,0:T(8,128)(2,1)S(1)}, u32[]{:S(2)}, u32[]{:S(2)}) %all-to-all-start.1) | async-done | bytes 524320 | tf_op jit(solution)/shard_map/all_to_all | solution.py:167
  225.5 0.1 reduce
  225.6 0.6 fusion.2
  226.2 0.6 gather_fusion.1
  226.8 0.6 gather_fusion.2
  227.4 13.8 %all-gather = bf16[256,1152]{1,0:T(8,128)(2,1)S(1)} all-gather(bf16[32,1152]{1,0:T(8,128)(2,1)S(1)} %pad_maximum_fusion), channel_id=2, replica_groups=mesh['cz'=8,'cy'=8,'section'=2,'dp'=4] {'section','dp'}, dimensions={0}, use_global_device_ids=true | all-gather | bytes 663552 | tf_op jit(solution)/shard_map/all_gather | solution.py:179
  241.2 0.6 copy.27
  241.8 0.1 copy.32
  241.9 0.0 copy-done
  241.9 0.0 copy-start.6
  241.9 3.8 %convolution_convert_fusion = bf16[128,2560]{1,0:T(8,128)(2,1)} fusion(bf16[448,2560]{1,0:T(8,128)(2,1)S(1)} %copy-done, bf16[128,2304]{1,0:T(8,128)(2,1)S(1)} %bitcast.64, bf16[2304,448]{0,1:T(8,128)(2,1)} %param.18), kind=kOutput, calls=%fused_computation.4 | convolution fusion | flops 558227456 | bytes 5603328 | tf_op jit(solution)/shard_map/dot_general | solution.py:193
  245.7 3.8 %all-to-all-start.2 = ((bf16[8,16,2560]{2,1,0:T(8,128)(2,1)}), bf16[8,16,2560]{2,1,0:T(8,128)(2,1)S(1)}, u32[]{:S(2)}, u32[]{:S(2)}) async-start(bf16[8,16,2560]{2,1,0:T(8,128)(2,1)} %bitcast.61), calls=%async_computation.3 | async-start | bytes 1310720 | tf_op jit(solution)/shard_map/all_to_all | solution.py:192
  249.5 0.0 copy-done.6
  249.6 10.9 %all-to-all-done.2 = bf16[8,16,2560]{2,1,0:T(8,128)(2,1)S(1)} async-done(((bf16[8,16,2560]{2,1,0:T(8,128)(2,1)}), bf16[8,16,2560]{2,1,0:T(8,128)(2,1)S(1)}, u32[]{:S(2)}, u32[]{:S(2)}) %all-to-all-start.2) | async-done | bytes 655392 | tf_op jit(solution)/shard_map/all_to_all | solution.py:192
  260.4 0.1 convert_reduce_fusion
  260.5 0.1 reshape.145
  260.6 1.3 gather_fusion.3
  (14 shorter events, 0.1 us)
Async XLA Ops:
  7.2 234.8 %copy-start = (bf16[448,2560]{1,0:T(8,128)(2,1)S(1)}, bf16[448,2560]{1,0:T(8,128)(2,1)}, u32[]{:S(2)}) copy-start(bf16[448,2560]{1,0:T(8,128)(2,1)} %param.19) | copy-start | bytes 6881284
  7.2 28.0 %copy-start.3 = (s32[1,8192]{1,0:T(1,128)S(1)}, s32[1,8192]{1,0:T(1,128)}, u32[]{:S(2)}) copy-start(s32[1,8192]{1,0:T(1,128)} %param.15) | copy-start | bytes 98308
  7.2 30.1 %copy-start.1 = (bf16[1,128,896]{2,1,0:T(8,128)(2,1)S(1)}, bf16[1,128,896]{2,1,0:T(8,128)(2,1)}, u32[]{:S(2)}) copy-start(bf16[1,128,896]{2,1,0:T(8,128)(2,1)} %param.10) | copy-start | bytes 688132
  7.2 83.2 %all-gather.3.cloned.1.call-start = ((), (), s32[]{:S(2)}) async-start(), calls=%async_computation.4 | async-start | bytes 4718592 | tf_op jit(solution)/shard_map/all_gather | solution.py:127
  8.2 30.2 %copy-start.2 = (bf16[1,128,896]{2,1,0:T(8,128)(2,1)S(1)}, bf16[1,128,896]{2,1,0:T(8,128)(2,1)}, u32[]{:S(2)}) copy-start(bf16[1,128,896]{2,1,0:T(8,128)(2,1)} %param.13) | copy-start | bytes 688132
  8.2 31.1 %copy-start.4 = (f32[1,7,128]{2,0,1:T(1,128)S(1)}, f32[1,7,128]{2,0,1:T(1,128)}, u32[]{:S(2)}) copy-start(f32[1,7,128]{2,0,1:T(1,128)} %param.14) | copy-start | bytes 10756
  35.2 165.3 %reduce-scatter.2.cloned.1.call-start = ((), (), s32[]{:S(2)}) async-start(), calls=%async_computation.5 | async-start | bytes 4718592 | tf_op jit(solution)/shard_map/reduce_scatter | solution.py:161
  143.6 64.0 %copy-start.5 = (s32[1,1,32]{2,1,0:T(1,128)S(1)}, s32[1,1,32]{2,1,0:T(1,128)}, u32[]{:S(2)}) copy-start(s32[1,1,32]{2,1,0:T(1,128)} %param.16) | copy-start | bytes 388
  200.5 25.1 %all-to-all-start.1 = ((bf16[8,128,256]{2,1,0:T(8,128)(2,1)}), bf16[8,128,256]{2,1,0:T(8,128)(2,1)S(1)}, u32[]{:S(2)}, u32[]{:S(2)}) async-start(bf16[8,128,256]{2,1,0:T(8,128)(2,1)} %bitcast.74), calls=%async_computation.2 | async-start | bytes 1048576 | tf_op jit(solution)/shard_map/all_to_all | solution.py:167
  241.9 7.6 %copy-start.6 = (s32[1,1,64]{2,1,0:T(1,128)S(1)}, s32[1,1,64]{2,1,0:T(1,128)}, u32[]{:S(2)}) copy-start(s32[1,1,64]{2,1,0:T(1,128)} %param.17) | copy-start | bytes 772
  245.7 14.7 %all-to-all-start.2 = ((bf16[8,16,2560]{2,1,0:T(8,128)(2,1)}), bf16[8,16,2560]{2,1,0:T(8,128)(2,1)S(1)}, u32[]{:S(2)}, u32[]{:S(2)}) async-start(bf16[8,16,2560]{2,1,0:T(8,128)(2,1)} %bitcast.61), calls=%async_computation.3 | async-start | bytes 1310720 | tf_op jit(solution)/shard_map/all_to_all | solution.py:192
Sparse Core Ops, SparseCore 0:
  35.3 55.0 all-gather.2
  143.7 56.7 reduce-scatter.1

commit v8 on v7

--- a/solution.py
+++ b/solution.py
@@ -20,6 +20,8 @@
     q_ref, g_ref, dots_ref, qpos_ref, qframe_ref, kv_ref, kpos_ref, kframe_ref, dq_ref, dkv_ref
 ):
     rows = q_ref.shape[0]
+    local_rows = qpos_ref.shape[0]
+    heads = rows // local_rows
     tiles = kpos_ref.shape[0]
     scale_factor = 1.0 / math.sqrt(HEAD_DIM)
     query_block = q_ref[...]
@@ -30,24 +32,25 @@
     def allowed_at(tile):
         kpos = kpos_ref[pl.ds(tile, 1), :]
         kframe = kframe_ref[pl.ds(tile, 1), :]
-        return (kpos <= qpos) | (kframe == qframe)
+        return ((kpos <= qpos) | (kframe == qframe))[None]
 
     def scores_at(tile):
         start = pl.multiple_of(tile * KEY_TILE, KEY_TILE)
         keys = kv_ref[pl.ds(start, KEY_TILE), pl.ds(0, HEAD_DIM)]
-        return (
+        scores = (
             lax.dot_general(
                 query_block, keys, (((1,), (1,)), ((), ())), preferred_element_type=jnp.float32
             )
             * scale_factor
         )
+        return scores.reshape(heads, local_rows, KEY_TILE)
 
     def statistics(tile, carried):
         running, summed = carried
         scores = jnp.where(allowed_at(tile), scores_at(tile), MASKED)
-        newest = jnp.maximum(running, scores.max(axis=1, keepdims=True))
+        newest = jnp.maximum(running, scores.max(axis=2, keepdims=True))
         summed = summed * jnp.exp(running - newest) + jnp.exp(scores - newest).sum(
-            axis=1, keepdims=True
+            axis=2, keepdims=True
         )
         return (newest, summed)
 
@@ -55,10 +58,13 @@
         0,
         tiles,
         statistics,
-        (jnp.full((rows, 1), MASKED, jnp.float32), jnp.zeros((rows, 1), jnp.float32)),
+        (
+            jnp.full((heads, local_rows, 1), MASKED, jnp.float32),
+            jnp.zeros((heads, local_rows, 1), jnp.float32),
+        ),
     )
     log_total = running + jnp.log(summed)
-    dots = dots_ref[...]
+    dots = dots_ref[...].reshape(heads, local_rows, 1)
 
     def gradients(tile, query_now):
         start = pl.multiple_of(tile * KEY_TILE, KEY_TILE)
@@ -67,14 +73,15 @@
         probability = jnp.exp(jnp.where(allowed_at(tile), scores_at(tile) - log_total, MASKED))
         grad_probs = lax.dot_general(
             grad_block, values, (((1,), (1,)), ((), ())), preferred_element_type=jnp.float32
-        )
-        grad_scores = (probability * (grad_probs - dots)).astype(jnp.bfloat16)
+        ).reshape(heads, local_rows, KEY_TILE)
+        grad_scores = (
+            (probability * (grad_probs - dots)).astype(jnp.bfloat16).reshape(rows, KEY_TILE)
+        )
+        probs_low = probability.astype(jnp.bfloat16).reshape(rows, KEY_TILE)
         key_part = (
             jnp.dot(grad_scores.T, query_block, preferred_element_type=jnp.float32) * scale_factor
         )
-        value_part = jnp.dot(
-            probability.astype(jnp.bfloat16).T, grad_block, preferred_element_type=jnp.float32
-        )
+        value_part = jnp.dot(probs_low.T, grad_block, preferred_element_type=jnp.float32)
         dkv_ref[pl.ds(start, KEY_TILE), pl.ds(0, HEAD_DIM)] = key_part.astype(dkv_ref.dtype)
         dkv_ref[pl.ds(start, KEY_TILE), pl.ds(HEAD_DIM, HEAD_DIM)] = value_part.astype(
             dkv_ref.dtype
@@ -144,8 +151,8 @@
     q2 = query_heads.transpose(1, 0, 2).reshape(rows, HEAD_DIM)
     g2 = grad_heads.transpose(1, 0, 2).reshape(rows, HEAD_DIM)
     dots2 = corrections.reshape(rows, 1)
-    qpos2 = jnp.tile(query_pos, GROUP).reshape(rows, 1)
-    qframe2 = jnp.tile(query_frames, GROUP).reshape(rows, 1)
+    qpos2 = query_pos.reshape(local_rows, 1)
+    qframe2 = query_frames.reshape(local_rows, 1)
     tiles = seq_total // KEY_TILE
     dq2, partials = attention_backward(
         q2,

time: 269 us -> 263 us (0.978)
  Pallas kernels: 53.1 us -> 47.5 us
    pallas_call x1, Pallas kernels: 53.1 us -> 47.5 us  [attention_backward(): pl.pallas_call(backward_kernel, out_shape=(jax.ShapeDtypeStruct((rows, HE...]
where the time goes in v8:
time: 263 us
  waiting for transfers between devices  133 us (51%)
  Pallas kernels  47.5 us (18%)
  blocking collectives  40.6 us (15%)
  between operations  14.2 us (5%)
  starting transfers between devices  11 us (4%)
  local copies, waits for them, and re-layouts  9.99 us (4%)
  matrix products  3.76 us (1%)
  other arithmetic  2.81 us (1%)
    reduce_scatter x1, waiting for transfers between devices, shards(): lax.psum_scatter(partials, 'cy', scatter_dimension=0, tiled=True)  56.9 us
    all_gather x1, waiting for transfers between devices, shards(): lax.all_gather(lax.all_to_all(jnp.tile(own_pair, (ring_z, 1)), 'cz', 0, 0...  49.5 us
    pallas_call x1, Pallas kernels, attention_backward(): pl.pallas_call(backward_kernel, out_shape=(jax.ShapeDtypeStruct((rows, HE...  47.5 us
    all_to_all x1, blocking collectives, shards(): lax.all_to_all(jnp.tile(own_pair, (ring_z, 1)), 'cz', 0, 0, tiled=True)  26.8 us
    all_to_all x1, waiting for transfers between devices, shards(): stage_two = lax.all_to_all(stage_one, 'cz', 0, 0, tiled=True)  15.9 us
    all_gather x1, blocking collectives, shards(): lax.all_gather(chosen[None], ('section', 'dp'), axis=0, tiled=True)  13.8 us
    all_to_all x1, waiting for transfers between devices, shards(): lax.all_to_all(jnp.dot(visual_grad, projector_weight, preferred_element_t...  10.9 us
    all_to_all x1, starting transfers between devices, shards(): stage_two = lax.all_to_all(stage_one, 'cz', 0, 0, tiled=True)  7.1 us
  transfers between devices with their start and end apart: 4, of which 4 were waited for; matrix products, arithmetic and copies ran while one was open for 3% of the time, Pallas kernels for 0%

profile of v8, /device:TPU:1, one launch (start us, length us, event | category | flops | bytes accessed | tf_op | source)
XLA Modules:
  0.0 263.0 jit_solution(17022596255141335099)
XLA Ops:
  7.2 0.0 copy-start
  7.2 0.0 copy-start.3
  7.2 0.0 copy-start.1
  7.2 0.0 copy-start.2
  7.2 0.0 all-gather.3.cloned.1.call-start
  7.3 0.9 pad_maximum_fusion.1
  8.2 0.0 copy-start.4
  8.2 26.8 %all_to_all.27 = bf16[8,128,256]{2,1,0:T(8,128)(2,1)} all-to-all(bf16[8,128,256]{2,1,0:T(8,128)(2,1)S(1)} %tile.2), channel_id=1, replica_groups=mesh['cz'=8,'cy'=8,'section'=2,'dp'=4] {'cz'}, dimensions={0} | all-to-all | bytes 1048576 | tf_op jit(solution)/shard_map/all_to_all | solution.py:135
  35.0 0.0 all-gather.3.cloned.1.call-update
  35.0 0.0 reduce-scatter.2.cloned.1.call-start
  35.1 0.0 copy-done.3
  35.1 0.7 copy.24.qframe_ref
  35.8 0.0 copy-done.1
  35.8 0.2 copy.18
  36.0 0.8 copy.19
  36.9 0.0 copy-done.2
  36.9 0.2 copy.20
  37.0 0.8 copy.21
  37.9 0.0 copy-done.4
  37.9 1.0 copy.23.dots_ref
  38.9 0.6 reshape.149.kpos_ref
  39.5 0.6 reshape_reshape.4.kframe_ref
  40.2 0.6 iota_add_fusion.qpos_ref
  40.8 49.5 %all-gather.3.cloned.1.call-done.kv_ref = bf16[8192,256]{1,0:T(8,128)(2,1)} async-done(((bf16[1024,256]{1,0:T(8,128)(2,1)}), bf16[8192,256]{1,0:T(8,128)(2,1)}) %all-gather.3.cloned.1.call-update) | async-done | bytes 4194320 | tf_op jit(solution)/shard_map/all_gather | solution.py:134
  90.3 47.5 %shard_map.121 = (f32[896,128]{1,0:T(8,128)}, bf16[8192,256]{1,0:T(8,128)(2,1)}) custom-call(bf16[896,128]{1,0:T(8,128)(2,1)} %bitcast.56, bf16[896,128]{1,0:T(8,128)(2,1)} %bitcast.57, f32[896,1]{1,0:T(8,128)} %copy.23.dots_ref, s32[128,1]{1,0:T(8,128)} %iota_add_fusion.qpos_ref, s32[128,1]{1,0:T(8,128)} %copy.24.qframe_ref, ...), custom_call_target="tpu_custom_call" | custom-call | tf_op jit(solution)/shard_map/pallas_call | solution.py:97
  137.8 0.0 copy-start.5
  137.8 0.0 reduce-scatter.2.cloned.1.call-update
  137.8 56.9 %reduce-scatter.2.cloned.1.call-done = bf16[1024,256]{1,0:T(8,128)(2,1)} async-done(((bf16[8192,256]{1,0:T(8,128)(2,1)}), bf16[1024,256]{1,0:T(8,128)(2,1)}) %reduce-scatter.2.cloned.1.call-update) | async-done | bytes 524304 | tf_op jit(solution)/shard_map/reduce_scatter | solution.py:168
  194.7 7.1 %all-to-all-start.1 = ((bf16[8,128,256]{2,1,0:T(8,128)(2,1)}), bf16[8,128,256]{2,1,0:T(8,128)(2,1)S(1)}, u32[]{:S(2)}, u32[]{:S(2)}) async-start(bf16[8,128,256]{2,1,0:T(8,128)(2,1)} %bitcast.58), calls=%async_computation.2 | async-start | bytes 1048576 | tf_op jit(solution)/shard_map/all_to_all | solution.py:174
  201.8 0.0 copy-done.5
  201.8 1.0 convert_element_type.39
  202.9 0.2 copy.25
  203.0 0.2 copy.26
  203.2 0.6 gather_fusion
  203.8 15.9 %all-to-all-done.1 = bf16[8,128,256]{2,1,0:T(8,128)(2,1)S(1)} async-done(((bf16[8,128,256]{2,1,0:T(8,128)(2,1)}), bf16[8,128,256]{2,1,0:T(8,128)(2,1)S(1)}, u32[]{:S(2)}, u32[]{:S(2)}) %all-to-all-start.1) | async-done | bytes 524320 | tf_op jit(solution)/shard_map/all_to_all | solution.py:174
  219.7 0.1 reduce
  219.8 0.6 fusion.2
  220.5 0.6 gather_fusion.1
  221.0 0.6 gather_fusion.2
  221.7 13.8 %all-gather = bf16[256,1152]{1,0:T(8,128)(2,1)S(1)} all-gather(bf16[32,1152]{1,0:T(8,128)(2,1)S(1)} %pad_maximum_fusion), channel_id=2, replica_groups=mesh['cz'=8,'cy'=8,'section'=2,'dp'=4] {'section','dp'}, dimensions={0}, use_global_device_ids=true | all-gather | bytes 663552 | tf_op jit(solution)/shard_map/all_gather | solution.py:186
  235.5 0.6 copy.27
  236.1 0.1 copy.28
  236.2 0.0 copy-done
  236.2 0.0 copy-start.6
  236.2 3.8 %convolution_convert_fusion = bf16[128,2560]{1,0:T(8,128)(2,1)} fusion(bf16[448,2560]{1,0:T(8,128)(2,1)S(1)} %copy-done, bf16[128,2304]{1,0:T(8,128)(2,1)S(1)} %bitcast.50, bf16[2304,448]{0,1:T(8,128)(2,1)} %param.18), kind=kOutput, calls=%fused_computation.4 | convolution fusion | flops 558227456 | bytes 5603328 | tf_op jit(solution)/shard_map/dot_general | solution.py:200
  239.9 3.8 %all-to-all-start.2 = ((bf16[8,16,2560]{2,1,0:T(8,128)(2,1)}), bf16[8,16,2560]{2,1,0:T(8,128)(2,1)S(1)}, u32[]{:S(2)}, u32[]{:S(2)}) async-start(bf16[8,16,2560]{2,1,0:T(8,128)(2,1)} %bitcast.47), calls=%async_computation.3 | async-start | bytes 1310720 | tf_op jit(solution)/shard_map/all_to_all | solution.py:199
  243.8 0.0 copy-done.6
  243.8 10.9 %all-to-all-done.2 = bf16[8,16,2560]{2,1,0:T(8,128)(2,1)S(1)} async-done(((bf16[8,16,2560]{2,1,0:T(8,128)(2,1)}), bf16[8,16,2560]{2,1,0:T(8,128)(2,1)S(1)}, u32[]{:S(2)}, u32[]{:S(2)}) %all-to-all-start.2) | async-done | bytes 655392 | tf_op jit(solution)/shard_map/all_to_all | solution.py:199
  254.6 0.1 convert_reduce_fusion
  254.7 0.1 reshape.153
  254.8 1.3 gather_fusion.3
  (9 shorter events, 0.1 us)
Async XLA Ops:
  7.2 229.0 %copy-start = (bf16[448,2560]{1,0:T(8,128)(2,1)S(1)}, bf16[448,2560]{1,0:T(8,128)(2,1)}, u32[]{:S(2)}) copy-start(bf16[448,2560]{1,0:T(8,128)(2,1)} %param.19) | copy-start | bytes 6881284
  7.2 27.9 %copy-start.3 = (s32[1,8192]{1,0:T(1,128)S(1)}, s32[1,8192]{1,0:T(1,128)}, u32[]{:S(2)}) copy-start(s32[1,8192]{1,0:T(1,128)} %param.15) | copy-start | bytes 98308
  7.2 28.7 %copy-start.1 = (bf16[1,128,896]{2,1,0:T(8,128)(2,1)S(1)}, bf16[1,128,896]{2,1,0:T(8,128)(2,1)}, u32[]{:S(2)}) copy-start(bf16[1,128,896]{2,1,0:T(8,128)(2,1)} %param.10) | copy-start | bytes 688132
  7.2 29.7 %copy-start.2 = (bf16[1,128,896]{2,1,0:T(8,128)(2,1)S(1)}, bf16[1,128,896]{2,1,0:T(8,128)(2,1)}, u32[]{:S(2)}) copy-start(bf16[1,128,896]{2,1,0:T(8,128)(2,1)} %param.13) | copy-start | bytes 688132
  7.2 83.1 %all-gather.3.cloned.1.call-start = ((), (), s32[]{:S(2)}) async-start(), calls=%async_computation.4 | async-start | bytes 4718592 | tf_op jit(solution)/shard_map/all_gather | solution.py:134
  8.2 29.7 %copy-start.4 = (f32[1,7,128]{2,0,1:T(1,128)S(1)}, f32[1,7,128]{2,0,1:T(1,128)}, u32[]{:S(2)}) copy-start(f32[1,7,128]{2,0,1:T(1,128)} %param.14) | copy-start | bytes 10756
  35.0 159.7 %reduce-scatter.2.cloned.1.call-start = ((), (), s32[]{:S(2)}) async-start(), calls=%async_computation.5 | async-start | bytes 4718592 | tf_op jit(solution)/shard_map/reduce_scatter | solution.py:168
  137.8 64.0 %copy-start.5 = (s32[1,1,32]{2,1,0:T(1,128)S(1)}, s32[1,1,32]{2,1,0:T(1,128)}, u32[]{:S(2)}) copy-start(s32[1,1,32]{2,1,0:T(1,128)} %param.16) | copy-start | bytes 388
  194.7 25.1 %all-to-all-start.1 = ((bf16[8,128,256]{2,1,0:T(8,128)(2,1)}), bf16[8,128,256]{2,1,0:T(8,128)(2,1)S(1)}, u32[]{:S(2)}, u32[]{:S(2)}) async-start(bf16[8,128,256]{2,1,0:T(8,128)(2,1)} %bitcast.58), calls=%async_computation.2 | async-start | bytes 1048576 | tf_op jit(solution)/shard_map/all_to_all | solution.py:174
  236.2 7.6 %copy-start.6 = (s32[1,1,64]{2,1,0:T(1,128)S(1)}, s32[1,1,64]{2,1,0:T(1,128)}, u32[]{:S(2)}) copy-start(s32[1,1,64]{2,1,0:T(1,128)} %param.17) | copy-start | bytes 772
  239.9 14.7 %all-to-all-start.2 = ((bf16[8,16,2560]{2,1,0:T(8,128)(2,1)}), bf16[8,16,2560]{2,1,0:T(8,128)(2,1)S(1)}, u32[]{:S(2)}, u32[]{:S(2)}) async-start(bf16[8,16,2560]{2,1,0:T(8,128)(2,1)} %bitcast.47), calls=%async_computation.3 | async-start | bytes 1310720 | tf_op jit(solution)/shard_map/all_to_all | solution.py:199
Sparse Core Ops, SparseCore 0:
  35.1 55.0 all-gather.2
  137.9 56.6 reduce-scatter.1

commit v9 on v8

--- a/solution.py
+++ b/solution.py
@@ -12,7 +12,7 @@
 
 
 MASKED = -1e30
-KEY_TILE = 512
+KEY_TILE = 2048
 INTERPRET = False
 
 

time: 263 us -> 255 us (0.970)
  Pallas kernels: 47.5 us -> 39.2 us
    pallas_call x1, Pallas kernels: 47.5 us -> 39.2 us  [attention_backward(): pl.pallas_call(backward_kernel, out_shape=(jax.ShapeDtypeStruct((rows, HE...]
where the time goes in v9:
time: 255 us
  waiting for transfers between devices  133 us (52%)
  blocking collectives  40.8 us (16%)
  Pallas kernels  39.2 us (15%)
  between operations  14.2 us (6%)
  starting transfers between devices  11 us (4%)
  local copies, waits for them, and re-layouts  10 us (4%)
  matrix products  3.76 us (1%)
  other arithmetic  2.81 us (1%)
    reduce_scatter x1, waiting for transfers between devices, shards(): lax.psum_scatter(partials, 'cy', scatter_dimension=0, tiled=True)  56.9 us
    all_gather x1, waiting for transfers between devices, shards(): lax.all_gather(lax.all_to_all(jnp.tile(own_pair, (ring_z, 1)), 'cz', 0, 0...  49.5 us
    pallas_call x1, Pallas kernels, attention_backward(): pl.pallas_call(backward_kernel, out_shape=(jax.ShapeDtypeStruct((rows, HE...  39.2 us
    all_to_all x1, blocking collectives, shards(): lax.all_to_all(jnp.tile(own_pair, (ring_z, 1)), 'cz', 0, 0, tiled=True)  26.8 us
    all_to_all x1, waiting for transfers between devices, shards(): stage_two = lax.all_to_all(stage_one, 'cz', 0, 0, tiled=True)  15.9 us
    all_gather x1, blocking collectives, shards(): lax.all_gather(chosen[None], ('section', 'dp'), axis=0, tiled=True)  14 us
    all_to_all x1, waiting for transfers between devices, shards(): lax.all_to_all(jnp.dot(visual_grad, projector_weight, preferred_element_t...  10.9 us
    all_to_all x1, starting transfers between devices, shards(): stage_two = lax.all_to_all(stage_one, 'cz', 0, 0, tiled=True)  7.1 us
  transfers between devices with their start and end apart: 4, of which 4 were waited for; matrix products, arithmetic and copies ran while one was open for 3% of the time, Pallas kernels for 0%

profile of v9, /device:TPU:1, one launch (start us, length us, event | category | flops | bytes accessed | tf_op | source)
XLA Modules:
  0.0 254.9 jit_solution(8033404364214792208)
XLA Ops:
  7.2 0.0 copy-start
  7.2 0.0 copy-start.3
  7.2 0.0 copy-start.1
  7.2 0.0 copy-start.2
  7.2 0.0 all-gather.3.cloned.1.call-start
  7.3 0.9 pad_maximum_fusion.1
  8.2 0.0 copy-start.4
  8.2 26.8 %all_to_all.27 = bf16[8,128,256]{2,1,0:T(8,128)(2,1)} all-to-all(bf16[8,128,256]{2,1,0:T(8,128)(2,1)S(1)} %tile.2), channel_id=1, replica_groups=mesh['cz'=8,'cy'=8,'section'=2,'dp'=4] {'cz'}, dimensions={0} | all-to-all | bytes 1048576 | tf_op jit(solution)/shard_map/all_to_all | solution.py:135
  35.0 0.0 all-gather.3.cloned.1.call-update
  35.0 0.0 reduce-scatter.2.cloned.1.call-start
  35.1 0.0 copy-done.3
  35.1 0.7 copy.24.qframe_ref
  35.8 0.0 copy-done.1
  35.8 0.2 copy.18
  36.0 0.8 copy.19
  36.9 0.0 copy-done.2
  36.9 0.2 copy.20
  37.0 0.8 copy.21
  37.9 0.0 copy-done.4
  37.9 1.0 copy.23.dots_ref
  38.9 0.6 reshape.149.kpos_ref
  39.6 0.6 reshape_reshape.4.kframe_ref
  40.2 0.6 iota_add_fusion.qpos_ref
  40.8 49.5 %all-gather.3.cloned.1.call-done.kv_ref = bf16[8192,256]{1,0:T(8,128)(2,1)} async-done(((bf16[1024,256]{1,0:T(8,128)(2,1)}), bf16[8192,256]{1,0:T(8,128)(2,1)}) %all-gather.3.cloned.1.call-update) | async-done | bytes 4194320 | tf_op jit(solution)/shard_map/all_gather | solution.py:134
  90.3 39.2 %shard_map.121 = (f32[896,128]{1,0:T(8,128)}, bf16[8192,256]{1,0:T(8,128)(2,1)}) custom-call(bf16[896,128]{1,0:T(8,128)(2,1)} %bitcast.56, bf16[896,128]{1,0:T(8,128)(2,1)} %bitcast.57, f32[896,1]{1,0:T(8,128)} %copy.23.dots_ref, s32[128,1]{1,0:T(8,128)} %iota_add_fusion.qpos_ref, s32[128,1]{1,0:T(8,128)} %copy.24.qframe_ref, ...), custom_call_target="tpu_custom_call" | custom-call | tf_op jit(solution)/shard_map/pallas_call | solution.py:97
  129.5 0.0 copy-start.5
  129.5 0.0 reduce-scatter.2.cloned.1.call-update
  129.5 56.9 %reduce-scatter.2.cloned.1.call-done = bf16[1024,256]{1,0:T(8,128)(2,1)} async-done(((bf16[8192,256]{1,0:T(8,128)(2,1)}), bf16[1024,256]{1,0:T(8,128)(2,1)}) %reduce-scatter.2.cloned.1.call-update) | async-done | bytes 524304 | tf_op jit(solution)/shard_map/reduce_scatter | solution.py:168
  186.4 7.1 %all-to-all-start.1 = ((bf16[8,128,256]{2,1,0:T(8,128)(2,1)}), bf16[8,128,256]{2,1,0:T(8,128)(2,1)S(1)}, u32[]{:S(2)}, u32[]{:S(2)}) async-start(bf16[8,128,256]{2,1,0:T(8,128)(2,1)} %bitcast.58), calls=%async_computation.2 | async-start | bytes 1048576 | tf_op jit(solution)/shard_map/all_to_all | solution.py:174
  193.5 0.0 copy-done.5
  193.5 1.0 convert_element_type.39
  194.6 0.2 copy.25
  194.8 0.2 copy.26
  194.9 0.6 gather_fusion
  195.6 15.9 %all-to-all-done.1 = bf16[8,128,256]{2,1,0:T(8,128)(2,1)S(1)} async-done(((bf16[8,128,256]{2,1,0:T(8,128)(2,1)}), bf16[8,128,256]{2,1,0:T(8,128)(2,1)S(1)}, u32[]{:S(2)}, u32[]{:S(2)}) %all-to-all-start.1) | async-done | bytes 524320 | tf_op jit(solution)/shard_map/all_to_all | solution.py:174
  211.5 0.1 reduce
  211.5 0.6 fusion.2
  212.2 0.6 gather_fusion.1
  212.8 0.6 gather_fusion.2
  213.4 14.0 %all-gather = bf16[256,1152]{1,0:T(8,128)(2,1)S(1)} all-gather(bf16[32,1152]{1,0:T(8,128)(2,1)S(1)} %pad_maximum_fusion), channel_id=2, replica_groups=mesh['cz'=8,'cy'=8,'section'=2,'dp'=4] {'section','dp'}, dimensions={0}, use_global_device_ids=true | all-gather | bytes 663552 | tf_op jit(solution)/shard_map/all_gather | solution.py:186
  227.4 0.6 copy.27
  228.0 0.1 copy.28
  228.1 0.0 copy-done
  228.1 0.0 copy-start.6
  228.1 3.8 %convolution_convert_fusion = bf16[128,2560]{1,0:T(8,128)(2,1)} fusion(bf16[448,2560]{1,0:T(8,128)(2,1)S(1)} %copy-done, bf16[128,2304]{1,0:T(8,128)(2,1)S(1)} %bitcast.50, bf16[2304,448]{0,1:T(8,128)(2,1)} %param.18), kind=kOutput, calls=%fused_computation.4 | convolution fusion | flops 558227456 | bytes 5603328 | tf_op jit(solution)/shard_map/dot_general | solution.py:200
  231.8 3.8 %all-to-all-start.2 = ((bf16[8,16,2560]{2,1,0:T(8,128)(2,1)}), bf16[8,16,2560]{2,1,0:T(8,128)(2,1)S(1)}, u32[]{:S(2)}, u32[]{:S(2)}) async-start(bf16[8,16,2560]{2,1,0:T(8,128)(2,1)} %bitcast.47), calls=%async_computation.3 | async-start | bytes 1310720 | tf_op jit(solution)/shard_map/all_to_all | solution.py:199
  235.7 0.0 copy-done.6
  235.7 10.9 %all-to-all-done.2 = bf16[8,16,2560]{2,1,0:T(8,128)(2,1)S(1)} async-done(((bf16[8,16,2560]{2,1,0:T(8,128)(2,1)}), bf16[8,16,2560]{2,1,0:T(8,128)(2,1)S(1)}, u32[]{:S(2)}, u32[]{:S(2)}) %all-to-all-start.2) | async-done | bytes 655392 | tf_op jit(solution)/shard_map/all_to_all | solution.py:199
  246.5 0.1 convert_reduce_fusion
  246.6 0.1 reshape.153
  246.7 1.3 gather_fusion.3
  (9 shorter events, 0.1 us)
Async XLA Ops:
  7.2 220.9 %copy-start = (bf16[448,2560]{1,0:T(8,128)(2,1)S(1)}, bf16[448,2560]{1,0:T(8,128)(2,1)}, u32[]{:S(2)}) copy-start(bf16[448,2560]{1,0:T(8,128)(2,1)} %param.19) | copy-start | bytes 6881284
  7.2 27.9 %copy-start.3 = (s32[1,8192]{1,0:T(1,128)S(1)}, s32[1,8192]{1,0:T(1,128)}, u32[]{:S(2)}) copy-start(s32[1,8192]{1,0:T(1,128)} %param.15) | copy-start | bytes 98308
  7.2 28.7 %copy-start.1 = (bf16[1,128,896]{2,1,0:T(8,128)(2,1)S(1)}, bf16[1,128,896]{2,1,0:T(8,128)(2,1)}, u32[]{:S(2)}) copy-start(bf16[1,128,896]{2,1,0:T(8,128)(2,1)} %param.10) | copy-start | bytes 688132
  7.2 29.7 %copy-start.2 = (bf16[1,128,896]{2,1,0:T(8,128)(2,1)S(1)}, bf16[1,128,896]{2,1,0:T(8,128)(2,1)}, u32[]{:S(2)}) copy-start(bf16[1,128,896]{2,1,0:T(8,128)(2,1)} %param.13) | copy-start | bytes 688132
  7.2 83.1 %all-gather.3.cloned.1.call-start = ((), (), s32[]{:S(2)}) async-start(), calls=%async_computation.4 | async-start | bytes 4718592 | tf_op jit(solution)/shard_map/all_gather | solution.py:134
  8.2 29.7 %copy-start.4 = (f32[1,7,128]{2,0,1:T(1,128)S(1)}, f32[1,7,128]{2,0,1:T(1,128)}, u32[]{:S(2)}) copy-start(f32[1,7,128]{2,0,1:T(1,128)} %param.14) | copy-start | bytes 10756
  35.0 151.4 %reduce-scatter.2.cloned.1.call-start = ((), (), s32[]{:S(2)}) async-start(), calls=%async_computation.5 | async-start | bytes 4718592 | tf_op jit(solution)/shard_map/reduce_scatter | solution.py:168
  129.5 64.0 %copy-start.5 = (s32[1,1,32]{2,1,0:T(1,128)S(1)}, s32[1,1,32]{2,1,0:T(1,128)}, u32[]{:S(2)}) copy-start(s32[1,1,32]{2,1,0:T(1,128)} %param.16) | copy-start | bytes 388
  186.4 25.1 %all-to-all-start.1 = ((bf16[8,128,256]{2,1,0:T(8,128)(2,1)}), bf16[8,128,256]{2,1,0:T(8,128)(2,1)S(1)}, u32[]{:S(2)}, u32[]{:S(2)}) async-start(bf16[8,128,256]{2,1,0:T(8,128)(2,1)} %bitcast.58), calls=%async_computation.2 | async-start | bytes 1048576 | tf_op jit(solution)/shard_map/all_to_all | solution.py:174
  228.1 7.6 %copy-start.6 = (s32[1,1,64]{2,1,0:T(1,128)S(1)}, s32[1,1,64]{2,1,0:T(1,128)}, u32[]{:S(2)}) copy-start(s32[1,1,64]{2,1,0:T(1,128)} %param.17) | copy-start | bytes 772
  231.8 14.7 %all-to-all-start.2 = ((bf16[8,16,2560]{2,1,0:T(8,128)(2,1)}), bf16[8,16,2560]{2,1,0:T(8,128)(2,1)S(1)}, u32[]{:S(2)}, u32[]{:S(2)}) async-start(bf16[8,16,2560]{2,1,0:T(8,128)(2,1)} %bitcast.47), calls=%async_computation.3 | async-start | bytes 1310720 | tf_op jit(solution)/shard_map/all_to_all | solution.py:199
Sparse Core Ops, SparseCore 0:
  35.1 55.0 all-gather.2
  129.7 56.6 reduce-scatter.1

commit v10 on v9

--- a/solution.py
+++ b/solution.py
@@ -165,11 +165,12 @@
         key_frames.reshape(tiles, KEY_TILE),
     )
     grad_query = dq2.reshape(GROUP, local_rows, HEAD_DIM).transpose(1, 0, 2)
-    stage_one = lax.psum_scatter(
-        partials,
-        "cy",
-        scatter_dimension=0,
-        tiled=True,
+    received = lax.all_to_all(partials, "cy", 0, 0, tiled=True)
+    stage_one = (
+        received.astype(jnp.float32)
+        .reshape(ring_y, seq_total // ring_y, received.shape[1])
+        .sum(0)
+        .astype(jnp.bfloat16)
     )
     stage_two = lax.all_to_all(stage_one, "cz", 0, 0, tiled=True)
     summed_grads = (

time: 255 us -> 302 us (1.18)
  blocking collectives: 40.8 us -> 143 us
  waiting for transfers between devices: 133 us -> 74.4 us
    all_to_all x0 -> x1, blocking collectives: none -> 99.5 us  [shards(): received = lax.all_to_all(partials, 'cy', 0, 0, tiled=True)]
    reduce_scatter x1 -> x0, waiting for transfers between devices: 56.9 us -> none  [shards(): lax.psum_scatter(partials, 'cy', scatter_dimension=0, tiled=True)]
    reduce_sum x0 -> x1, other arithmetic: none -> 3.77 us  [shards(): stage_one = received.astype(jnp.float32).reshape(ring_y, seq_total // rin...]
  transfers between devices with their start and end apart: 4 -> 3, of which waited for: 4 -> 3; matrix products, arithmetic and copies ran while one was open for 3% -> 2% of each run, Pallas kernels for 0% -> 0%
where the time goes in v10:
time: 302 us
  blocking collectives  143 us (47%)
  waiting for transfers between devices  74.4 us (25%)
  Pallas kernels  39.3 us (13%)
  between operations  14.2 us (5%)
  starting transfers between devices  10.9 us (4%)
  local copies, waits for them, and re-layouts  10 us (3%)
  other arithmetic  5.56 us (2%)
  matrix products  4.22 us (1%)
    all_to_all x1, blocking collectives, shards(): received = lax.all_to_all(partials, 'cy', 0, 0, tiled=True)  99.5 us
    all_gather x1, waiting for transfers between devices, shards(): lax.all_gather(lax.all_to_all(jnp.tile(own_pair, (ring_z, 1)), 'cz', 0, 0...  49.5 us
    pallas_call x1, Pallas kernels, attention_backward(): pl.pallas_call(backward_kernel, out_shape=(jax.ShapeDtypeStruct((rows, HE...  39.3 us
    all_to_all x1, blocking collectives, shards(): lax.all_to_all(jnp.tile(own_pair, (ring_z, 1)), 'cz', 0, 0, tiled=True)  26.8 us
    all_gather x1, blocking collectives, shards(): lax.all_gather(chosen[None], ('section', 'dp'), axis=0, tiled=True)  16.7 us
    all_to_all x1, waiting for transfers between devices, shards(): stage_two = lax.all_to_all(stage_one, 'cz', 0, 0, tiled=True)  14 us
    all_to_all x1, waiting for transfers between devices, shards(): lax.all_to_all(jnp.dot(visual_grad, projector_weight, preferred_element_t...  10.9 us
    all_to_all x1, starting transfers between devices, shards(): stage_two = lax.all_to_all(stage_one, 'cz', 0, 0, tiled=True)  7.08 us
  transfers between devices with their start and end apart: 3, of which 3 were waited for; matrix products, arithmetic and copies ran while one was open for 2% of the time, Pallas kernels for 0%

profile of v10, /device:TPU:1, one launch (start us, length us, event | category | flops | bytes accessed | tf_op | source)
XLA Modules:
  0.0 301.6 jit_solution(9186877558517748023)
XLA Ops:
  7.2 0.0 copy-start
  7.2 0.0 copy-start.4
  7.2 0.0 copy-start.2
  7.2 0.0 copy-start.3
  7.2 0.0 copy-start.5
  7.2 0.0 all-gather.3.cloned.1.call-start
  7.3 0.9 pad_maximum_fusion.1
  8.2 26.8 %all_to_all.33 = bf16[8,128,256]{2,1,0:T(8,128)(2,1)} all-to-all(bf16[8,128,256]{2,1,0:T(8,128)(2,1)S(1)} %tile.2), channel_id=1, replica_groups=mesh['cz'=8,'cy'=8,'section'=2,'dp'=4] {'cz'}, dimensions={0} | all-to-all | bytes 1048576 | tf_op jit(solution)/shard_map/all_to_all | solution.py:135
  35.0 0.0 all-gather.3.cloned.1.call-update
  35.0 0.0 copy-done.4
  35.1 0.7 copy.34.qframe_ref
  35.8 0.0 copy-done.2
  35.8 0.2 copy.28
  36.0 0.8 copy.29
  36.8 0.0 copy-done.3
  36.8 0.2 copy.30
  37.0 0.9 copy.31
  37.9 0.0 copy-done.5
  37.9 1.0 copy.33.dots_ref
  38.9 0.6 reshape.154.kpos_ref
  39.5 0.6 reshape_reshape.4.kframe_ref
  40.2 0.6 iota_add_fusion.qpos_ref
  40.8 49.5 %all-gather.3.cloned.1.call-done.kv_ref = bf16[8192,256]{1,0:T(8,128)(2,1)} async-done(((bf16[1024,256]{1,0:T(8,128)(2,1)}), bf16[8192,256]{1,0:T(8,128)(2,1)}) %all-gather.3.cloned.1.call-update) | async-done | bytes 4194320 | tf_op jit(solution)/shard_map/all_gather | solution.py:134
  90.3 39.3 %shard_map.121 = (f32[896,128]{1,0:T(8,128)}, bf16[8192,256]{1,0:T(8,128)(2,1)}) custom-call(bf16[896,128]{1,0:T(8,128)(2,1)} %bitcast.58, bf16[896,128]{1,0:T(8,128)(2,1)} %bitcast.59, f32[896,1]{1,0:T(8,128)} %copy.33.dots_ref, s32[128,1]{1,0:T(8,128)} %iota_add_fusion.qpos_ref, s32[128,1]{1,0:T(8,128)} %copy.34.qframe_ref, ...), custom_call_target="tpu_custom_call" | custom-call | tf_op jit(solution)/shard_map/pallas_call | solution.py:97
  129.6 99.5 %all_to_all.34 = bf16[8,1024,256]{2,1,0:T(8,128)(2,1)} all-to-all(bf16[8,1024,256]{2,1,0:T(8,128)(2,1)} %bitcast.48), channel_id=1, replica_groups=mesh['cz'=8,'cy'=8,'section'=2,'dp'=4] {'cy'}, dimensions={0} | all-to-all | bytes 8388608 | tf_op jit(solution)/shard_map/all_to_all | solution.py:168
  229.0 0.0 copy-start.6
  229.0 0.0 copy-start.1
  229.1 3.8 %reduce_sum.30 = bf16[1024,256]{1,0:T(8,128)(2,1)} reduce(bf16[8,1024,256]{2,1,0:T(8,128)(2,1)} %all_to_all.34, bf16[]{:T(256)} %constant.27.clone.1), dimensions={0}, to_apply=%region_0.0 | reduce | flops 1835008 | bytes 4718594 | tf_op jit(solution)/shard_map/reduce_sum | solution.py:172
  232.8 7.1 %all-to-all-start.2 = ((bf16[8,128,256]{2,1,0:T(8,128)(2,1)}), bf16[8,128,256]{2,1,0:T(8,128)(2,1)S(1)}, u32[]{:S(2)}, u32[]{:S(2)}) async-start(bf16[8,128,256]{2,1,0:T(8,128)(2,1)} %bitcast.14), calls=%async_computation.2 | async-start | bytes 1048576 | tf_op jit(solution)/shard_map/all_to_all | solution.py:175
  239.9 0.0 copy-done.6
  239.9 0.0 copy-done.1
  240.0 0.2 copy.35
  240.2 0.2 copy.36
  240.3 0.6 gather_fusion
  241.0 14.0 %all-to-all-done.2 = bf16[8,128,256]{2,1,0:T(8,128)(2,1)S(1)} async-done(((bf16[8,128,256]{2,1,0:T(8,128)(2,1)}), bf16[8,128,256]{2,1,0:T(8,128)(2,1)S(1)}, u32[]{:S(2)}, u32[]{:S(2)}) %all-to-all-start.2) | async-done | bytes 524320 | tf_op jit(solution)/shard_map/all_to_all | solution.py:175
  255.0 0.1 reduce.1
  255.1 0.6 fusion.2
  255.7 0.6 gather_fusion.1
  256.3 0.6 gather_fusion.2
  256.9 16.7 %all-gather = bf16[256,1152]{1,0:T(8,128)(2,1)S(1)} all-gather(bf16[32,1152]{1,0:T(8,128)(2,1)S(1)} %pad_maximum_fusion), channel_id=2, replica_groups=mesh['cz'=8,'cy'=8,'section'=2,'dp'=4] {'section','dp'}, dimensions={0}, use_global_device_ids=true | all-gather | bytes 663552 | tf_op jit(solution)/shard_map/all_gather | solution.py:187
  273.6 0.6 copy.37
  274.2 0.1 copy.38
  274.3 0.0 copy-done
  274.3 0.0 copy-start.7
  274.3 4.2 %convolution_convert_fusion = bf16[128,2560]{1,0:T(8,128)(2,1)} fusion(bf16[448,2560]{1,0:T(8,128)(2,1)S(1)} %copy-done, bf16[128,2304]{1,0:T(8,128)(2,1)S(1)} %bitcast.52, bf16[2304,448]{0,1:T(8,128)(2,1)} %param.18), kind=kOutput, calls=%fused_computation.4 | convolution fusion | flops 558227456 | bytes 5603328 | tf_op jit(solution)/shard_map/dot_general | solution.py:201
  278.6 3.8 %all-to-all-start.3 = ((bf16[8,16,2560]{2,1,0:T(8,128)(2,1)}), bf16[8,16,2560]{2,1,0:T(8,128)(2,1)S(1)}, u32[]{:S(2)}, u32[]{:S(2)}) async-start(bf16[8,16,2560]{2,1,0:T(8,128)(2,1)} %bitcast.49), calls=%async_computation.3 | async-start | bytes 1310720 | tf_op jit(solution)/shard_map/all_to_all | solution.py:200
  282.4 0.0 copy-done.7
  282.4 10.9 %all-to-all-done.3 = bf16[8,16,2560]{2,1,0:T(8,128)(2,1)S(1)} async-done(((bf16[8,16,2560]{2,1,0:T(8,128)(2,1)}), bf16[8,16,2560]{2,1,0:T(8,128)(2,1)S(1)}, u32[]{:S(2)}, u32[]{:S(2)}) %all-to-all-start.3) | async-done | bytes 655392 | tf_op jit(solution)/shard_map/all_to_all | solution.py:200
  293.2 0.1 convert_reduce_fusion
  293.3 0.1 reshape.158
  293.4 1.3 gather_fusion.3
  (10 shorter events, 0.1 us)
Async XLA Ops:
  7.2 267.1 %copy-start = (bf16[448,2560]{1,0:T(8,128)(2,1)S(1)}, bf16[448,2560]{1,0:T(8,128)(2,1)}, u32[]{:S(2)}) copy-start(bf16[448,2560]{1,0:T(8,128)(2,1)} %param.19) | copy-start | bytes 6881284
  7.2 27.9 %copy-start.4 = (s32[1,8192]{1,0:T(1,128)S(1)}, s32[1,8192]{1,0:T(1,128)}, u32[]{:S(2)}) copy-start(s32[1,8192]{1,0:T(1,128)} %param.15) | copy-start | bytes 98308
  7.2 28.6 %copy-start.2 = (bf16[1,128,896]{2,1,0:T(8,128)(2,1)S(1)}, bf16[1,128,896]{2,1,0:T(8,128)(2,1)}, u32[]{:S(2)}) copy-start(bf16[1,128,896]{2,1,0:T(8,128)(2,1)} %param.10) | copy-start | bytes 688132
  7.2 29.6 %copy-start.3 = (bf16[1,128,896]{2,1,0:T(8,128)(2,1)S(1)}, bf16[1,128,896]{2,1,0:T(8,128)(2,1)}, u32[]{:S(2)}) copy-start(bf16[1,128,896]{2,1,0:T(8,128)(2,1)} %param.13) | copy-start | bytes 688132
  7.2 30.6 %copy-start.5 = (f32[1,7,128]{2,0,1:T(1,128)S(1)}, f32[1,7,128]{2,0,1:T(1,128)}, u32[]{:S(2)}) copy-start(f32[1,7,128]{2,0,1:T(1,128)} %param.14) | copy-start | bytes 10756
  7.2 83.1 %all-gather.3.cloned.1.call-start = ((), (), s32[]{:S(2)}) async-start(), calls=%async_computation.4 | async-start | bytes 4718592 | tf_op jit(solution)/shard_map/all_gather | solution.py:134
  229.0 10.9 %copy-start.6 = (s32[1,1,32]{2,1,0:T(1,128)S(1)}, s32[1,1,32]{2,1,0:T(1,128)}, u32[]{:S(2)}) copy-start(s32[1,1,32]{2,1,0:T(1,128)} %param.16) | copy-start | bytes 388
  229.0 10.9 %copy-start.1 = (f32[896,128]{1,0:T(8,128)S(1)}, f32[896,128]{1,0:T(8,128)}, u32[]{:S(2)}) copy-start(f32[896,128]{1,0:T(8,128)} %get-tuple-element.6) | copy-start | bytes 1376260
  232.8 22.2 %all-to-all-start.2 = ((bf16[8,128,256]{2,1,0:T(8,128)(2,1)}), bf16[8,128,256]{2,1,0:T(8,128)(2,1)S(1)}, u32[]{:S(2)}, u32[]{:S(2)}) async-start(bf16[8,128,256]{2,1,0:T(8,128)(2,1)} %bitcast.14), calls=%async_computation.2 | async-start | bytes 1048576 | tf_op jit(solution)/shard_map/all_to_all | solution.py:175
  274.3 8.0 %copy-start.7 = (s32[1,1,64]{2,1,0:T(1,128)S(1)}, s32[1,1,64]{2,1,0:T(1,128)}, u32[]{:S(2)}) copy-start(s32[1,1,64]{2,1,0:T(1,128)} %param.17) | copy-start | bytes 772
  278.6 14.7 %all-to-all-start.3 = ((bf16[8,16,2560]{2,1,0:T(8,128)(2,1)}), bf16[8,16,2560]{2,1,0:T(8,128)(2,1)S(1)}, u32[]{:S(2)}, u32[]{:S(2)}) async-start(bf16[8,16,2560]{2,1,0:T(8,128)(2,1)} %bitcast.49), calls=%async_computation.3 | async-start | bytes 1310720 | tf_op jit(solution)/shard_map/all_to_all | solution.py:200
Sparse Core Ops, SparseCore 0:
  35.1 55.0 all-gather.2

commit v11 on v9

--- a/solution.py
+++ b/solution.py
@@ -132,21 +132,14 @@
 
     own_pair = jnp.concatenate([key_vectors[0], value_vectors[0]], axis=1)
     all_pairs = lax.all_gather(
-        lax.all_to_all(jnp.tile(own_pair, (ring_z, 1)), "cz", 0, 0, tiled=True),
-        "cy",
+        lax.all_to_all(jnp.tile(own_pair, (ring_y, 1)), "cy", 0, 0, tiled=True),
+        "cz",
         axis=0,
         tiled=True,
     )
 
-    key_pos = (
-        jnp.arange(seq_total, dtype=jnp.int32)
-        .reshape(ring_z, ring_y, local_rows)
-        .transpose(1, 0, 2)
-        .reshape(seq_total)
-    )
-    key_frames = (
-        frame_line.reshape(ring_z, ring_y, local_rows).transpose(1, 0, 2).reshape(seq_total)
-    )
+    key_pos = jnp.arange(seq_total, dtype=jnp.int32)
+    key_frames = frame_line
     rows = GROUP * local_rows
     q2 = query_heads.transpose(1, 0, 2).reshape(rows, HEAD_DIM)
     g2 = grad_heads.transpose(1, 0, 2).reshape(rows, HEAD_DIM)
@@ -167,13 +160,13 @@
     grad_query = dq2.reshape(GROUP, local_rows, HEAD_DIM).transpose(1, 0, 2)
     stage_one = lax.psum_scatter(
         partials,
-        "cy",
+        "cz",
         scatter_dimension=0,
         tiled=True,
     )
-    stage_two = lax.all_to_all(stage_one, "cz", 0, 0, tiled=True)
+    stage_two = lax.all_to_all(stage_one, "cy", 0, 0, tiled=True)
     summed_grads = (
-        stage_two.astype(jnp.float32).reshape(ring_z, local_rows, stage_two.shape[1]).sum(0)
+        stage_two.astype(jnp.float32).reshape(ring_y, local_rows, stage_two.shape[1]).sum(0)
     )
     grad_keys_low = summed_grads[:, :HEAD_DIM].astype(jnp.bfloat16)
     grad_values_low = summed_grads[:, HEAD_DIM:].astype(jnp.bfloat16)

time: 255 us -> 256 us (level)
  waiting for transfers between devices: 133 us -> 138 us
  blocking collectives: 40.8 us -> 36 us
    all_to_all x1, blocking collectives: 26.8 us -> 22 us  [shards(): lax.all_to_all(jnp.tile(own_pair, (ring_y, 1)), 'cy', 0, 0, tiled=True)]
    all_gather x1, waiting for transfers between devices: 49.5 us -> 54.1 us  [shards(): lax.all_gather(lax.all_to_all(jnp.tile(own_pair, (ring_y, 1)), 'cy', 0, 0...]
  transfers between devices with their start and end apart: 4 -> 4, of which waited for: 4 -> 4; matrix products, arithmetic and copies ran while one was open for 3% -> 4% of each run, Pallas kernels for 0% -> 0%
where the time goes in v11:
time: 256 us
  waiting for transfers between devices  138 us (54%)
  Pallas kernels  39.2 us (15%)
  blocking collectives  36 us (14%)
  between operations  14.2 us (6%)
  starting transfers between devices  10.4 us (4%)
  local copies, waits for them, and re-layouts  9.89 us (4%)
  other arithmetic  4.15 us (2%)
  matrix products  3.75 us (1%)
    reduce_scatter x1, waiting for transfers between devices, shards(): lax.psum_scatter(partials, 'cz', scatter_dimension=0, tiled=True)  57 us
    all_gather x1, waiting for transfers between devices, shards(): lax.all_gather(lax.all_to_all(jnp.tile(own_pair, (ring_y, 1)), 'cy', 0, 0...  54.1 us
    pallas_call x1, Pallas kernels, attention_backward(): pl.pallas_call(backward_kernel, out_shape=(jax.ShapeDtypeStruct((rows, HE...  39.2 us
    all_to_all x1, blocking collectives, shards(): lax.all_to_all(jnp.tile(own_pair, (ring_y, 1)), 'cy', 0, 0, tiled=True)  22 us
    all_to_all x1, waiting for transfers between devices, shards(): stage_two = lax.all_to_all(stage_one, 'cy', 0, 0, tiled=True)  15.9 us
    all_gather x1, blocking collectives, shards(): lax.all_gather(chosen[None], ('section', 'dp'), axis=0, tiled=True)  14 us
    all_to_all x1, waiting for transfers between devices, shards(): lax.all_to_all(jnp.dot(visual_grad, projector_weight, preferred_element_t...  10.9 us
    all_to_all x1, starting transfers between devices, shards(): stage_two = lax.all_to_all(stage_one, 'cy', 0, 0, tiled=True)  6.44 us
  transfers between devices with their start and end apart: 4, of which 4 were waited for; matrix products, arithmetic and copies ran while one was open for 4% of the time, Pallas kernels for 0%

profile of v11, /device:TPU:1, one launch (start us, length us, event | category | flops | bytes accessed | tf_op | source)
XLA Modules:
  0.0 255.5 jit_solution(8041406067609448184)
XLA Ops:
  7.2 0.0 copy-start
  7.2 0.0 copy-start.3
  7.2 0.0 copy-start.1
  7.2 0.0 copy-start.2
  7.2 0.0 all-gather.3.cloned.1.call-start
  7.3 0.9 pad_maximum_fusion.1
  8.2 0.0 copy-start.4
  8.2 22.0 %all_to_all.27 = bf16[8,128,256]{2,1,0:T(8,128)(2,1)} all-to-all(bf16[8,128,256]{2,1,0:T(8,128)(2,1)S(1)} %tile.2), channel_id=1, replica_groups=mesh['cz'=8,'cy'=8,'section'=2,'dp'=4] {'cy'}, dimensions={0} | all-to-all | bytes 1048576 | tf_op jit(solution)/shard_map/all_to_all | solution.py:135
  30.2 0.0 all-gather.3.cloned.1.call-update
  30.3 0.0 reduce-scatter.2.cloned.1.call-start
  30.3 0.0 copy-done.3
  30.3 0.7 copy.22.qframe_ref
  31.1 0.0 copy-done.1
  31.1 0.2 copy.17
  31.3 0.9 copy.18
  32.1 0.0 copy-done.2
  32.1 0.2 copy.19
  32.3 0.8 copy.20
  33.1 0.0 copy-done.4
  33.1 1.0 copy.21.dots_ref
  34.2 0.5 broadcast.64
  34.7 0.7 reduce.4
  35.4 0.6 reshape_squeeze.15.kframe_ref
  36.0 0.6 iota_add_fusion.qpos_ref
  36.7 0.6 multiply_add_fusion.kpos_ref
  37.3 54.1 %all-gather.3.cloned.1.call-done.kv_ref = bf16[8192,256]{1,0:T(8,128)(2,1)} async-done(((bf16[1024,256]{1,0:T(8,128)(2,1)}), bf16[8192,256]{1,0:T(8,128)(2,1)}) %all-gather.3.cloned.1.call-update) | async-done | bytes 4194320 | tf_op jit(solution)/shard_map/all_gather | solution.py:134
  91.4 39.2 %shard_map.121 = (f32[896,128]{1,0:T(8,128)}, bf16[8192,256]{1,0:T(8,128)(2,1)}) custom-call(bf16[896,128]{1,0:T(8,128)(2,1)} %bitcast.52, bf16[896,128]{1,0:T(8,128)(2,1)} %bitcast.53, f32[896,1]{1,0:T(8,128)} %copy.21.dots_ref, s32[128,1]{1,0:T(8,128)} %iota_add_fusion.qpos_ref, s32[128,1]{1,0:T(8,128)} %copy.22.qframe_ref, ...), custom_call_target="tpu_custom_call" | custom-call | tf_op jit(solution)/shard_map/pallas_call | solution.py:97
  130.6 0.0 copy-start.5
  130.6 0.0 reduce-scatter.2.cloned.1.call-update
  130.7 57.0 %reduce-scatter.2.cloned.1.call-done = bf16[1024,256]{1,0:T(8,128)(2,1)} async-done(((bf16[8192,256]{1,0:T(8,128)(2,1)}), bf16[1024,256]{1,0:T(8,128)(2,1)}) %reduce-scatter.2.cloned.1.call-update) | async-done | bytes 524304 | tf_op jit(solution)/shard_map/reduce_scatter | solution.py:161
  187.7 6.4 %all-to-all-start.1 = ((bf16[8,128,256]{2,1,0:T(8,128)(2,1)}), bf16[8,128,256]{2,1,0:T(8,128)(2,1)S(1)}, u32[]{:S(2)}, u32[]{:S(2)}) async-start(bf16[8,128,256]{2,1,0:T(8,128)(2,1)} %bitcast.54), calls=%async_computation.2 | async-start | bytes 1048576 | tf_op jit(solution)/shard_map/all_to_all | solution.py:167
  194.1 0.0 copy-done.5
  194.2 1.0 convert_element_type.39
  195.2 0.2 copy.23
  195.4 0.2 copy.24
  195.6 0.6 gather_fusion
  196.2 15.9 %all-to-all-done.1 = bf16[8,128,256]{2,1,0:T(8,128)(2,1)S(1)} async-done(((bf16[8,128,256]{2,1,0:T(8,128)(2,1)}), bf16[8,128,256]{2,1,0:T(8,128)(2,1)S(1)}, u32[]{:S(2)}, u32[]{:S(2)}) %all-to-all-start.1) | async-done | bytes 524320 | tf_op jit(solution)/shard_map/all_to_all | solution.py:167
  212.1 0.1 reduce
  212.2 0.6 fusion.2
  212.8 0.6 gather_fusion.1
  213.4 0.6 gather_fusion.2
  214.0 14.0 %all-gather = bf16[256,1152]{1,0:T(8,128)(2,1)S(1)} all-gather(bf16[32,1152]{1,0:T(8,128)(2,1)S(1)} %pad_maximum_fusion), channel_id=2, replica_groups=mesh['cz'=8,'cy'=8,'section'=2,'dp'=4] {'section','dp'}, dimensions={0}, use_global_device_ids=true | all-gather | bytes 663552 | tf_op jit(solution)/shard_map/all_gather | solution.py:179
  228.0 0.6 copy.25
  228.6 0.1 copy.26
  228.7 0.0 copy-done
  228.7 0.0 copy-start.6
  228.7 3.8 %convolution_convert_fusion = bf16[128,2560]{1,0:T(8,128)(2,1)} fusion(bf16[448,2560]{1,0:T(8,128)(2,1)S(1)} %copy-done, bf16[128,2304]{1,0:T(8,128)(2,1)S(1)} %bitcast.46, bf16[2304,448]{0,1:T(8,128)(2,1)} %param.18), kind=kOutput, calls=%fused_computation.4 | convolution fusion | flops 558227456 | bytes 5603328 | tf_op jit(solution)/shard_map/dot_general | solution.py:193
  232.5 3.8 %all-to-all-start.2 = ((bf16[8,16,2560]{2,1,0:T(8,128)(2,1)}), bf16[8,16,2560]{2,1,0:T(8,128)(2,1)S(1)}, u32[]{:S(2)}, u32[]{:S(2)}) async-start(bf16[8,16,2560]{2,1,0:T(8,128)(2,1)} %bitcast.43), calls=%async_computation.3 | async-start | bytes 1310720 | tf_op jit(solution)/shard_map/all_to_all | solution.py:192
  236.3 0.0 copy-done.6
  236.3 10.9 %all-to-all-done.2 = bf16[8,16,2560]{2,1,0:T(8,128)(2,1)S(1)} async-done(((bf16[8,16,2560]{2,1,0:T(8,128)(2,1)}), bf16[8,16,2560]{2,1,0:T(8,128)(2,1)S(1)}, u32[]{:S(2)}, u32[]{:S(2)}) %all-to-all-start.2) | async-done | bytes 655392 | tf_op jit(solution)/shard_map/all_to_all | solution.py:192
  247.2 0.1 convert_reduce_fusion
  247.3 0.1 reshape.132
  247.3 1.3 gather_fusion.3
  (7 shorter events, 0.1 us)
Async XLA Ops:
  7.2 221.5 %copy-start = (bf16[448,2560]{1,0:T(8,128)(2,1)S(1)}, bf16[448,2560]{1,0:T(8,128)(2,1)}, u32[]{:S(2)}) copy-start(bf16[448,2560]{1,0:T(8,128)(2,1)} %param.19) | copy-start | bytes 6881284
  7.2 23.1 %copy-start.3 = (s32[1,8192]{1,0:T(1,128)S(1)}, s32[1,8192]{1,0:T(1,128)}, u32[]{:S(2)}) copy-start(s32[1,8192]{1,0:T(1,128)} %param.15) | copy-start | bytes 98308
  7.2 23.9 %copy-start.1 = (bf16[1,128,896]{2,1,0:T(8,128)(2,1)S(1)}, bf16[1,128,896]{2,1,0:T(8,128)(2,1)}, u32[]{:S(2)}) copy-start(bf16[1,128,896]{2,1,0:T(8,128)(2,1)} %param.10) | copy-start | bytes 688132
  7.2 24.9 %copy-start.2 = (bf16[1,128,896]{2,1,0:T(8,128)(2,1)S(1)}, bf16[1,128,896]{2,1,0:T(8,128)(2,1)}, u32[]{:S(2)}) copy-start(bf16[1,128,896]{2,1,0:T(8,128)(2,1)} %param.13) | copy-start | bytes 688132
  7.2 84.2 %all-gather.3.cloned.1.call-start = ((), (), s32[]{:S(2)}) async-start(), calls=%async_computation.4 | async-start | bytes 4718592 | tf_op jit(solution)/shard_map/all_gather | solution.py:134
  8.2 24.9 %copy-start.4 = (f32[1,7,128]{2,0,1:T(1,128)S(1)}, f32[1,7,128]{2,0,1:T(1,128)}, u32[]{:S(2)}) copy-start(f32[1,7,128]{2,0,1:T(1,128)} %param.14) | copy-start | bytes 10756
  30.3 157.4 %reduce-scatter.2.cloned.1.call-start = ((), (), s32[]{:S(2)}) async-start(), calls=%async_computation.5 | async-start | bytes 4718592 | tf_op jit(solution)/shard_map/reduce_scatter | solution.py:161
  130.6 63.5 %copy-start.5 = (s32[1,1,32]{2,1,0:T(1,128)S(1)}, s32[1,1,32]{2,1,0:T(1,128)}, u32[]{:S(2)}) copy-start(s32[1,1,32]{2,1,0:T(1,128)} %param.16) | copy-start | bytes 388
  187.7 24.4 %all-to-all-start.1 = ((bf16[8,128,256]{2,1,0:T(8,128)(2,1)}), bf16[8,128,256]{2,1,0:T(8,128)(2,1)S(1)}, u32[]{:S(2)}, u32[]{:S(2)}) async-start(bf16[8,128,256]{2,1,0:T(8,128)(2,1)} %bitcast.54), calls=%async_computation.2 | async-start | bytes 1048576 | tf_op jit(solution)/shard_map/all_to_all | solution.py:167
  228.7 7.6 %copy-start.6 = (s32[1,1,64]{2,1,0:T(1,128)S(1)}, s32[1,1,64]{2,1,0:T(1,128)}, u32[]{:S(2)}) copy-start(s32[1,1,64]{2,1,0:T(1,128)} %param.17) | copy-start | bytes 772
  232.5 14.7 %all-to-all-start.2 = ((bf16[8,16,2560]{2,1,0:T(8,128)(2,1)}), bf16[8,16,2560]{2,1,0:T(8,128)(2,1)S(1)}, u32[]{:S(2)}, u32[]{:S(2)}) async-start(bf16[8,16,2560]{2,1,0:T(8,128)(2,1)} %bitcast.43), calls=%async_computation.3 | async-start | bytes 1310720 | tf_op jit(solution)/shard_map/all_to_all | solution.py:192
Sparse Core Ops, SparseCore 0:
  30.4 60.9 all-gather.2
  130.8 56.8 reduce-scatter.1

commit v12 on v9

--- a/solution.py
+++ b/solution.py
@@ -62,6 +62,7 @@
             jnp.full((heads, local_rows, 1), MASKED, jnp.float32),
             jnp.zeros((heads, local_rows, 1), jnp.float32),
         ),
+        unroll=True,
     )
     log_total = running + jnp.log(summed)
     dots = dots_ref[...].reshape(heads, local_rows, 1)

time: 255 us -> 254 us (level)
  no operation moved by 1% of the time
where the time goes in v12:
time: 254 us; the launch traced here: 253 us
  waiting for transfers between devices  133 us (52%)
  blocking collectives  40.6 us (16%)
  Pallas kernels  37.9 us (15%)
  between operations  14.2 us (6%)
  starting transfers between devices  11 us (4%)
  local copies, waits for them, and re-layouts  10 us (4%)
  matrix products  3.76 us (1%)
  other arithmetic  2.81 us (1%)
    reduce_scatter x1, waiting for transfers between devices, shards(): lax.psum_scatter(partials, 'cy', scatter_dimension=0, tiled=True)  56.9 us
    all_gather x1, waiting for transfers between devices, shards(): lax.all_gather(lax.all_to_all(jnp.tile(own_pair, (ring_z, 1)), 'cz', 0, 0...  49.5 us
    pallas_call x1, Pallas kernels, attention_backward(): pl.pallas_call(backward_kernel, out_shape=(jax.ShapeDtypeStruct((rows, HE...  37.9 us
    all_to_all x1, blocking collectives, shards(): lax.all_to_all(jnp.tile(own_pair, (ring_z, 1)), 'cz', 0, 0, tiled=True)  26.8 us
    all_to_all x1, waiting for transfers between devices, shards(): stage_two = lax.all_to_all(stage_one, 'cz', 0, 0, tiled=True)  15.9 us
    all_gather x1, blocking collectives, shards(): lax.all_gather(chosen[None], ('section', 'dp'), axis=0, tiled=True)  13.8 us
    all_to_all x1, waiting for transfers between devices, shards(): lax.all_to_all(jnp.dot(visual_grad, projector_weight, preferred_element_t...  10.9 us
    all_to_all x1, starting transfers between devices, shards(): stage_two = lax.all_to_all(stage_one, 'cz', 0, 0, tiled=True)  7.1 us
  transfers between devices with their start and end apart: 4, of which 4 were waited for; matrix products, arithmetic and copies ran while one was open for 3% of the time, Pallas kernels for 0%

profile of v12, /device:TPU:1, one launch (start us, length us, event | category | flops | bytes accessed | tf_op | source)
XLA Modules:
  0.0 253.4 jit_solution(5288574004719618811)
XLA Ops:
  7.2 0.0 copy-start
  7.2 0.0 copy-start.3
  7.2 0.0 copy-start.1
  7.2 0.0 copy-start.2
  7.2 0.0 all-gather.3.cloned.1.call-start
  7.3 0.9 pad_maximum_fusion.1
  8.2 0.0 copy-start.4
  8.2 26.8 %all_to_all.27 = bf16[8,128,256]{2,1,0:T(8,128)(2,1)} all-to-all(bf16[8,128,256]{2,1,0:T(8,128)(2,1)S(1)} %tile.2), channel_id=1, replica_groups=mesh['cz'=8,'cy'=8,'section'=2,'dp'=4] {'cz'}, dimensions={0} | all-to-all | bytes 1048576 | tf_op jit(solution)/shard_map/all_to_all | solution.py:136
  35.0 0.0 all-gather.3.cloned.1.call-update
  35.0 0.0 reduce-scatter.2.cloned.1.call-start
  35.1 0.0 copy-done.3
  35.1 0.7 copy.24.qframe_ref
  35.8 0.0 copy-done.1
  35.8 0.2 copy.18
  36.0 0.8 copy.19
  36.9 0.0 copy-done.2
  36.9 0.2 copy.20
  37.0 0.8 copy.21
  37.9 0.0 copy-done.4
  37.9 1.0 copy.23.dots_ref
  38.9 0.6 reshape.149.kpos_ref
  39.6 0.6 reshape_reshape.4.kframe_ref
  40.2 0.6 iota_add_fusion.qpos_ref
  40.8 49.5 %all-gather.3.cloned.1.call-done.kv_ref = bf16[8192,256]{1,0:T(8,128)(2,1)} async-done(((bf16[1024,256]{1,0:T(8,128)(2,1)}), bf16[8192,256]{1,0:T(8,128)(2,1)}) %all-gather.3.cloned.1.call-update) | async-done | bytes 4194320 | tf_op jit(solution)/shard_map/all_gather | solution.py:135
  90.3 37.9 %shard_map.121 = (f32[896,128]{1,0:T(8,128)}, bf16[8192,256]{1,0:T(8,128)(2,1)}) custom-call(bf16[896,128]{1,0:T(8,128)(2,1)} %bitcast.56, bf16[896,128]{1,0:T(8,128)(2,1)} %bitcast.57, f32[896,1]{1,0:T(8,128)} %copy.23.dots_ref, s32[128,1]{1,0:T(8,128)} %iota_add_fusion.qpos_ref, s32[128,1]{1,0:T(8,128)} %copy.24.qframe_ref, ...), custom_call_target="tpu_custom_call" | custom-call | tf_op jit(solution)/shard_map/pallas_call | solution.py:98
  128.2 0.0 copy-start.5
  128.2 0.0 reduce-scatter.2.cloned.1.call-update
  128.2 56.9 %reduce-scatter.2.cloned.1.call-done = bf16[1024,256]{1,0:T(8,128)(2,1)} async-done(((bf16[8192,256]{1,0:T(8,128)(2,1)}), bf16[1024,256]{1,0:T(8,128)(2,1)}) %reduce-scatter.2.cloned.1.call-update) | async-done | bytes 524304 | tf_op jit(solution)/shard_map/reduce_scatter | solution.py:169
  185.1 7.1 %all-to-all-start.1 = ((bf16[8,128,256]{2,1,0:T(8,128)(2,1)}), bf16[8,128,256]{2,1,0:T(8,128)(2,1)S(1)}, u32[]{:S(2)}, u32[]{:S(2)}) async-start(bf16[8,128,256]{2,1,0:T(8,128)(2,1)} %bitcast.58), calls=%async_computation.2 | async-start | bytes 1048576 | tf_op jit(solution)/shard_map/all_to_all | solution.py:175
  192.2 0.0 copy-done.5
  192.2 1.0 convert_element_type.39
  193.3 0.2 copy.25
  193.5 0.2 copy.26
  193.6 0.6 gather_fusion
  194.3 15.9 %all-to-all-done.1 = bf16[8,128,256]{2,1,0:T(8,128)(2,1)S(1)} async-done(((bf16[8,128,256]{2,1,0:T(8,128)(2,1)}), bf16[8,128,256]{2,1,0:T(8,128)(2,1)S(1)}, u32[]{:S(2)}, u32[]{:S(2)}) %all-to-all-start.1) | async-done | bytes 524320 | tf_op jit(solution)/shard_map/all_to_all | solution.py:175
  210.2 0.1 reduce
  210.2 0.6 fusion.2
  210.9 0.6 gather_fusion.1
  211.5 0.6 gather_fusion.2
  212.1 13.8 %all-gather = bf16[256,1152]{1,0:T(8,128)(2,1)S(1)} all-gather(bf16[32,1152]{1,0:T(8,128)(2,1)S(1)} %pad_maximum_fusion), channel_id=2, replica_groups=mesh['cz'=8,'cy'=8,'section'=2,'dp'=4] {'section','dp'}, dimensions={0}, use_global_device_ids=true | all-gather | bytes 663552 | tf_op jit(solution)/shard_map/all_gather | solution.py:187
  225.9 0.6 copy.27
  226.5 0.1 copy.28
  226.6 0.0 copy-done
  226.6 0.0 copy-start.6
  226.6 3.8 %convolution_convert_fusion = bf16[128,2560]{1,0:T(8,128)(2,1)} fusion(bf16[448,2560]{1,0:T(8,128)(2,1)S(1)} %copy-done, bf16[128,2304]{1,0:T(8,128)(2,1)S(1)} %bitcast.50, bf16[2304,448]{0,1:T(8,128)(2,1)} %param.18), kind=kOutput, calls=%fused_computation.4 | convolution fusion | flops 558227456 | bytes 5603328 | tf_op jit(solution)/shard_map/dot_general | solution.py:201
  230.4 3.8 %all-to-all-start.2 = ((bf16[8,16,2560]{2,1,0:T(8,128)(2,1)}), bf16[8,16,2560]{2,1,0:T(8,128)(2,1)S(1)}, u32[]{:S(2)}, u32[]{:S(2)}) async-start(bf16[8,16,2560]{2,1,0:T(8,128)(2,1)} %bitcast.47), calls=%async_computation.3 | async-start | bytes 1310720 | tf_op jit(solution)/shard_map/all_to_all | solution.py:200
  234.2 0.0 copy-done.6
  234.2 10.9 %all-to-all-done.2 = bf16[8,16,2560]{2,1,0:T(8,128)(2,1)S(1)} async-done(((bf16[8,16,2560]{2,1,0:T(8,128)(2,1)}), bf16[8,16,2560]{2,1,0:T(8,128)(2,1)S(1)}, u32[]{:S(2)}, u32[]{:S(2)}) %all-to-all-start.2) | async-done | bytes 655392 | tf_op jit(solution)/shard_map/all_to_all | solution.py:200
  245.1 0.1 convert_reduce_fusion
  245.2 0.1 reshape.153
  245.2 1.3 gather_fusion.3
  (9 shorter events, 0.1 us)
Async XLA Ops:
  7.2 219.4 %copy-start = (bf16[448,2560]{1,0:T(8,128)(2,1)S(1)}, bf16[448,2560]{1,0:T(8,128)(2,1)}, u32[]{:S(2)}) copy-start(bf16[448,2560]{1,0:T(8,128)(2,1)} %param.19) | copy-start | bytes 6881284
  7.2 27.9 %copy-start.3 = (s32[1,8192]{1,0:T(1,128)S(1)}, s32[1,8192]{1,0:T(1,128)}, u32[]{:S(2)}) copy-start(s32[1,8192]{1,0:T(1,128)} %param.15) | copy-start | bytes 98308
  7.2 28.7 %copy-start.1 = (bf16[1,128,896]{2,1,0:T(8,128)(2,1)S(1)}, bf16[1,128,896]{2,1,0:T(8,128)(2,1)}, u32[]{:S(2)}) copy-start(bf16[1,128,896]{2,1,0:T(8,128)(2,1)} %param.10) | copy-start | bytes 688132
  7.2 29.7 %copy-start.2 = (bf16[1,128,896]{2,1,0:T(8,128)(2,1)S(1)}, bf16[1,128,896]{2,1,0:T(8,128)(2,1)}, u32[]{:S(2)}) copy-start(bf16[1,128,896]{2,1,0:T(8,128)(2,1)} %param.13) | copy-start | bytes 688132
  7.2 83.1 %all-gather.3.cloned.1.call-start = ((), (), s32[]{:S(2)}) async-start(), calls=%async_computation.4 | async-start | bytes 4718592 | tf_op jit(solution)/shard_map/all_gather | solution.py:135
  8.2 29.7 %copy-start.4 = (f32[1,7,128]{2,0,1:T(1,128)S(1)}, f32[1,7,128]{2,0,1:T(1,128)}, u32[]{:S(2)}) copy-start(f32[1,7,128]{2,0,1:T(1,128)} %param.14) | copy-start | bytes 10756
  35.0 150.1 %reduce-scatter.2.cloned.1.call-start = ((), (), s32[]{:S(2)}) async-start(), calls=%async_computation.5 | async-start | bytes 4718592 | tf_op jit(solution)/shard_map/reduce_scatter | solution.py:169
  128.2 64.0 %copy-start.5 = (s32[1,1,32]{2,1,0:T(1,128)S(1)}, s32[1,1,32]{2,1,0:T(1,128)}, u32[]{:S(2)}) copy-start(s32[1,1,32]{2,1,0:T(1,128)} %param.16) | copy-start | bytes 388
  185.1 25.1 %all-to-all-start.1 = ((bf16[8,128,256]{2,1,0:T(8,128)(2,1)}), bf16[8,128,256]{2,1,0:T(8,128)(2,1)S(1)}, u32[]{:S(2)}, u32[]{:S(2)}) async-start(bf16[8,128,256]{2,1,0:T(8,128)(2,1)} %bitcast.58), calls=%async_computation.2 | async-start | bytes 1048576 | tf_op jit(solution)/shard_map/all_to_all | solution.py:175
  226.6 7.6 %copy-start.6 = (s32[1,1,64]{2,1,0:T(1,128)S(1)}, s32[1,1,64]{2,1,0:T(1,128)}, u32[]{:S(2)}) copy-start(s32[1,1,64]{2,1,0:T(1,128)} %param.17) | copy-start | bytes 772
  230.4 14.7 %all-to-all-start.2 = ((bf16[8,16,2560]{2,1,0:T(8,128)(2,1)}), bf16[8,16,2560]{2,1,0:T(8,128)(2,1)S(1)}, u32[]{:S(2)}, u32[]{:S(2)}) async-start(bf16[8,16,2560]{2,1,0:T(8,128)(2,1)} %bitcast.47), calls=%async_computation.3 | async-start | bytes 1310720 | tf_op jit(solution)/shard_map/all_to_all | solution.py:200
Sparse Core Ops, SparseCore 0:
  35.1 55.0 all-gather.2
  128.3 56.7 reduce-scatter.1
